TPU v7x, 512 devices: a whole 4x8x8 slice. The times are simulated.
512 devices in a mesh: dp: 64 (over x, z, y_lo), fsdp: 8 (over y_hi, core).
Axes of the slice: x: 4, y: 8 (y_hi: 4, y_lo: 2; y = y_hi * 2 + y_lo), z: 8, core: 2. Of those that a mesh axis runs over, the one named last changes fastest.
Arguments:
- group_qkv: bfloat16 [64, 1024, 6144], P('dp', 'fsdp'), may hold values from -6 to 6
- cache_pool: bfloat16 [8192, 16, 4096], P('dp', None, 'fsdp'), may hold values from -6 to 6
- page_request: int32 [8192], P('dp'), may hold values from 0 to 64, as said below
- request_host: int32 [64], replicated, may hold values from 0 to 63, each once
- out_weight: bfloat16 [2048, 2048], P(('dp', 'fsdp')), may hold values from -0.5 to 0.5
Outputs:
- projected: bfloat16 [64, 1024, 2048], P('dp', 'fsdp')
Inputs may be any that keep to these rules, and one draw needn't show every extreme that they name: `page_request`: within the slots of one dp index, at most 2 pages belong to one request, and some request has exactly 2 pages in the slots of every dp index. A request holds 1 to 15 pages, or 64 to 128 pages. Some slot is empty.
All inputs are finite; a program needn't handle non-finite values.
Results may differ from a plain program's by a relative error of at most 0.0053.
Values may be sent and summed in bfloat16 or wider, within the bound.
No kernel may reach another device: no remote copies, remote signals or barrier semaphores. Data moves between devices by JAX's collectives and lax.ppermute only.
A program may use at most 64 MiB of HBM per device.

v0:
```python
import math

import jax
import jax.numpy as jnp
from jax import lax
from jax.sharding import PartitionSpec as P

HD = 128
PAGE = 16
MOST = 2


def per_device(group_qkv, cache_pool, page_request, request_host, out_weight):
    fsdp_count = lax.axis_size("fsdp")
    requests = request_host.shape[0]
    slot_count = page_request.shape[0]
    tokens_here = group_qkv.shape[1]
    features = cache_pool.shape[2]
    heads_here = features // (2 * HD)
    score_scale = 1.0 / math.sqrt(HD)
    request_ids = jnp.arange(requests, dtype=jnp.int32)
    member = (page_request[:, None] == request_ids[None, :]).astype(jnp.int32)
    slot_rank = jnp.sum(member * (jnp.cumsum(member, axis=0) - 1), axis=1)
    target_host = jnp.sum(member * request_host[None, :], axis=1)
    is_live = jnp.sum(member, axis=1)
    target_slot = jnp.where(is_live > 0, target_host * MOST + slot_rank, -1)
    chosen = target_slot[:, None] == jnp.arange(requests * MOST, dtype=jnp.int32)[None, :]
    flat_pool = cache_pool.reshape(slot_count, PAGE * features)
    packed = jnp.einsum(
        "sp,sf->pf", chosen.astype(jnp.bfloat16), flat_pool, preferred_element_type=jnp.float32
    )
    packed = packed.astype(jnp.bfloat16).reshape(requests, MOST, PAGE, features)
    occupied = jnp.sum(chosen.astype(jnp.int32), axis=0).reshape(requests, MOST)
    arrived, present = (
        lax.all_to_all(packed, "dp", split_axis=0, concat_axis=0, tiled=True),
        lax.all_to_all(occupied, "dp", split_axis=0, concat_axis=0, tiled=True),
    )
    cached = arrived.reshape(requests * MOST * PAGE, heads_here, 2, HD)
    key_cache = cached[:, :, 0]
    value_cache = cached[:, :, 1]
    live_tokens = jnp.repeat(present.reshape(requests * MOST), PAGE) > 0
    local_qkv = group_qkv.reshape(tokens_here, fsdp_count, heads_here * 3 * HD)
    gathered_qkv = lax.all_to_all(local_qkv, "fsdp", split_axis=1, concat_axis=0, tiled=True)
    group_len = tokens_here * fsdp_count
    gathered_qkv = gathered_qkv.reshape(group_len, heads_here, 3, HD)
    queries = gathered_qkv[:, :, 0]
    new_keys = gathered_qkv[:, :, 1]
    new_values = gathered_qkv[:, :, 2]
    block_rows = min(512, group_len)
    block_count = group_len // block_rows
    query_blocks = queries.reshape(block_count, block_rows, heads_here, HD)

    def attend(inputs):
        query_block, first_row = inputs
        cache_scores = (
            jnp.einsum("qhd,khd->hqk", query_block, key_cache, preferred_element_type=jnp.float32)
            * score_scale
        )
        cache_scores = jnp.where(live_tokens[None, None, :], cache_scores, -jnp.inf)
        group_scores = (
            jnp.einsum("qhd,khd->hqk", query_block, new_keys, preferred_element_type=jnp.float32)
            * score_scale
        )
        causal = jnp.arange(group_len)[None, :] <= first_row + jnp.arange(block_rows)[:, None]
        group_scores = jnp.where(causal[None, :, :], group_scores, -jnp.inf)
        row_max = jnp.maximum(jnp.max(cache_scores, axis=2), jnp.max(group_scores, axis=2))
        cache_expo = jnp.exp(cache_scores - row_max[:, :, None])
        group_expo = jnp.exp(group_scores - row_max[:, :, None])
        row_total = jnp.sum(cache_expo, axis=2) + jnp.sum(group_expo, axis=2)
        mixture = jnp.einsum(
            "hqk,khd->qhd",
            cache_expo.astype(jnp.bfloat16),
            value_cache,
            preferred_element_type=jnp.float32,
        )
        mixture = mixture + jnp.einsum(
            "hqk,khd->qhd",
            group_expo.astype(jnp.bfloat16),
            new_values,
            preferred_element_type=jnp.float32,
        )
        result = mixture / jnp.transpose(row_total)[:, :, None]
        return result.astype(jnp.bfloat16).reshape(block_rows, heads_here * HD)

    starts = jnp.arange(block_count, dtype=jnp.int32) * block_rows
    attn_heads = lax.map(attend, (query_blocks, starts)).reshape(group_len, heads_here * HD)
    tokens_attn = lax.all_to_all(attn_heads, "fsdp", split_axis=0, concat_axis=1, tiled=True)
    summed = jnp.dot(
        tokens_attn,
        lax.all_gather(out_weight, ("dp", "fsdp"), axis=0, tiled=True),
        preferred_element_type=jnp.float32,
    )
    return summed.astype(jnp.bfloat16).reshape(1, tokens_here, out_weight.shape[1])


def solution(mesh):
    return jax.shard_map(
        per_device,
        mesh=mesh,
        in_specs=(
            P("dp", "fsdp", None),
            P("dp", None, "fsdp"),
            P("dp"),
            P(),
            P(("dp", "fsdp"), None),
        ),
        out_specs=P("dp", "fsdp", None),
        check_vma=False,
    )
```

profile of v0, /device:TPU:1, one launch (start us, length us, event | category | flops | bytes accessed | tf_op | source)
XLA Modules:
  0.0 900.0 jit_solution(7879001282318499317)
XLA Ops:
  8.2 0.9 select_reduce_fusion.1
  9.9 15.3 %all-to-all-start = ((s32[64,1,2]{2,1,0:T(1,128)}), s32[64,1,2]{2,1,0:T(1,128)S(1)}, u32[]{:S(2)}, u32[]{:S(2)}) async-start(s32[64,1,2]{2,1,0:T(1,128)} %bitcast.9), calls=%async_computation | async-start | bytes 65536 | tf_op jit(solution)/shard_map/all_to_all | solution.py:36
  25.3 2.6 copy.34
  27.8 6.6 all-to-all-done
  34.4 8.3 all-to-all-start.1
  42.7 3.0 copy.49
  46.5 2.2 copy.50
  48.8 30.1 %all-to-all-done.1 = bf16[128,8,768]{0,2,1:T(8,128)(2,1)S(1)} async-done(((bf16[128,8,768]{0,2,1:T(8,128)(2,1)}), bf16[128,8,768]{0,2,1:T(8,128)(2,1)S(1)}, u32[]{:S(2)}, u32[]{:S(2)}) %all-to-all-start.1) | async-done | bytes 1572896 | tf_op jit(solution)/shard_map/all_to_all | solution.py:43
  78.9 8.8 all-to-all-start.2
  87.9 1.0 copy.35
  89.7 1.0 slice_bitcast_fusion
  91.2 45.4 %all-to-all-done.2 = bf16[64,2,16,512]{3,2,1,0:T(8,128)(2,1)} async-done(((bf16[64,2,16,512]{3,2,1,0:T(8,128)(2,1)}), bf16[64,2,16,512]{3,2,1,0:T(8,128)(2,1)}, u32[]{:S(2)}, u32[]{:S(2)}) %all-to-all-start.2) | async-done | bytes 2097184 | tf_op jit(solution)/shard_map/all_to_all | solution.py:35
  136.6 2.6 reshape.84
  139.1 3.9 fusion.42
  143.2 5.8 copy.45
  149.1 27.3 %while.11 = (s32[]{:T(128)}, bf16[2,512,256]{2,1,0:T(8,128)(2,1)S(1)}, bf16[2,512,2,128]{3,1,0,2:T(8,128)(2,1)S(1)}, bf16[2048,2,128]{2,0,1:T(8,128)(2,1)S(1)}, ...) while((s32[]{:T(128)}, ...), condition=%wide.region_10.11_spmd.clone, body=%wide.region_5.10_spmd.clone.sunk | while | flops 1646131712 | bytes 69022040 | solution.py:86
  150.7 2.9 fusion.68
  153.7 1.4 fusion.69
  155.9 1.2 fusion.72
  157.1 1.9 fusion.71
  159.0 1.3 fusion.70
  160.4 2.2 fusion.73
  164.3 2.9 fusion.68
  167.4 1.4 fusion.69
  169.6 1.2 fusion.72
  170.8 1.9 fusion.71
  172.7 1.3 fusion.70
  174.0 2.2 fusion.73
  176.4 20.7 %all_to_all.48 = bf16[8,128,256]{2,1,0:T(8,128)(2,1)S(1)} all-to-all(bf16[8,128,256]{2,1,0:T(8,128)(2,1)S(1)} %bitcast.90), channel_id=1, replica_groups=mesh['dp'=64,'fsdp'=8] {'fsdp'}, dimensions={0} | all-to-all | bytes 1048576 | tf_op jit(solution)/shard_map/all_to_all | solution.py:87
  197.4 677.8 %all-gather.3.cloned.1.call-done = bf16[512,4,2048]{2,1,0:T(4,128)(2,1)} async-done(((bf16[1,4,2048]{2,1,0:T(4,128)(2,1)}), bf16[512,4,2048]{2,1,0:T(4,128)(2,1)}) %all-gather.3.cloned.1.call-update) | async-done | bytes 8388624 | tf_op jit(solution)/shard_map/all_gather | solution.py:90
  875.2 12.5 %reshape.87 = bf16[2048,2048]{1,0:T(8,128)(2,1)} reshape(bf16[512,4,2048]{2,1,0:T(4,128)(2,1)} %all-gather.3.cloned.1.call-done) | data formatting | bytes 16777216
  887.7 5.5 fusion.38
  (49 shorter events, 10.7 us)
Async XLA Ops:
  6.5 868.7 %all-gather.3.cloned.1.call-start = ((), (), s32[]{:S(2)}) async-start(), calls=%async_computation.4 | async-start | bytes 8404992 | tf_op jit(solution)/shard_map/all_gather | solution.py:90
  9.9 24.5 %all-to-all-start = ((s32[64,1,2]{2,1,0:T(1,128)}), s32[64,1,2]{2,1,0:T(1,128)S(1)}, u32[]{:S(2)}, u32[]{:S(2)}) async-start(s32[64,1,2]{2,1,0:T(1,128)} %bitcast.9), calls=%async_computation | async-start | bytes 65536 | tf_op jit(solution)/shard_map/all_to_all | solution.py:36
  34.4 44.4 %all-to-all-start.1 = ((bf16[128,8,768]{0,2,1:T(8,128)(2,1)}), bf16[128,8,768]{0,2,1:T(8,128)(2,1)S(1)}, u32[]{:S(2)}, u32[]{:S(2)}) async-start(bf16[128,8,768]{0,2,1:T(8,128)(2,1)} %bitcast), calls=%async_computation.1 | async-start | bytes 3145728 | tf_op jit(solution)/shard_map/all_to_all | solution.py:43
  78.9 57.7 %all-to-all-start.2 = ((bf16[64,2,16,512]{3,2,1,0:T(8,128)(2,1)}), bf16[64,2,16,512]{3,2,1,0:T(8,128)(2,1)}, u32[]{:S(2)}, u32[]{:S(2)}) async-start(bf16[64,2,16,512]{3,2,1,0:T(8,128)(2,1)} %bitcast.29), calls=%async_computation.2 | async-start | bytes 4194304 | tf_op jit(solution)/shard_map/all_to_all | solution.py:35
  143.0 6.0 copy-start.2
  153.7 2.2 copy-start
  157.1 1.9 copy-start.3
  159.0 1.4 copy-start.1
  167.4 2.2 copy-start
  170.8 1.9 copy-start.3
  172.7 1.4 copy-start.1
Sparse Core Ops, SparseCore 0:
  9.5 865.6 all-gather.2
where the time goes:
time: 907 us; the launch traced here: 900 us
  waiting for transfers between devices  761 us (84%)
  local copies, waits for them, and re-layouts  40.5 us (4%)
  starting transfers between devices  32.4 us (4%)
  matrix products  21.8 us (2%)
  blocking collectives  20.7 us (2%)
  between operations  13.5 us (1%)
  other arithmetic  10.2 us (1%)
    all_gather x1, waiting for transfers between devices, per_device(): lax.all_gather(out_weight, ('dp', 'fsdp'), axis=0, tiled=True)  678 us
    all_to_all x1, waiting for transfers between devices, per_device(): lax.all_to_all(packed, 'dp', split_axis=0, concat_axis=0, tiled=True)  45.4 us
    all_to_all x1, waiting for transfers between devices, per_device(): lax.all_to_all(local_qkv, 'fsdp', split_axis=1, concat_axis=0, tiled=True)  30.1 us
    all_to_all x1, blocking collectives, per_device(): lax.all_to_all(attn_heads, 'fsdp', split_axis=0, concat_axis=1, tiled=True)  20.7 us
    unnamed x6, local copies, waits for them, and re-layouts  20.3 us
  transfers between devices with their start and end apart: 4, of which 4 were waited for; matrix products, arithmetic and copies ran while one was open for 6% of the time, Pallas kernels for 0%

commit v1 on v0

--- a/solution.py
+++ b/solution.py
@@ -3,7 +3,7 @@
 import jax
 import jax.numpy as jnp
 from jax import lax
-from jax.sharding import PartitionSpec as P
+from jax.sharding import Mesh, PartitionSpec as P
 
 HD = 128
 PAGE = 16
@@ -85,16 +85,38 @@
     starts = jnp.arange(block_count, dtype=jnp.int32) * block_rows
     attn_heads = lax.map(attend, (query_blocks, starts)).reshape(group_len, heads_here * HD)
     tokens_attn = lax.all_to_all(attn_heads, "fsdp", split_axis=0, concat_axis=1, tiled=True)
-    summed = jnp.dot(
-        tokens_attn,
-        lax.all_gather(out_weight, ("dp", "fsdp"), axis=0, tiled=True),
-        preferred_element_type=jnp.float32,
-    )
+    summed = jnp.dot(tokens_attn, out_weight, preferred_element_type=jnp.float32)
     return summed.astype(jnp.bfloat16).reshape(1, tokens_here, out_weight.shape[1])
 
 
+PHYSICAL_SPLIT = {"dp": (("x", 4), ("z", 8), ("y_lo", 2)), "fsdp": (("y_hi", 4), ("core", 2))}
+
+
+def gather_rows(mesh):
+    split = [part for axis in mesh.axis_names for part in PHYSICAL_SPLIT[axis]]
+    names = tuple(name for name, _ in split)
+    fine = Mesh(mesh.devices.reshape([size for _, size in split]), names)
+
+    def body(block):
+        for name in reversed(names):
+            block = lax.all_gather(block, name, axis=0, tiled=True)
+        return block
+
+    return jax.shard_map(
+        body, mesh=fine, in_specs=P(names, None), out_specs=P(), check_vma=False
+    )
+
+
 def solution(mesh):
-    return jax.shard_map(
+    split_sizes = [math.prod(s for _, s in PHYSICAL_SPLIT[a]) for a in mesh.axis_names]
+    if tuple(split_sizes) == tuple(mesh.devices.shape):
+        gather = gather_rows(mesh)
+    else:
+        gather = jax.shard_map(
+            lambda w: lax.all_gather(w, ("dp", "fsdp"), axis=0, tiled=True),
+            mesh=mesh, in_specs=P(("dp", "fsdp"), None), out_specs=P(), check_vma=False,
+        )
+    attend_all = jax.shard_map(
         per_device,
         mesh=mesh,
         in_specs=(
@@ -102,8 +124,13 @@
             P("dp", None, "fsdp"),
             P("dp"),
             P(),
-            P(("dp", "fsdp"), None),
+            P(),
         ),
         out_specs=P("dp", "fsdp", None),
         check_vma=False,
     )
+
+    def run(group_qkv, cache_pool, page_request, request_host, out_weight):
+        return attend_all(group_qkv, cache_pool, page_request, request_host, gather(out_weight))
+
+    return run

time: 907 us -> 232 us (0.26)
  waiting for transfers between devices: 761 us -> 81.5 us
  blocking collectives: 20.7 us -> 46.2 us
  local copies, waits for them, and re-layouts: 40.5 us -> 28.2 us
    all_gather x1 -> x2, waiting for transfers between devices: 678 us -> 0.04 us  [body(): block = lax.all_gather(block, name, axis=0, tiled=True)]
    all_gather x0 -> x3, blocking collectives: none -> 24 us  [body(): block = lax.all_gather(block, name, axis=0, tiled=True)]
    unnamed x6, local copies, waits for them, and re-layouts: 20.3 us -> 7.79 us
  transfers between devices with their start and end apart: 4 -> 5, of which waited for: 4 -> 3; matrix products, arithmetic and copies ran while one was open for 6% -> 23% of each run, Pallas kernels for 0% -> 0%
where the time goes in v1:
time: 232 us; the launch traced here: 229 us
  waiting for transfers between devices  81.5 us (35%)
  blocking collectives  46.2 us (20%)
  local copies, waits for them, and re-layouts  28.2 us (12%)
  starting transfers between devices  27.4 us (12%)
  matrix products  21.8 us (9%)
  between operations  13.5 us (6%)
  other arithmetic  10.2 us (4%)
    all_to_all x1, waiting for transfers between devices, per_device(): lax.all_to_all(packed, 'dp', split_axis=0, concat_axis=0, tiled=True)  43.2 us
    all_to_all x1, waiting for transfers between devices, per_device(): lax.all_to_all(local_qkv, 'fsdp', split_axis=1, concat_axis=0, tiled=True)  31.2 us
    all_gather x3, blocking collectives, body(): block = lax.all_gather(block, name, axis=0, tiled=True)  24 us
    all_to_all x1, blocking collectives, per_device(): lax.all_to_all(attn_heads, 'fsdp', split_axis=0, concat_axis=1, tiled=True)  22.2 us
    all_to_all x1, starting transfers between devices, per_device(): lax.all_to_all(local_qkv, 'fsdp', split_axis=1, concat_axis=0, tiled=True)  10.9 us
    all_to_all x1, starting transfers between devices, per_device(): lax.all_to_all(occupied, 'dp', split_axis=0, concat_axis=0, tiled=True)  10.7 us
    unnamed x6, local copies, waits for them, and re-layouts  7.79 us
    all_to_all x1, waiting for transfers between devices, per_device(): lax.all_to_all(occupied, 'dp', split_axis=0, concat_axis=0, tiled=True)  6.58 us
  transfers between devices with their start and end apart: 5, of which 3 were waited for; matrix products, arithmetic and copies ran while one was open for 23% of the time, Pallas kernels for 0%

profile of v1, /device:TPU:1, one launch (start us, length us, event | category | flops | bytes accessed | tf_op | source)
XLA Modules:
  0.0 229.1 jit_solution(3782415318880836378)
XLA Ops:
  6.5 8.5 %all-gather = bf16[2,4,2048]{2,1,0:T(4,128)(2,1)S(1)} all-gather(bf16[1,4,2048]{2,1,0:T(4,128)(2,1)} %bitcast.91), channel_id=1, replica_groups=mesh['x'=4,'z'=8,'y_lo'=2,'y_hi'=4,'core'=2] {'core'}, dimensions={0}, use_global_device_ids=true | all-gather | bytes 49152 | tf_op jit(solution)/shard_map/all_gather | solution.py:102
  15.1 10.9 %all_gather.16 = bf16[32,2048]{1,0:T(8,128)(2,1)S(1)} all-gather(bf16[8,2048]{1,0:T(8,128)(2,1)S(1)} %reshape.87), channel_id=1, replica_groups=mesh['x'=4,'z'=8,'y_lo'=2,'y_hi'=4,'core'=2] {'y_hi'}, dimensions={0}, use_global_device_ids=true | all-gather | bytes 163840 | tf_op jit(solution)/shard_map/all_gather | solution.py:102
  26.0 4.6 %all_gather.17 = bf16[64,2048]{1,0:T(8,128)(2,1)} all-gather(bf16[32,2048]{1,0:T(8,128)(2,1)S(1)} %all_gather.16), channel_id=1, replica_groups=mesh['x'=4,'z'=8,'y_lo'=2,'y_hi'=4,'core'=2] {'y_lo'}, dimensions={0}, use_global_device_ids=true | all-gather | bytes 393216 | tf_op jit(solution)/shard_map/all_gather | solution.py:102
  33.3 10.7 %all-to-all-start = ((s32[64,1,2]{2,1,0:T(1,128)}), s32[64,1,2]{2,1,0:T(1,128)S(1)}, u32[]{:S(2)}, u32[]{:S(2)}) async-start(s32[64,1,2]{2,1,0:T(1,128)} %bitcast.9), calls=%async_computation | async-start | bytes 65536 | tf_op jit(solution)/shard_map/all_to_all | solution.py:36
  44.0 2.6 %copy.36 = bf16[1,128,6144]{1,2,0:T(8,128)(2,1)} copy(bf16[1,128,6144]{2,1,0:T(8,128)(2,1)} %param.8) | data formatting | bytes 3145728 | tf_op args[0]
  46.6 6.6 %all-to-all-done = s32[64,1,2]{2,1,0:T(1,128)S(1)} async-done(((s32[64,1,2]{2,1,0:T(1,128)}), s32[64,1,2]{2,1,0:T(1,128)S(1)}, u32[]{:S(2)}, u32[]{:S(2)}) %all-to-all-start) | async-done | bytes 544 | tf_op jit(solution)/shard_map/all_to_all | solution.py:36
  53.2 10.9 %all-to-all-start.1 = ((bf16[128,8,768]{0,2,1:T(8,128)(2,1)}), bf16[128,8,768]{0,2,1:T(8,128)(2,1)S(1)}, u32[]{:S(2)}, u32[]{:S(2)}) async-start(bf16[128,8,768]{0,2,1:T(8,128)(2,1)} %bitcast), calls=%async_computation.1 | async-start | bytes 3145728 | tf_op jit(solution)/shard_map/all_to_all | solution.py:43
  64.1 3.0 %copy.51 = bf16[16,8,16,512]{3,1,2,0:T(8,128)(2,1)S(1)} copy(bf16[16,8,16,512]{3,2,1,0:T(8,128)(2,1)} %bitcast.87) | data formatting | bytes 4194304
  67.9 2.2 copy.52
  70.1 31.2 %all-to-all-done.1 = bf16[128,8,768]{0,2,1:T(8,128)(2,1)S(1)} async-done(((bf16[128,8,768]{0,2,1:T(8,128)(2,1)}), bf16[128,8,768]{0,2,1:T(8,128)(2,1)S(1)}, u32[]{:S(2)}, u32[]{:S(2)}) %all-to-all-start.1) | async-done | bytes 1572896 | tf_op jit(solution)/shard_map/all_to_all | solution.py:43
  101.3 5.6 %all-to-all-start.2 = ((bf16[64,2,16,512]{3,2,1,0:T(8,128)(2,1)}), bf16[64,2,16,512]{3,2,1,0:T(8,128)(2,1)}, u32[]{:S(2)}, u32[]{:S(2)}) async-start(bf16[64,2,16,512]{3,2,1,0:T(8,128)(2,1)} %bitcast.29), calls=%async_computation.2 | async-start | bytes 4194304 | tf_op jit(solution)/shard_map/all_to_all | solution.py:35
  107.9 1.0 copy.37
  109.6 1.0 slice_bitcast_fusion
  111.2 43.2 %all-to-all-done.2 = bf16[64,2,16,512]{3,2,1,0:T(8,128)(2,1)} async-done(((bf16[64,2,16,512]{3,2,1,0:T(8,128)(2,1)}), bf16[64,2,16,512]{3,2,1,0:T(8,128)(2,1)}, u32[]{:S(2)}, u32[]{:S(2)}) %all-to-all-start.2) | async-done | bytes 2097184 | tf_op jit(solution)/shard_map/all_to_all | solution.py:35
  154.4 2.6 %reshape.84 = bf16[2048,2,2,128]{3,2,1,0:T(2,128)(2,1)S(1)} reshape(bf16[64,2,16,512]{3,2,1,0:T(8,128)(2,1)} %all-to-all-done.2) | data formatting | bytes 4194304 | tf_op jit(solution)/shard_map/reshape | solution.py:38
  157.0 3.9 %fusion.42 = (bf16[2048,2,1,128]{3,2,1,0:T(2,128)(2,1)}, bf16[2048,2,1,128]{3,2,1,0:T(2,128)(2,1)S(1)}) fusion(bf16[2048,2,2,128]{3,2,1,0:T(2,128)(2,1)S(1)} %reshape.84), kind=kLoop, calls=%fused_computation.51 | loop fusion | bytes 4194304 | tf_op jit(solution)/shard_map/slice | solution.py:40
  161.0 5.9 %copy.47 = bf16[2048,2,1,128]{0,3,1,2:T(8,128)(2,1)} copy(bf16[2048,2,1,128]{3,2,1,0:T(2,128)(2,1)} %get-tuple-element.136) | data formatting | bytes 2097152 | tf_op jit(solution)/shard_map/squeeze | solution.py:40
  166.9 27.4 %while.11 = (s32[]{:T(128)}, bf16[2,512,256]{2,1,0:T(8,128)(2,1)S(1)}, bf16[2,512,2,128]{3,1,0,2:T(8,128)(2,1)S(1)}, bf16[2048,2,128]{2,0,1:T(8,128)(2,1)S(1)}, ...) while((s32[]{:T(128)}, ...), condition=%wide.region_10.12_spmd.clone, body=%wide.region_5.11_spmd.clone.sunk | while | flops 1646131712 | bytes 69022040 | solution.py:86
  168.5 2.9 %fusion.68 = (f32[2,512]{1,0:T(2,128)S(1)}, f32[2,512,1024]{2,1,0:T(8,128)}) fusion(pred[512,1024]{1,0:T(8,128)(4,1)S(1)} %iota_compare_fusion.5, bf16[1024,2,128]{2,0,1:T(8,128)(2,1)S(1)} %get-tuple-element.229, bf16[2,512,2,128]{3,1,0,2:T(8,128)(2,1)S(1)} %get-tuple-element.226, s32[]{:T(128)} %get-tuple-element.214), kind=kOutput, calls=%fused_computation.10.clone.1 | convolution fusion | flops 271580160 | bytes 5509124 | tf_op jit(solution)/shard_map/while/body/eval_jaxpr/qhd,khd->hqk/dot_general | solution.py:61
  171.6 1.4 fusion.69
  173.9 1.2 fusion.72
  175.1 1.9 fusion.71
  177.0 1.3 fusion.70
  178.3 2.2 fusion.73
  182.3 2.9 %fusion.68 = (f32[2,512]{1,0:T(2,128)S(1)}, f32[2,512,1024]{2,1,0:T(8,128)}) fusion(pred[512,1024]{1,0:T(8,128)(4,1)S(1)} %iota_compare_fusion.5, bf16[1024,2,128]{2,0,1:T(8,128)(2,1)S(1)} %get-tuple-element.229, bf16[2,512,2,128]{3,1,0,2:T(8,128)(2,1)S(1)} %get-tuple-element.226, s32[]{:T(128)} %get-tuple-element.214), kind=kOutput, calls=%fused_computation.10.clone.1 | convolution fusion | flops 271580160 | bytes 5509124 | tf_op jit(solution)/shard_map/while/body/eval_jaxpr/qhd,khd->hqk/dot_general | solution.py:61
  185.3 1.4 fusion.69
  187.5 1.2 fusion.72
  188.7 1.9 fusion.71
  190.6 1.3 fusion.70
  192.0 2.2 fusion.73
  194.3 22.2 %all_to_all.48 = bf16[8,128,256]{2,1,0:T(8,128)(2,1)S(1)} all-to-all(bf16[8,128,256]{2,1,0:T(8,128)(2,1)S(1)} %bitcast.90), channel_id=1, replica_groups=mesh['x'=4,'z'=8,'y_lo'=2,'y_hi'=4,'core'=2] {'y_hi','core'}, dimensions={0} | all-to-all | bytes 1048576 | tf_op jit(solution)/shard_map/all_to_all | solution.py:87
  216.8 5.5 %fusion.38 = bf16[1,128,2048]{2,1,0:T(8,128)(2,1)} fusion(bf16[128,2048]{0,1:T(8,128)(2,1)S(1)} %bitcast.86, bf16[2048,2048]{1,0:T(8,128)(2,1)} %all-gather.6.cloned.1.call-done), kind=kOutput, calls=%fused_computation.37 | convolution fusion | flops 1074003968 | bytes 9437184 | tf_op jit(solution)/shard_map/dot_general | solution.py:88
  (55 shorter events, 11.7 us)
Async XLA Ops:
  6.5 100.6 %all-gather.4.cloned.1.call-start = ((), (), s32[]{:S(2)}) async-start(), calls=%async_computation.4 | async-start | bytes 2359296 | tf_op jit(solution)/shard_map/all_gather | solution.py:102
  33.3 19.9 %all-to-all-start = ((s32[64,1,2]{2,1,0:T(1,128)}), s32[64,1,2]{2,1,0:T(1,128)S(1)}, u32[]{:S(2)}, u32[]{:S(2)}) async-start(s32[64,1,2]{2,1,0:T(1,128)} %bitcast.9), calls=%async_computation | async-start | bytes 65536 | tf_op jit(solution)/shard_map/all_to_all | solution.py:36
  53.2 48.1 %all-to-all-start.1 = ((bf16[128,8,768]{0,2,1:T(8,128)(2,1)}), bf16[128,8,768]{0,2,1:T(8,128)(2,1)S(1)}, u32[]{:S(2)}, u32[]{:S(2)}) async-start(bf16[128,8,768]{0,2,1:T(8,128)(2,1)} %bitcast), calls=%async_computation.1 | async-start | bytes 3145728 | tf_op jit(solution)/shard_map/all_to_all | solution.py:43
  101.3 53.1 %all-to-all-start.2 = ((bf16[64,2,16,512]{3,2,1,0:T(8,128)(2,1)}), bf16[64,2,16,512]{3,2,1,0:T(8,128)(2,1)}, u32[]{:S(2)}, u32[]{:S(2)}) async-start(bf16[64,2,16,512]{3,2,1,0:T(8,128)(2,1)} %bitcast.29), calls=%async_computation.2 | async-start | bytes 4194304 | tf_op jit(solution)/shard_map/all_to_all | solution.py:35
  106.8 110.0 %all-gather.6.cloned.1.call-start = ((), (), s32[]{:S(2)}) async-start(), calls=%async_computation.5 | async-start | bytes 10485760 | tf_op jit(solution)/shard_map/all_gather | solution.py:102
  160.9 6.1 %copy-start.2 = (bf16[2,512,256]{2,1,0:T(8,128)(2,1)S(1)}, bf16[2,512,256]{2,1,0:T(8,128)(2,1)}, u32[]{:S(2)}) copy-start(bf16[2,512,256]{2,1,0:T(8,128)(2,1)} %custom-call) | copy-start | bytes 1572868
  171.6 2.3 copy-start
  175.0 1.9 copy-start.3
  176.9 1.4 copy-start.1
  185.3 2.2 copy-start
  188.7 1.9 copy-start.3
  190.6 1.4 copy-start.1
Sparse Core Ops, SparseCore 0:
  30.7 42.9 all-gather.3
  109.8 100.6 all-gather.5

commit v2 on v1

--- a/solution.py
+++ b/solution.py
@@ -29,16 +29,15 @@
     packed = jnp.einsum(
         "sp,sf->pf", chosen.astype(jnp.bfloat16), flat_pool, preferred_element_type=jnp.float32
     )
+    occupied = jnp.sum(chosen.astype(jnp.int32), axis=0) > 0
+    packed = jnp.where(occupied[:, None], packed, jnp.nan)
     packed = packed.astype(jnp.bfloat16).reshape(requests, MOST, PAGE, features)
-    occupied = jnp.sum(chosen.astype(jnp.int32), axis=0).reshape(requests, MOST)
-    arrived, present = (
-        lax.all_to_all(packed, "dp", split_axis=0, concat_axis=0, tiled=True),
-        lax.all_to_all(occupied, "dp", split_axis=0, concat_axis=0, tiled=True),
-    )
+    arrived = lax.all_to_all(packed, "dp", split_axis=0, concat_axis=0, tiled=True)
+    present = jnp.logical_not(jnp.isnan(arrived[:, :, 0, 0]))
+    live_tokens = jnp.repeat(present.reshape(requests * MOST), PAGE)
     cached = arrived.reshape(requests * MOST * PAGE, heads_here, 2, HD)
     key_cache = cached[:, :, 0]
-    value_cache = cached[:, :, 1]
-    live_tokens = jnp.repeat(present.reshape(requests * MOST), PAGE) > 0
+    value_cache = jnp.where(live_tokens[:, None, None], cached[:, :, 1], jnp.zeros((), cached.dtype))
     local_qkv = group_qkv.reshape(tokens_here, fsdp_count, heads_here * 3 * HD)
     gathered_qkv = lax.all_to_all(local_qkv, "fsdp", split_axis=1, concat_axis=0, tiled=True)
     group_len = tokens_here * fsdp_count

time: 232 us -> 257 us (1.11)
  blocking collectives: 46.2 us -> 69.6 us
  local copies, waits for them, and re-layouts: 28.2 us -> 33 us
  starting transfers between devices: 27.4 us -> 23 us
    all_gather x2, waiting for transfers between devices: 0.04 us -> 83 us  [body(): block = lax.all_gather(block, name, axis=0, tiled=True)]
    all_to_all x1, waiting for transfers between devices: 43.2 us -> 0.01 us  [per_device(): lax.all_to_all(packed, 'dp', split_axis=0, concat_axis=0, tiled=True)]
    all_to_all x1, waiting for transfers between devices: 31.2 us -> 0.01 us  [per_device(): lax.all_to_all(local_qkv, 'fsdp', split_axis=1, concat_axis=0, tiled=True)]
    all_gather x3, blocking collectives: 24 us -> 48.3 us  [body(): block = lax.all_gather(block, name, axis=0, tiled=True)]
    all_to_all x1 -> x0, starting transfers between devices: 10.7 us -> none  [per_device(): lax.all_to_all(occupied, 'dp', split_axis=0, concat_axis=0, tiled=True)]
    all_to_all x1 -> x0, waiting for transfers between devices: 6.58 us -> none  [per_device(): lax.all_to_all(occupied, 'dp', split_axis=0, concat_axis=0, tiled=True)]
    all_to_all x1, starting transfers between devices: 5.56 us -> 11.9 us  [per_device(): lax.all_to_all(packed, 'dp', split_axis=0, concat_axis=0, tiled=True)]
    squeeze x1 -> x0, local copies, waits for them, and re-layouts: 5.87 us -> none  [per_device(): value_cache = cached[:, :, 1]]
  transfers between devices with their start and end apart: 5 -> 4, of which waited for: 3 -> 2; matrix products, arithmetic and copies ran while one was open for 23% -> 22% of each run, Pallas kernels for 0% -> 0%
where the time goes in v2:
time: 257 us; the launch traced here: 256 us
  waiting for transfers between devices  83.1 us (32%)
  blocking collectives  69.6 us (27%)
  local copies, waits for them, and re-layouts  33 us (13%)
  starting transfers between devices  23 us (9%)
  matrix products  21.8 us (8%)
  between operations  13.6 us (5%)
  other arithmetic  11.8 us (5%)
    all_gather x2, waiting for transfers between devices, body(): block = lax.all_gather(block, name, axis=0, tiled=True)  83 us
    all_gather x3, blocking collectives, body(): block = lax.all_gather(block, name, axis=0, tiled=True)  48.3 us
    all_to_all x1, blocking collectives, per_device(): lax.all_to_all(attn_heads, 'fsdp', split_axis=0, concat_axis=1, tiled=True)  21.3 us
    all_to_all x1, starting transfers between devices, per_device(): lax.all_to_all(packed, 'dp', split_axis=0, concat_axis=0, tiled=True)  11.9 us
    all_to_all x1, starting transfers between devices, per_device(): lax.all_to_all(local_qkv, 'fsdp', split_axis=1, concat_axis=0, tiled=True)  11.1 us
    unnamed x15, local copies, waits for them, and re-layouts  9.17 us
    reduce_sum x4, other arithmetic, attend(): row_total = jnp.sum(cache_expo, axis=2) + jnp.sum(group_expo, axis=2)  6.12 us
    dot_general x2, matrix products, attend(): jnp.einsum('qhd,khd->hqk', query_block, new_keys, preferred_element_type=...  5.78 us
  transfers between devices with their start and end apart: 4, of which 2 were waited for; matrix products, arithmetic and copies ran while one was open for 22% of the time, Pallas kernels for 0%

profile of v2, /device:TPU:1, one launch (start us, length us, event | category | flops | bytes accessed | tf_op | source)
XLA Modules:
  0.0 256.1 jit_solution(8256035155567891996)
XLA Ops:
  6.5 2.6 %copy.40 = bf16[1,128,6144]{1,2,0:T(8,128)(2,1)} copy(bf16[1,128,6144]{2,1,0:T(8,128)(2,1)} %param.8) | data formatting | bytes 3145728 | tf_op args[0]
  9.2 11.1 %all-to-all-start.1 = ((bf16[128,8,768]{0,2,1:T(8,128)(2,1)}), bf16[128,8,768]{0,2,1:T(8,128)(2,1)}, u32[]{:S(2)}, u32[]{:S(2)}) async-start(bf16[128,8,768]{0,2,1:T(8,128)(2,1)} %bitcast), calls=%async_computation.1 | async-start | bytes 3145728 | tf_op jit(solution)/shard_map/all_to_all | solution.py:42
  20.3 1.8 all-gather
  22.1 41.9 %all_gather.16 = bf16[32,2048]{1,0:T(8,128)(2,1)S(1)} all-gather(bf16[8,2048]{1,0:T(8,128)(2,1)S(1)} %reshape.84), channel_id=1, replica_groups=mesh['x'=4,'z'=8,'y_lo'=2,'y_hi'=4,'core'=2] {'y_hi'}, dimensions={0}, use_global_device_ids=true | all-gather | bytes 163840 | tf_op jit(solution)/shard_map/all_gather | solution.py:101
  64.0 4.6 %all_gather.17 = bf16[64,2048]{1,0:T(8,128)(2,1)} all-gather(bf16[32,2048]{1,0:T(8,128)(2,1)S(1)} %all_gather.16), channel_id=1, replica_groups=mesh['x'=4,'z'=8,'y_lo'=2,'y_hi'=4,'core'=2] {'y_lo'}, dimensions={0}, use_global_device_ids=true | all-gather | bytes 393216 | tf_op jit(solution)/shard_map/all_gather | solution.py:101
  68.6 3.0 %copy.53 = bf16[16,8,16,512]{3,1,2,0:T(8,128)(2,1)S(1)} copy(bf16[16,8,16,512]{3,2,1,0:T(8,128)(2,1)} %bitcast.86) | data formatting | bytes 4194304
  73.0 2.2 copy.54
  75.3 11.9 %all-to-all-start = ((bf16[64,2,16,512]{3,2,1,0:T(8,128)(2,1)}), bf16[64,2,16,512]{3,2,1,0:T(8,128)(2,1)S(1)}, u32[]{:S(2)}, u32[]{:S(2)}) async-start(bf16[64,2,16,512]{3,2,1,0:T(8,128)(2,1)} %bitcast.83), calls=%async_computation | async-start | bytes 4194304 | tf_op jit(solution)/shard_map/all_to_all | solution.py:35
  87.2 68.5 %all-gather.4.cloned.1.call-done = bf16[512,2048]{1,0:T(8,128)(2,1)} async-done(((bf16[64,2048]{1,0:T(8,128)(2,1)}), bf16[512,2048]{1,0:T(8,128)(2,1)}) %all-gather.4.cloned.1.call-update) | async-done | bytes 2097168 | tf_op jit(solution)/shard_map/all_gather | solution.py:101
  155.7 3.6 %copy.41 = bf16[8,128,1,768]{1,0,3,2:T(8,128)(2,1)} copy(bf16[8,128,1,768]{1,3,0,2:T(8,128)(2,1)} %bitcast.2) | data formatting | bytes 3145728 | tf_op jit(solution)/shard_map/all_to_all | solution.py:42
  159.4 3.7 %reshape.80 = bf16[1024,2,3,128]{0,3,2,1:T(8,128)(2,1)} reshape(bf16[8,128,1,768]{1,0,3,2:T(8,128)(2,1)} %copy.41) | data formatting | bytes 3145728 | tf_op jit(solution)/shard_map/reshape | solution.py:44
  163.0 2.5 slice_bitcast_fusion
  165.8 1.3 copy.44
  167.2 2.4 not_reduce_fusion
  169.9 2.8 %reshape.81 = bf16[2048,2,2,128]{3,2,1,0:T(2,128)(2,1)S(1)} reshape(bf16[64,2,16,512]{3,2,1,0:T(8,128)(2,1)} %copy-done.1) | data formatting | bytes 4194304 | tf_op jit(solution)/shard_map/reshape | solution.py:38
  172.7 3.9 %fusion.43 = (bf16[2048,2,1,128]{3,2,1,0:T(2,128)(2,1)S(1)}, bf16[2048,2,1,128]{3,2,1,0:T(2,128)(2,1)}) fusion(bf16[2048,2,2,128]{3,2,1,0:T(2,128)(2,1)S(1)} %reshape.81), kind=kLoop, calls=%fused_computation.54 | loop fusion | bytes 4194304 | tf_op jit(solution)/shard_map/slice | solution.py:40
  177.2 1.3 copy.47
  178.5 1.8 copy.57
  180.3 27.4 %while.11 = (s32[]{:T(128)}, bf16[2,512,256]{2,1,0:T(8,128)(2,1)S(1)}, bf16[2,512,2,128]{3,1,0,2:T(8,128)(2,1)S(1)}, bf16[2048,2,128]{2,0,1:T(8,128)(2,1)S(1)}, ...) while((s32[]{:T(128)}, ...), condition=%wide.region_10.12_spmd.clone, body=%wide.region_5.11_spmd.clone.sunk | while | flops 1646131712 | bytes 69022040 | solution.py:85
  181.9 2.9 %fusion.69 = (f32[2,512]{1,0:T(2,128)S(1)}, f32[2,512,1024]{2,1,0:T(8,128)}) fusion(pred[512,1024]{1,0:T(8,128)(4,1)S(1)} %iota_compare_fusion.5, bf16[1024,2,128]{2,0,1:T(8,128)(2,1)S(1)} %get-tuple-element.229, bf16[2,512,2,128]{3,1,0,2:T(8,128)(2,1)S(1)} %get-tuple-element.226, s32[]{:T(128)} %get-tuple-element.214), kind=kOutput, calls=%fused_computation.10.clone.1 | convolution fusion | flops 271580160 | bytes 5509124 | tf_op jit(solution)/shard_map/while/body/eval_jaxpr/qhd,khd->hqk/dot_general | solution.py:60
  185.0 1.4 fusion.70
  188.4 1.9 fusion.72
  190.3 1.3 fusion.71
  191.6 2.2 fusion.74
  195.6 2.9 %fusion.69 = (f32[2,512]{1,0:T(2,128)S(1)}, f32[2,512,1024]{2,1,0:T(8,128)}) fusion(pred[512,1024]{1,0:T(8,128)(4,1)S(1)} %iota_compare_fusion.5, bf16[1024,2,128]{2,0,1:T(8,128)(2,1)S(1)} %get-tuple-element.229, bf16[2,512,2,128]{3,1,0,2:T(8,128)(2,1)S(1)} %get-tuple-element.226, s32[]{:T(128)} %get-tuple-element.214), kind=kOutput, calls=%fused_computation.10.clone.1 | convolution fusion | flops 271580160 | bytes 5509124 | tf_op jit(solution)/shard_map/while/body/eval_jaxpr/qhd,khd->hqk/dot_general | solution.py:60
  198.7 1.4 fusion.70
  202.1 1.9 fusion.72
  204.0 1.3 fusion.71
  205.4 2.2 fusion.74
  207.7 21.3 %all_to_all.39 = bf16[8,128,256]{2,1,0:T(8,128)(2,1)S(1)} all-to-all(bf16[8,128,256]{2,1,0:T(8,128)(2,1)S(1)} %bitcast.88), channel_id=1, replica_groups=mesh['x'=4,'z'=8,'y_lo'=2,'y_hi'=4,'core'=2] {'y_hi','core'}, dimensions={0} | all-to-all | bytes 1048576 | tf_op jit(solution)/shard_map/all_to_all | solution.py:86
  229.3 14.5 %all-gather.6.cloned.1.call-done = bf16[2048,2048]{1,0:T(8,128)(2,1)} async-done(((bf16[512,2048]{1,0:T(8,128)(2,1)}), bf16[2048,2048]{1,0:T(8,128)(2,1)}) %all-gather.6.cloned.1.call-update) | async-done | bytes 8388624 | tf_op jit(solution)/shard_map/all_gather | solution.py:101
  243.8 5.5 %fusion.39 = bf16[1,128,2048]{2,1,0:T(8,128)(2,1)} fusion(bf16[128,2048]{0,1:T(8,128)(2,1)S(1)} %bitcast.85, bf16[2048,2048]{1,0:T(8,128)(2,1)} %all-gather.6.cloned.1.call-done), kind=kOutput, calls=%fused_computation.38 | convolution fusion | flops 1074003968 | bytes 9437184 | tf_op jit(solution)/shard_map/dot_general | solution.py:87
  (64 shorter events, 10.9 us)
Async XLA Ops:
  6.5 13.8 %copy-start.5 = (bf16[4,2048]{1,0:T(4,128)(2,1)S(1)}, bf16[4,2048]{1,0:T(4,128)(2,1)}, u32[]{:S(2)}) copy-start(bf16[4,2048]{1,0:T(4,128)(2,1)} %param.12) | copy-start | bytes 49156
  9.1 62.5 %copy-start.6 = (s32[128]{0:T(128)S(1)}, s32[128]{0:T(128)}, u32[]{:S(2)}) copy-start(s32[128]{0:T(128)} %param.10) | copy-start | bytes 1540
  9.1 62.7 %copy-start.7 = (s32[64]{0:T(128)S(1)}, s32[64]{0:T(128)}, u32[]{:S(2)}) copy-start(s32[64]{0:T(128)} %param.11) | copy-start | bytes 772
  9.2 66.1 %all-to-all-start.1 = ((bf16[128,8,768]{0,2,1:T(8,128)(2,1)}), bf16[128,8,768]{0,2,1:T(8,128)(2,1)}, u32[]{:S(2)}, u32[]{:S(2)}) async-start(bf16[128,8,768]{0,2,1:T(8,128)(2,1)} %bitcast), calls=%async_computation.1 | async-start | bytes 3145728 | tf_op jit(solution)/shard_map/all_to_all | solution.py:42
  20.3 135.4 %all-gather.4.cloned.1.call-start = ((), (), s32[]{:S(2)}) async-start(), calls=%async_computation.3 | async-start | bytes 2359296 | tf_op jit(solution)/shard_map/all_gather | solution.py:101
  75.3 91.9 %all-to-all-start = ((bf16[64,2,16,512]{3,2,1,0:T(8,128)(2,1)}), bf16[64,2,16,512]{3,2,1,0:T(8,128)(2,1)S(1)}, u32[]{:S(2)}, u32[]{:S(2)}) async-start(bf16[64,2,16,512]{3,2,1,0:T(8,128)(2,1)} %bitcast.83), calls=%async_computation | async-start | bytes 4194304 | tf_op jit(solution)/shard_map/all_to_all | solution.py:35
  87.1 156.7 %all-gather.6.cloned.1.call-start = ((), (), s32[]{:S(2)}) async-start(), calls=%async_computation.4 | async-start | bytes 10485760 | tf_op jit(solution)/shard_map/all_gather | solution.py:101
  167.2 2.6 %copy-start.1 = (bf16[64,2,16,512]{3,2,1,0:T(8,128)(2,1)}, bf16[64,2,16,512]{3,2,1,0:T(8,128)(2,1)S(1)}, u32[]{:S(2)}) copy-start(bf16[64,2,16,512]{3,2,1,0:T(8,128)(2,1)S(1)} %all-to-all-done) | copy-start | bytes 6291460
  176.5 3.8 %copy-start.3 = (bf16[2,512,256]{2,1,0:T(8,128)(2,1)S(1)}, bf16[2,512,256]{2,1,0:T(8,128)(2,1)}, u32[]{:S(2)}) copy-start(bf16[2,512,256]{2,1,0:T(8,128)(2,1)} %custom-call) | copy-start | bytes 1572868
  185.0 2.2 copy-start
  188.4 1.9 copy-start.4
  190.3 1.4 copy-start.2
  198.7 2.3 copy-start
  202.1 1.9 copy-start.4
  204.0 1.4 copy-start.2
Sparse Core Ops, SparseCore 0:
  68.7 86.9 all-gather.3
  157.8 85.9 all-gather.5

commit v3 on v0

--- a/solution.py
+++ b/solution.py
@@ -3,21 +3,44 @@
 import jax
 import jax.numpy as jnp
 from jax import lax
-from jax.sharding import PartitionSpec as P
+from jax.sharding import Mesh, PartitionSpec as P
 
 HD = 128
 PAGE = 16
 MOST = 2
 
+PHYSICAL_SPLIT = {"dp": (("x", 4), ("z", 8), ("y_lo", 2)), "fsdp": (("y_hi", 4), ("core", 2))}
+DP = tuple(name for name, _ in PHYSICAL_SPLIT["dp"])
+FSDP = tuple(name for name, _ in PHYSICAL_SPLIT["fsdp"])
 
-def per_device(group_qkv, cache_pool, page_request, request_host, out_weight):
-    fsdp_count = lax.axis_size("fsdp")
+
+def per_device(group_qkv, cache_pool, page_request, request_host, out_weight, *, fsdp_count, dp_count):
     requests = request_host.shape[0]
     slot_count = page_request.shape[0]
     tokens_here = group_qkv.shape[1]
     features = cache_pool.shape[2]
     heads_here = features // (2 * HD)
     score_scale = 1.0 / math.sqrt(HD)
+    rows_here, width = out_weight.shape
+
+    local_qkv = group_qkv.reshape(tokens_here, fsdp_count, heads_here * 3 * HD)
+    rider = rows_here * width // tokens_here
+    riding = jnp.broadcast_to(
+        out_weight.reshape(tokens_here, 1, rider), (tokens_here, fsdp_count, rider)
+    )
+    outgoing = jnp.concatenate([local_qkv, riding], axis=2)
+    gathered = lax.all_to_all(outgoing, FSDP, split_axis=1, concat_axis=0, tiled=True)
+    group_len = tokens_here * fsdp_count
+    gathered_qkv = gathered[:, 0, : heads_here * 3 * HD].reshape(group_len, heads_here, 3, HD)
+    group_rows = gathered[:, 0, heads_here * 3 * HD :].reshape(fsdp_count * rows_here, width)
+
+    half = group_rows.shape[0] // 2
+    core = lax.axis_index("core")
+    mine = lax.dynamic_slice_in_dim(group_rows, core * half, half, axis=0)
+    for name in reversed(DP):
+        mine = lax.all_gather(mine, name, axis=0, tiled=True)
+    weight = lax.all_gather(mine, "core", axis=0, tiled=True)
+
     request_ids = jnp.arange(requests, dtype=jnp.int32)
     member = (page_request[:, None] == request_ids[None, :]).astype(jnp.int32)
     slot_rank = jnp.sum(member * (jnp.cumsum(member, axis=0) - 1), axis=1)
@@ -29,20 +52,16 @@
     packed = jnp.einsum(
         "sp,sf->pf", chosen.astype(jnp.bfloat16), flat_pool, preferred_element_type=jnp.float32
     )
+    occupied = jnp.sum(chosen.astype(jnp.int32), axis=0) > 0
+    packed = jnp.where(occupied[:, None], packed, jnp.nan)
     packed = packed.astype(jnp.bfloat16).reshape(requests, MOST, PAGE, features)
-    occupied = jnp.sum(chosen.astype(jnp.int32), axis=0).reshape(requests, MOST)
-    arrived, present = (
-        lax.all_to_all(packed, "dp", split_axis=0, concat_axis=0, tiled=True),
-        lax.all_to_all(occupied, "dp", split_axis=0, concat_axis=0, tiled=True),
-    )
+    arrived = lax.all_to_all(packed, DP, split_axis=0, concat_axis=0, tiled=True)
+    present = jnp.logical_not(jnp.isnan(arrived[:, :, 0, 0]))
+    live_tokens = jnp.repeat(present.reshape(requests * MOST), PAGE)
     cached = arrived.reshape(requests * MOST * PAGE, heads_here, 2, HD)
     key_cache = cached[:, :, 0]
-    value_cache = cached[:, :, 1]
-    live_tokens = jnp.repeat(present.reshape(requests * MOST), PAGE) > 0
-    local_qkv = group_qkv.reshape(tokens_here, fsdp_count, heads_here * 3 * HD)
-    gathered_qkv = lax.all_to_all(local_qkv, "fsdp", split_axis=1, concat_axis=0, tiled=True)
-    group_len = tokens_here * fsdp_count
-    gathered_qkv = gathered_qkv.reshape(group_len, heads_here, 3, HD)
+    value_cache = jnp.where(live_tokens[:, None, None], cached[:, :, 1], jnp.zeros((), cached.dtype))
+
     queries = gathered_qkv[:, :, 0]
     new_keys = gathered_qkv[:, :, 1]
     new_values = gathered_qkv[:, :, 2]
@@ -84,26 +103,28 @@
 
     starts = jnp.arange(block_count, dtype=jnp.int32) * block_rows
     attn_heads = lax.map(attend, (query_blocks, starts)).reshape(group_len, heads_here * HD)
-    tokens_attn = lax.all_to_all(attn_heads, "fsdp", split_axis=0, concat_axis=1, tiled=True)
-    summed = jnp.dot(
-        tokens_attn,
-        lax.all_gather(out_weight, ("dp", "fsdp"), axis=0, tiled=True),
-        preferred_element_type=jnp.float32,
-    )
-    return summed.astype(jnp.bfloat16).reshape(1, tokens_here, out_weight.shape[1])
+    tokens_attn = lax.all_to_all(attn_heads, FSDP, split_axis=0, concat_axis=1, tiled=True)
+    tokens_attn = tokens_attn.reshape(tokens_here, dp_count, 2, half)
+    tokens_attn = jnp.transpose(tokens_attn, (0, 2, 1, 3)).reshape(tokens_here, width)
+    summed = jnp.dot(tokens_attn, weight, preferred_element_type=jnp.float32)
+    return summed.astype(jnp.bfloat16).reshape(1, tokens_here, width)
 
 
 def solution(mesh):
+    split = [part for axis in mesh.axis_names for part in PHYSICAL_SPLIT[axis]]
+    fine = Mesh(mesh.devices.reshape([size for _, size in split]), DP + FSDP)
     return jax.shard_map(
-        per_device,
-        mesh=mesh,
+        lambda *args: per_device(
+            *args, fsdp_count=mesh.shape["fsdp"], dp_count=mesh.shape["dp"]
+        ),
+        mesh=fine,
         in_specs=(
-            P("dp", "fsdp", None),
-            P("dp", None, "fsdp"),
-            P("dp"),
+            P(DP, FSDP, None),
+            P(DP, None, FSDP),
+            P(DP),
             P(),
-            P(("dp", "fsdp"), None),
+            P(DP + FSDP, None),
         ),
-        out_specs=P("dp", "fsdp", None),
+        out_specs=P(DP, FSDP, None),
         check_vma=False,
     )

time: 907 us -> 247 us (0.27)
  waiting for transfers between devices: 761 us -> 124 us
  starting transfers between devices: 32.4 us -> 19.4 us
  local copies, waits for them, and re-layouts: 40.5 us -> 28.4 us
    all_gather x1 -> x3, waiting for transfers between devices: 678 us -> 40.3 us  [the longest x2 40.3 us: per_device(): mine = lax.all_gather(mine, name, axis=0, tiled=True)]
    all_to_all x3 -> x2, starting transfers between devices: 32.4 us -> 19.1 us  [the longest x1 10.5 us: per_device(): lax.all_to_all(outgoing, FSDP, split_axis=1, concat_axis=0, tiled=True)]
    unnamed x6 -> x14, local copies, waits for them, and re-layouts: 20.3 us -> 9.58 us
    all_to_all x3 -> x2, waiting for transfers between devices: 82.1 us -> 83.2 us  [the longest x1 42.7 us: per_device(): lax.all_to_all(packed, DP, split_axis=0, concat_axis=0, tiled=True)]
  transfers between devices with their start and end apart: 4 -> 5, of which waited for: 4 -> 4; matrix products, arithmetic and copies ran while one was open for 6% -> 20% of each run, Pallas kernels for 0% -> 0%
where the time goes in v3:
time: 247 us; the launch traced here: 246 us
  waiting for transfers between devices  124 us (50%)
  local copies, waits for them, and re-layouts  28.4 us (11%)
  blocking collectives  26.5 us (11%)
  matrix products  22.1 us (9%)
  starting transfers between devices  19.4 us (8%)
  between operations  13.3 us (5%)
  other arithmetic  13.1 us (5%)
    all_to_all x1, waiting for transfers between devices, per_device(): lax.all_to_all(packed, DP, split_axis=0, concat_axis=0, tiled=True)  42.7 us
    all_to_all x1, waiting for transfers between devices, per_device(): lax.all_to_all(outgoing, FSDP, split_axis=1, concat_axis=0, tiled=True)  40.4 us
    all_gather x2, waiting for transfers between devices, per_device(): mine = lax.all_gather(mine, name, axis=0, tiled=True)  40.3 us
    all_to_all x1, blocking collectives, per_device(): lax.all_to_all(attn_heads, FSDP, split_axis=0, concat_axis=1, tiled=True)  22.6 us
    all_to_all x1, starting transfers between devices, per_device(): lax.all_to_all(outgoing, FSDP, split_axis=1, concat_axis=0, tiled=True)  10.5 us
    unnamed x14, local copies, waits for them, and re-layouts  9.58 us
    all_to_all x1, starting transfers between devices, per_device(): lax.all_to_all(packed, DP, split_axis=0, concat_axis=0, tiled=True)  8.69 us
    reduce_sum x4, other arithmetic, attend(): row_total = jnp.sum(cache_expo, axis=2) + jnp.sum(group_expo, axis=2)  6.12 us
  transfers between devices with their start and end apart: 5, of which 4 were waited for; matrix products, arithmetic and copies ran while one was open for 20% of the time, Pallas kernels for 0%

profile of v3, /device:TPU:1, one launch (start us, length us, event | category | flops | bytes accessed | tf_op | source)
XLA Modules:
  0.0 246.5 jit_solution(3933507378928245566)
XLA Ops:
  6.5 1.9 copy.47
  9.4 1.3 pad_maximum_fusion
  10.7 10.5 %all-to-all-start.1 = ((bf16[128,8,832]{0,2,1:T(8,128)(2,1)}), bf16[128,8,832]{0,2,1:T(8,128)(2,1)S(1)}, u32[]{:S(2)}, u32[]{:S(2)}) async-start(bf16[128,8,832]{0,2,1:T(8,128)(2,1)} %pad_maximum_fusion), calls=%async_computation.1 | async-start | bytes 3407872 | tf_op jit(solution)/shard_map/all_to_all | solution.py:32
  21.2 40.4 %all-to-all-done.1 = bf16[128,8,832]{0,2,1:T(8,128)(2,1)S(1)} async-done(((bf16[128,8,832]{0,2,1:T(8,128)(2,1)}), bf16[128,8,832]{0,2,1:T(8,128)(2,1)S(1)}, u32[]{:S(2)}, u32[]{:S(2)}) %all-to-all-start.1) | async-done | bytes 1703968 | tf_op jit(solution)/shard_map/all_to_all | solution.py:32
  63.5 3.9 %all_gather.12 = bf16[32,2048]{1,0:T(8,128)(2,1)} all-gather(bf16[16,2048]{1,0:T(8,128)(2,1)S(1)} %constant_dynamic-slice_fusion), channel_id=1, replica_groups=mesh['x'=4,'z'=8,'y_lo'=2,'y_hi'=4,'core'=2] {'y_lo'}, dimensions={0}, use_global_device_ids=true | all-gather | bytes 196608 | tf_op jit(solution)/shard_map/all_gather | solution.py:41
  67.7 3.0 %copy.64 = bf16[16,8,16,512]{3,1,2,0:T(8,128)(2,1)S(1)} copy(bf16[16,8,16,512]{3,2,1,0:T(8,128)(2,1)} %bitcast.94) | data formatting | bytes 4194304
  70.9 35.2 %all-gather.4.cloned.1.call-done = bf16[256,2048]{1,0:T(8,128)(2,1)} async-done(((bf16[32,2048]{1,0:T(8,128)(2,1)}), bf16[256,2048]{1,0:T(8,128)(2,1)}) %all-gather.4.cloned.1.call-update) | async-done | bytes 1048592 | tf_op jit(solution)/shard_map/all_gather | solution.py:41
  107.1 2.2 copy.65
  109.3 8.7 %all-to-all-start = ((bf16[64,2,16,512]{3,2,1,0:T(8,128)(2,1)}), bf16[64,2,16,512]{3,2,1,0:T(8,128)(2,1)S(1)}, u32[]{:S(2)}, u32[]{:S(2)}) async-start(bf16[64,2,16,512]{3,2,1,0:T(8,128)(2,1)} %bitcast.89), calls=%async_computation | async-start | bytes 4194304 | tf_op jit(solution)/shard_map/all_to_all | solution.py:58
  118.3 1.4 slice-done
  121.1 1.3 copy.52
  122.4 42.7 %all-to-all-done = bf16[64,2,16,512]{3,2,1,0:T(8,128)(2,1)S(1)} async-done(((bf16[64,2,16,512]{3,2,1,0:T(8,128)(2,1)}), bf16[64,2,16,512]{3,2,1,0:T(8,128)(2,1)S(1)}, u32[]{:S(2)}, u32[]{:S(2)}) %all-to-all-start) | async-done | bytes 2097184 | tf_op jit(solution)/shard_map/all_to_all | solution.py:58
  165.1 2.4 not_reduce_fusion
  167.9 2.6 %reshape.85 = bf16[2048,2,2,128]{3,2,1,0:T(2,128)(2,1)S(1)} reshape(bf16[64,2,16,512]{3,2,1,0:T(8,128)(2,1)} %copy-done.1) | data formatting | bytes 4194304 | tf_op jit(solution)/shard_map/reshape | solution.py:61
  170.4 3.8 %fusion.43 = (bf16[2048,2,1,128]{3,2,1,0:T(2,128)(2,1)S(1)}, bf16[2048,2,1,128]{3,2,1,0:T(2,128)(2,1)}) fusion(bf16[2048,2,2,128]{3,2,1,0:T(2,128)(2,1)S(1)} %reshape.85), kind=kLoop, calls=%fused_computation.57 | loop fusion | bytes 4194304 | tf_op jit(solution)/shard_map/slice | solution.py:63
  174.9 1.3 copy.55
  176.3 1.8 copy.69
  178.1 5.0 %all-gather.6.cloned.1.call-done = bf16[1024,2048]{1,0:T(8,128)(2,1)} async-done(((bf16[256,2048]{1,0:T(8,128)(2,1)}), bf16[1024,2048]{1,0:T(8,128)(2,1)}) %all-gather.6.cloned.1.call-update) | async-done | bytes 4194320 | tf_op jit(solution)/shard_map/all_gather | solution.py:41
  183.2 28.4 %while.11 = (s32[]{:T(128)}, bf16[2,512,256]{2,1,0:T(8,128)(2,1)S(1)}, bf16[2,512,2,128]{3,1,0,2:T(8,128)(2,1)S(1)}, bf16[2048,2,128]{2,0,1:T(8,128)(2,1)S(1)}, ...) while((s32[]{:T(128)}, ...), condition=%wide.region_10.11_spmd.clone, body=%wide.region_5.10_spmd.clone.sunk | while | flops 1646131712 | bytes 69022040 | solution.py:105
  184.8 2.9 %fusion.70 = (f32[2,512]{1,0:T(2,128)S(1)}, f32[2,512,1024]{2,1,0:T(8,128)}) fusion(pred[512,1024]{1,0:T(8,128)(4,1)S(1)} %iota_compare_fusion.5, bf16[1024,2,128]{2,0,1:T(8,128)(2,1)S(1)} %get-tuple-element.228, bf16[2,512,2,128]{3,1,0,2:T(8,128)(2,1)S(1)} %get-tuple-element.225, s32[]{:T(128)} %get-tuple-element.213), kind=kOutput, calls=%fused_computation.10.clone.1 | convolution fusion | flops 271580160 | bytes 5509124 | tf_op jit(solution)/shard_map/while/body/eval_jaxpr/qhd,khd->hqk/dot_general | solution.py:80
  187.9 1.4 fusion.71
  191.2 1.9 fusion.73
  193.1 1.3 fusion.72
  194.5 2.2 fusion.75
  198.4 3.1 %fusion.70 = (f32[2,512]{1,0:T(2,128)S(1)}, f32[2,512,1024]{2,1,0:T(8,128)}) fusion(pred[512,1024]{1,0:T(8,128)(4,1)S(1)} %iota_compare_fusion.5, bf16[1024,2,128]{2,0,1:T(8,128)(2,1)S(1)} %get-tuple-element.228, bf16[2,512,2,128]{3,1,0,2:T(8,128)(2,1)S(1)} %get-tuple-element.225, s32[]{:T(128)} %get-tuple-element.213), kind=kOutput, calls=%fused_computation.10.clone.1 | convolution fusion | flops 271580160 | bytes 5509124 | tf_op jit(solution)/shard_map/while/body/eval_jaxpr/qhd,khd->hqk/dot_general | solution.py:80
  201.8 1.4 fusion.71
  203.2 1.6 copy-done
  206.0 1.9 fusion.73
  207.9 1.3 fusion.72
  209.2 2.2 fusion.75
  211.5 22.6 %all_to_all.39 = bf16[8,128,256]{2,1,0:T(8,128)(2,1)S(1)} all-to-all(bf16[8,128,256]{2,1,0:T(8,128)(2,1)S(1)} %bitcast.97), channel_id=1, replica_groups=mesh['x'=4,'z'=8,'y_lo'=2,'y_hi'=4,'core'=2] {'y_hi','core'}, dimensions={0} | all-to-all | bytes 1048576 | tf_op jit(solution)/shard_map/all_to_all | solution.py:106
  234.5 5.5 %fusion.39 = bf16[1,128,2048]{2,1,0:T(8,128)(2,1)} fusion(bf16[128,2048]{0,1:T(8,128)(2,1)S(1)} %bitcast.93, bf16[2048,2048]{1,0:T(8,128)(2,1)} %all-gather.8.cloned.1.call-done), kind=kOutput, calls=%fused_computation.38 | convolution fusion | flops 1074003968 | bytes 9437184 | tf_op jit(solution)/shard_map/dot_general | solution.py:109
  (74 shorter events, 14.3 us)
Async XLA Ops:
  10.7 56.8 %copy-start.6 = (s32[128]{0:T(128)S(1)}, s32[128]{0:T(128)}, u32[]{:S(2)}) copy-start(s32[128]{0:T(128)} %param.9) | copy-start | bytes 1540
  10.7 50.9 %all-to-all-start.1 = ((bf16[128,8,832]{0,2,1:T(8,128)(2,1)}), bf16[128,8,832]{0,2,1:T(8,128)(2,1)S(1)}, u32[]{:S(2)}, u32[]{:S(2)}) async-start(bf16[128,8,832]{0,2,1:T(8,128)(2,1)} %pad_maximum_fusion), calls=%async_computation.1 | async-start | bytes 3407872 | tf_op jit(solution)/shard_map/all_to_all | solution.py:32
  21.2 85.0 %all-gather.4.cloned.1.call-start = ((), (), s32[]{:S(2)}) async-start(), calls=%async_computation.3 | async-start | bytes 1179648 | tf_op jit(solution)/shard_map/all_gather | solution.py:41
  21.2 49.6 %copy-start.7 = (s32[64]{0:T(128)S(1)}, s32[64]{0:T(128)}, u32[]{:S(2)}) copy-start(s32[64]{0:T(128)} %param.10) | copy-start | bytes 772
  61.8 1.2 copy-start.2
  67.4 115.7 %all-gather.6.cloned.1.call-start = ((), (), s32[]{:S(2)}) async-start(), calls=%async_computation.4 | async-start | bytes 5242880 | tf_op jit(solution)/shard_map/all_gather | solution.py:41
  109.3 55.8 %all-to-all-start = ((bf16[64,2,16,512]{3,2,1,0:T(8,128)(2,1)}), bf16[64,2,16,512]{3,2,1,0:T(8,128)(2,1)S(1)}, u32[]{:S(2)}, u32[]{:S(2)}) async-start(bf16[64,2,16,512]{3,2,1,0:T(8,128)(2,1)} %bitcast.89), calls=%async_computation | async-start | bytes 4194304 | tf_op jit(solution)/shard_map/all_to_all | solution.py:58
  118.0 116.5 %all-gather.8.cloned.1.call-start = ((), (), s32[]{:S(2)}) async-start(), calls=%async_computation.5 | async-start | bytes 12582912 | tf_op jit(solution)/shard_map/all_gather | solution.py:42
  118.3 1.4 slice-start
  165.1 2.6 %copy-start.1 = (bf16[64,2,16,512]{3,2,1,0:T(8,128)(2,1)}, bf16[64,2,16,512]{3,2,1,0:T(8,128)(2,1)S(1)}, u32[]{:S(2)}) copy-start(bf16[64,2,16,512]{3,2,1,0:T(8,128)(2,1)S(1)} %all-to-all-done) | copy-start | bytes 6291460
  176.3 6.9 %copy-start.4 = (bf16[2,512,256]{2,1,0:T(8,128)(2,1)S(1)}, bf16[2,512,256]{2,1,0:T(8,128)(2,1)}, u32[]{:S(2)}) copy-start(bf16[2,512,256]{2,1,0:T(8,128)(2,1)} %custom-call) | copy-start | bytes 1572868
  187.9 2.2 copy-start
  191.2 1.9 copy-start.5
  193.1 1.4 copy-start.3
  201.8 3.0 %copy-start = (f32[2,512,1024]{2,1,0:T(8,128)S(1)}, f32[2,512,1024]{2,1,0:T(8,128)}, u32[]{:S(2)}) copy-start(f32[2,512,1024]{2,1,0:T(8,128)} %get-tuple-element.199) | copy-start | bytes 12582916 | tf_op jit(solution)/shard_map/while
  205.9 1.9 copy-start.5
  207.8 1.4 copy-start.3
Sparse Core Ops, SparseCore 0:
  67.5 38.5 all-gather.3
  108.3 74.8 all-gather.5
  185.2 27.4 all-gather.7

commit v4 on v3

--- a/solution.py
+++ b/solution.py
@@ -37,8 +37,8 @@
     half = group_rows.shape[0] // 2
     core = lax.axis_index("core")
     mine = lax.dynamic_slice_in_dim(group_rows, core * half, half, axis=0)
-    for name in reversed(DP):
-        mine = lax.all_gather(mine, name, axis=0, tiled=True)
+    mine = lax.all_gather(mine, DP[-1], axis=0, tiled=True)
+    mine = lax.all_gather(mine, DP[:-1], axis=0, tiled=True)
     weight = lax.all_gather(mine, "core", axis=0, tiled=True)
 
     request_ids = jnp.arange(requests, dtype=jnp.int32)

time: 247 us -> 246 us (level)
  waiting for transfers between devices: 124 us -> 116 us
  blocking collectives: 26.5 us -> 30.5 us
    all_gather x2 -> x1, waiting for transfers between devices: 40.3 us -> 26.7 us  [per_device(): mine = lax.all_gather(mine, DP[:-1], axis=0, tiled=True)]
    all_to_all x1, waiting for transfers between devices: 42.7 us -> 48.6 us  [per_device(): lax.all_to_all(packed, DP, split_axis=0, concat_axis=0, tiled=True)]
    all_to_all x1, blocking collectives: 22.6 us -> 26.6 us  [per_device(): lax.all_to_all(attn_heads, FSDP, split_axis=0, concat_axis=1, tiled=True)]
  transfers between devices with their start and end apart: 5 -> 4, of which waited for: 4 -> 3; matrix products, arithmetic and copies ran while one was open for 20% -> 20% of each run, Pallas kernels for 0% -> 0%
where the time goes in v4:
time: 246 us
  waiting for transfers between devices  116 us (47%)
  blocking collectives  30.5 us (12%)
  local copies, waits for them, and re-layouts  28.6 us (12%)
  matrix products  21.9 us (9%)
  starting transfers between devices  21.8 us (9%)
  between operations  13.6 us (6%)
  other arithmetic  13.1 us (5%)
    all_to_all x1, waiting for transfers between devices, per_device(): lax.all_to_all(packed, DP, split_axis=0, concat_axis=0, tiled=True)  48.6 us
    all_to_all x1, waiting for transfers between devices, per_device(): lax.all_to_all(outgoing, FSDP, split_axis=1, concat_axis=0, tiled=True)  40.4 us
    all_gather x1, waiting for transfers between devices, per_device(): mine = lax.all_gather(mine, DP[:-1], axis=0, tiled=True)  26.7 us
    all_to_all x1, blocking collectives, per_device(): lax.all_to_all(attn_heads, FSDP, split_axis=0, concat_axis=1, tiled=True)  26.6 us
    all_to_all x1, starting transfers between devices, per_device(): lax.all_to_all(packed, DP, split_axis=0, concat_axis=0, tiled=True)  11.1 us
    all_to_all x1, starting transfers between devices, per_device(): lax.all_to_all(outgoing, FSDP, split_axis=1, concat_axis=0, tiled=True)  10.5 us
    unnamed x14, local copies, waits for them, and re-layouts  9.58 us
    reduce_sum x4, other arithmetic, attend(): row_total = jnp.sum(cache_expo, axis=2) + jnp.sum(group_expo, axis=2)  6.12 us
  transfers between devices with their start and end apart: 4, of which 3 were waited for; matrix products, arithmetic and copies ran while one was open for 20% of the time, Pallas kernels for 0%

profile of v4, /device:TPU:1, one launch (start us, length us, event | category | flops | bytes accessed | tf_op | source)
XLA Modules:
  0.0 245.5 jit_solution(3133209257337582483)
XLA Ops:
  6.5 1.9 copy.47
  9.4 1.3 pad_maximum_fusion
  10.7 10.5 %all-to-all-start.1 = ((bf16[128,8,832]{0,2,1:T(8,128)(2,1)}), bf16[128,8,832]{0,2,1:T(8,128)(2,1)S(1)}, u32[]{:S(2)}, u32[]{:S(2)}) async-start(bf16[128,8,832]{0,2,1:T(8,128)(2,1)} %pad_maximum_fusion), calls=%async_computation.1 | async-start | bytes 3407872 | tf_op jit(solution)/shard_map/all_to_all | solution.py:32
  21.2 40.4 %all-to-all-done.1 = bf16[128,8,832]{0,2,1:T(8,128)(2,1)S(1)} async-done(((bf16[128,8,832]{0,2,1:T(8,128)(2,1)}), bf16[128,8,832]{0,2,1:T(8,128)(2,1)S(1)}, u32[]{:S(2)}, u32[]{:S(2)}) %all-to-all-start.1) | async-done | bytes 1703968 | tf_op jit(solution)/shard_map/all_to_all | solution.py:32
  61.8 1.2 copy-done.2
  63.5 3.9 %all_gather.9 = bf16[32,2048]{1,0:T(8,128)(2,1)} all-gather(bf16[16,2048]{1,0:T(8,128)(2,1)S(1)} %constant_dynamic-slice_fusion), channel_id=1, replica_groups=mesh['x'=4,'z'=8,'y_lo'=2,'y_hi'=4,'core'=2] {'y_lo'}, dimensions={0}, use_global_device_ids=true | all-gather | bytes 196608 | tf_op jit(solution)/shard_map/all_gather | solution.py:40
  67.7 3.0 %copy.64 = bf16[16,8,16,512]{3,1,2,0:T(8,128)(2,1)S(1)} copy(bf16[16,8,16,512]{3,2,1,0:T(8,128)(2,1)} %bitcast.94) | data formatting | bytes 4194304
  71.8 2.2 copy.65
  74.0 11.1 %all-to-all-start = ((bf16[64,2,16,512]{3,2,1,0:T(8,128)(2,1)}), bf16[64,2,16,512]{3,2,1,0:T(8,128)(2,1)S(1)}, u32[]{:S(2)}, u32[]{:S(2)}) async-start(bf16[64,2,16,512]{3,2,1,0:T(8,128)(2,1)} %bitcast.89), calls=%async_computation | async-start | bytes 4194304 | tf_op jit(solution)/shard_map/all_to_all | solution.py:58
  85.4 1.4 slice-done
  88.3 1.3 copy.52
  89.6 48.6 %all-to-all-done = bf16[64,2,16,512]{3,2,1,0:T(8,128)(2,1)S(1)} async-done(((bf16[64,2,16,512]{3,2,1,0:T(8,128)(2,1)}), bf16[64,2,16,512]{3,2,1,0:T(8,128)(2,1)S(1)}, u32[]{:S(2)}, u32[]{:S(2)}) %all-to-all-start) | async-done | bytes 2097184 | tf_op jit(solution)/shard_map/all_to_all | solution.py:58
  138.1 2.4 not_reduce_fusion
  140.9 2.6 %reshape.85 = bf16[2048,2,2,128]{3,2,1,0:T(2,128)(2,1)S(1)} reshape(bf16[64,2,16,512]{3,2,1,0:T(8,128)(2,1)} %copy-done.1) | data formatting | bytes 4194304 | tf_op jit(solution)/shard_map/reshape | solution.py:61
  143.4 3.8 %fusion.43 = (bf16[2048,2,1,128]{3,2,1,0:T(2,128)(2,1)S(1)}, bf16[2048,2,1,128]{3,2,1,0:T(2,128)(2,1)}) fusion(bf16[2048,2,2,128]{3,2,1,0:T(2,128)(2,1)S(1)} %reshape.85), kind=kLoop, calls=%fused_computation.57 | loop fusion | bytes 4194304 | tf_op jit(solution)/shard_map/slice | solution.py:63
  147.9 1.3 copy.55
  149.3 1.8 copy.69
  151.1 26.7 %all-gather.3.cloned.1.call-done = bf16[1024,2048]{1,0:T(8,128)(2,1)} async-done(((bf16[32,2048]{1,0:T(8,128)(2,1)}), bf16[1024,2048]{1,0:T(8,128)(2,1)}) %all-gather.3.cloned.1.call-update) | async-done | bytes 4194320 | tf_op jit(solution)/shard_map/all_gather | solution.py:41
  177.8 28.4 %while.11 = (s32[]{:T(128)}, bf16[2,512,256]{2,1,0:T(8,128)(2,1)S(1)}, bf16[2,512,2,128]{3,1,0,2:T(8,128)(2,1)S(1)}, bf16[2048,2,128]{2,0,1:T(8,128)(2,1)S(1)}, ...) while((s32[]{:T(128)}, ...), condition=%wide.region_10.11_spmd.clone, body=%wide.region_5.10_spmd.clone.sunk | while | flops 1646131712 | bytes 69022040 | solution.py:105
  179.4 2.9 %fusion.70 = (f32[2,512]{1,0:T(2,128)S(1)}, f32[2,512,1024]{2,1,0:T(8,128)}) fusion(pred[512,1024]{1,0:T(8,128)(4,1)S(1)} %iota_compare_fusion.5, bf16[1024,2,128]{2,0,1:T(8,128)(2,1)S(1)} %get-tuple-element.228, bf16[2,512,2,128]{3,1,0,2:T(8,128)(2,1)S(1)} %get-tuple-element.225, s32[]{:T(128)} %get-tuple-element.213), kind=kOutput, calls=%fused_computation.10.clone.1 | convolution fusion | flops 271580160 | bytes 5509124 | tf_op jit(solution)/shard_map/while/body/eval_jaxpr/qhd,khd->hqk/dot_general | solution.py:80
  182.5 1.4 fusion.71
  185.9 1.9 fusion.73
  187.8 1.3 fusion.72
  189.1 2.2 fusion.75
  193.1 3.0 %fusion.70 = (f32[2,512]{1,0:T(2,128)S(1)}, f32[2,512,1024]{2,1,0:T(8,128)}) fusion(pred[512,1024]{1,0:T(8,128)(4,1)S(1)} %iota_compare_fusion.5, bf16[1024,2,128]{2,0,1:T(8,128)(2,1)S(1)} %get-tuple-element.228, bf16[2,512,2,128]{3,1,0,2:T(8,128)(2,1)S(1)} %get-tuple-element.225, s32[]{:T(128)} %get-tuple-element.213), kind=kOutput, calls=%fused_computation.10.clone.1 | convolution fusion | flops 271580160 | bytes 5509124 | tf_op jit(solution)/shard_map/while/body/eval_jaxpr/qhd,khd->hqk/dot_general | solution.py:80
  196.3 1.4 fusion.71
  197.7 1.6 copy-done
  200.5 1.9 fusion.73
  202.4 1.3 fusion.72
  203.9 2.1 fusion.75
  206.2 26.6 %all_to_all.39 = bf16[8,128,256]{2,1,0:T(8,128)(2,1)S(1)} all-to-all(bf16[8,128,256]{2,1,0:T(8,128)(2,1)S(1)} %bitcast.97), channel_id=1, replica_groups=mesh['x'=4,'z'=8,'y_lo'=2,'y_hi'=4,'core'=2] {'y_hi','core'}, dimensions={0} | all-to-all | bytes 1048576 | tf_op jit(solution)/shard_map/all_to_all | solution.py:106
  233.2 5.5 %fusion.39 = bf16[1,128,2048]{2,1,0:T(8,128)(2,1)} fusion(bf16[128,2048]{0,1:T(8,128)(2,1)S(1)} %bitcast.93, bf16[2048,2048]{1,0:T(8,128)(2,1)} %all-gather.5.cloned.1.call-done), kind=kOutput, calls=%fused_computation.38 | convolution fusion | flops 1074003968 | bytes 9437184 | tf_op jit(solution)/shard_map/dot_general | solution.py:109
  (71 shorter events, 13.3 us)
Async XLA Ops:
  10.7 56.7 %copy-start.6 = (s32[128]{0:T(128)S(1)}, s32[128]{0:T(128)}, u32[]{:S(2)}) copy-start(s32[128]{0:T(128)} %param.9) | copy-start | bytes 1540
  10.7 50.9 %all-to-all-start.1 = ((bf16[128,8,832]{0,2,1:T(8,128)(2,1)}), bf16[128,8,832]{0,2,1:T(8,128)(2,1)S(1)}, u32[]{:S(2)}, u32[]{:S(2)}) async-start(bf16[128,8,832]{0,2,1:T(8,128)(2,1)} %pad_maximum_fusion), calls=%async_computation.1 | async-start | bytes 3407872 | tf_op jit(solution)/shard_map/all_to_all | solution.py:32
  21.2 156.6 %all-gather.3.cloned.1.call-start = ((), (), s32[]{:S(2)}) async-start(), calls=%async_computation.3 | async-start | bytes 4325376 | tf_op jit(solution)/shard_map/all_gather | solution.py:41
  21.2 49.5 %copy-start.7 = (s32[64]{0:T(128)S(1)}, s32[64]{0:T(128)}, u32[]{:S(2)}) copy-start(s32[64]{0:T(128)} %param.10) | copy-start | bytes 772
  61.8 1.2 copy-start.2
  74.0 64.1 %all-to-all-start = ((bf16[64,2,16,512]{3,2,1,0:T(8,128)(2,1)}), bf16[64,2,16,512]{3,2,1,0:T(8,128)(2,1)S(1)}, u32[]{:S(2)}, u32[]{:S(2)}) async-start(bf16[64,2,16,512]{3,2,1,0:T(8,128)(2,1)} %bitcast.89), calls=%async_computation | async-start | bytes 4194304 | tf_op jit(solution)/shard_map/all_to_all | solution.py:58
  85.2 148.0 %all-gather.5.cloned.1.call-start = ((), (), s32[]{:S(2)}) async-start(), calls=%async_computation.4 | async-start | bytes 12582912 | tf_op jit(solution)/shard_map/all_gather | solution.py:42
  85.4 1.4 slice-start
  138.1 2.6 %copy-start.1 = (bf16[64,2,16,512]{3,2,1,0:T(8,128)(2,1)}, bf16[64,2,16,512]{3,2,1,0:T(8,128)(2,1)S(1)}, u32[]{:S(2)}) copy-start(bf16[64,2,16,512]{3,2,1,0:T(8,128)(2,1)S(1)} %all-to-all-done) | copy-start | bytes 6291460
  149.2 28.6 %copy-start.4 = (bf16[2,512,256]{2,1,0:T(8,128)(2,1)S(1)}, bf16[2,512,256]{2,1,0:T(8,128)(2,1)}, u32[]{:S(2)}) copy-start(bf16[2,512,256]{2,1,0:T(8,128)(2,1)} %custom-call) | copy-start | bytes 1572868
  182.5 2.2 copy-start
  185.9 1.9 copy-start.5
  187.8 1.4 copy-start.3
  196.3 3.0 %copy-start = (f32[2,512,1024]{2,1,0:T(8,128)S(1)}, f32[2,512,1024]{2,1,0:T(8,128)}, u32[]{:S(2)}) copy-start(f32[2,512,1024]{2,1,0:T(8,128)} %get-tuple-element.199) | copy-start | bytes 12582916 | tf_op jit(solution)/shard_map/while
  200.5 1.9 copy-start.5
  202.4 1.5 copy-start.3
Sparse Core Ops, SparseCore 0:
  67.5 110.1 all-gather.2
  179.9 29.4 all-gather.4

commit v5 on v4

--- a/solution.py
+++ b/solution.py
@@ -21,25 +21,18 @@
     features = cache_pool.shape[2]
     heads_here = features // (2 * HD)
     score_scale = 1.0 / math.sqrt(HD)
-    rows_here, width = out_weight.shape
+    width = out_weight.shape[1]
+
+    weight = out_weight
+    for name in reversed(DP[2:] + FSDP):
+        weight = lax.all_gather(weight, name, axis=0, tiled=True)
+    weight, group_qkv = lax.optimization_barrier((weight, group_qkv))
+    weight = lax.all_gather(weight, DP[1], axis=0, tiled=True)
 
     local_qkv = group_qkv.reshape(tokens_here, fsdp_count, heads_here * 3 * HD)
-    rider = rows_here * width // tokens_here
-    riding = jnp.broadcast_to(
-        out_weight.reshape(tokens_here, 1, rider), (tokens_here, fsdp_count, rider)
-    )
-    outgoing = jnp.concatenate([local_qkv, riding], axis=2)
-    gathered = lax.all_to_all(outgoing, FSDP, split_axis=1, concat_axis=0, tiled=True)
+    gathered_qkv = lax.all_to_all(local_qkv, FSDP, split_axis=1, concat_axis=0, tiled=True)
     group_len = tokens_here * fsdp_count
-    gathered_qkv = gathered[:, 0, : heads_here * 3 * HD].reshape(group_len, heads_here, 3, HD)
-    group_rows = gathered[:, 0, heads_here * 3 * HD :].reshape(fsdp_count * rows_here, width)
-
-    half = group_rows.shape[0] // 2
-    core = lax.axis_index("core")
-    mine = lax.dynamic_slice_in_dim(group_rows, core * half, half, axis=0)
-    mine = lax.all_gather(mine, DP[-1], axis=0, tiled=True)
-    mine = lax.all_gather(mine, DP[:-1], axis=0, tiled=True)
-    weight = lax.all_gather(mine, "core", axis=0, tiled=True)
+    gathered_qkv = gathered_qkv.reshape(group_len, heads_here, 3, HD)
 
     request_ids = jnp.arange(requests, dtype=jnp.int32)
     member = (page_request[:, None] == request_ids[None, :]).astype(jnp.int32)
@@ -55,6 +48,8 @@
     occupied = jnp.sum(chosen.astype(jnp.int32), axis=0) > 0
     packed = jnp.where(occupied[:, None], packed, jnp.nan)
     packed = packed.astype(jnp.bfloat16).reshape(requests, MOST, PAGE, features)
+    weight, packed = lax.optimization_barrier((weight, packed))
+    weight = lax.all_gather(weight, DP[0], axis=0, tiled=True)
     arrived = lax.all_to_all(packed, DP, split_axis=0, concat_axis=0, tiled=True)
     present = jnp.logical_not(jnp.isnan(arrived[:, :, 0, 0]))
     live_tokens = jnp.repeat(present.reshape(requests * MOST), PAGE)
@@ -104,8 +99,6 @@
     starts = jnp.arange(block_count, dtype=jnp.int32) * block_rows
     attn_heads = lax.map(attend, (query_blocks, starts)).reshape(group_len, heads_here * HD)
     tokens_attn = lax.all_to_all(attn_heads, FSDP, split_axis=0, concat_axis=1, tiled=True)
-    tokens_attn = tokens_attn.reshape(tokens_here, dp_count, 2, half)
-    tokens_attn = jnp.transpose(tokens_attn, (0, 2, 1, 3)).reshape(tokens_here, width)
     summed = jnp.dot(tokens_attn, weight, preferred_element_type=jnp.float32)
     return summed.astype(jnp.bfloat16).reshape(1, tokens_here, width)
 

time: 246 us -> 216 us (0.88)
  waiting for transfers between devices: 116 us -> 66.8 us
  blocking collectives: 30.5 us -> 46 us
  local copies, waits for them, and re-layouts: 28.6 us -> 32.8 us
    all_to_all x1, waiting for transfers between devices: 40.4 us -> 5.23 us  [per_device(): lax.all_to_all(local_qkv, FSDP, split_axis=1, concat_axis=0, tiled=True)]
    all_gather x1 -> x3, blocking collectives: 3.89 us -> 24 us  [per_device(): weight = lax.all_gather(weight, name, axis=0, tiled=True)]
    all_to_all x1, waiting for transfers between devices: 48.6 us -> 35.8 us  [per_device(): lax.all_to_all(packed, DP, split_axis=0, concat_axis=0, tiled=True)]
    all_to_all x1, blocking collectives: 26.6 us -> 22 us  [per_device(): lax.all_to_all(attn_heads, FSDP, split_axis=0, concat_axis=1, tiled=True)]
    reshape x0 -> x1, local copies, waits for them, and re-layouts: none -> 3.68 us  [per_device(): gathered_qkv = gathered_qkv.reshape(group_len, heads_here, 3, HD)]
    all_to_all x1, local copies, waits for them, and re-layouts: 0.24 us -> 3.6 us  [per_device(): lax.all_to_all(local_qkv, FSDP, split_axis=1, concat_axis=0, tiled=True)]
    unnamed x14 -> x12, local copies, waits for them, and re-layouts: 9.58 us -> 6.55 us
    optimization_barrier x0 -> x1, local copies, waits for them, and re-layouts: none -> 2.6 us  [per_device(): weight, group_qkv = lax.optimization_barrier((weight, group_qkv))]
  transfers between devices with their start and end apart: 4 -> 4, of which waited for: 3 -> 3; matrix products, arithmetic and copies ran while one was open for 20% -> 28% of each run, Pallas kernels for 0% -> 0%
where the time goes in v5:
time: 216 us; the launch traced here: 215 us
  waiting for transfers between devices  66.8 us (31%)
  blocking collectives  46 us (21%)
  local copies, waits for them, and re-layouts  32.8 us (15%)
  starting transfers between devices  22.4 us (10%)
  matrix products  21.8 us (10%)
  between operations  13.5 us (6%)
  other arithmetic  11.8 us (5%)
    all_to_all x1, waiting for transfers between devices, per_device(): lax.all_to_all(packed, DP, split_axis=0, concat_axis=0, tiled=True)  35.8 us
    all_gather x1, waiting for transfers between devices, per_device(): weight = lax.all_gather(weight, DP[1], axis=0, tiled=True)  25 us
    all_gather x3, blocking collectives, per_device(): weight = lax.all_gather(weight, name, axis=0, tiled=True)  24 us
    all_to_all x1, blocking collectives, per_device(): lax.all_to_all(attn_heads, FSDP, split_axis=0, concat_axis=1, tiled=True)  22 us
    all_to_all x1, starting transfers between devices, per_device(): lax.all_to_all(packed, DP, split_axis=0, concat_axis=0, tiled=True)  13.5 us
    all_to_all x1, starting transfers between devices, per_device(): lax.all_to_all(local_qkv, FSDP, split_axis=1, concat_axis=0, tiled=True)  8.87 us
    unnamed x12, local copies, waits for them, and re-layouts  6.55 us
    reduce_sum x4, other arithmetic, attend(): row_total = jnp.sum(cache_expo, axis=2) + jnp.sum(group_expo, axis=2)  6.12 us
  transfers between devices with their start and end apart: 4, of which 3 were waited for; matrix products, arithmetic and copies ran while one was open for 28% of the time, Pallas kernels for 0%

profile of v5, /device:TPU:1, one launch (start us, length us, event | category | flops | bytes accessed | tf_op | source)
XLA Modules:
  0.0 215.4 jit_solution(14413602714746578815)
XLA Ops:
  6.5 8.5 %all-gather = bf16[2,4,2048]{2,1,0:T(4,128)(2,1)S(1)} all-gather(bf16[1,4,2048]{2,1,0:T(4,128)(2,1)} %bitcast.89), channel_id=1, replica_groups=mesh['x'=4,'z'=8,'y_lo'=2,'y_hi'=4,'core'=2] {'core'}, dimensions={0}, use_global_device_ids=true | all-gather | bytes 49152 | tf_op jit(solution)/shard_map/all_gather | solution.py:28
  15.1 10.9 %all_gather.16 = bf16[32,2048]{1,0:T(8,128)(2,1)S(1)} all-gather(bf16[8,2048]{1,0:T(8,128)(2,1)S(1)} %reshape.84), channel_id=1, replica_groups=mesh['x'=4,'z'=8,'y_lo'=2,'y_hi'=4,'core'=2] {'y_hi'}, dimensions={0}, use_global_device_ids=true | all-gather | bytes 163840 | tf_op jit(solution)/shard_map/all_gather | solution.py:28
  26.0 4.6 %all_gather.17 = bf16[64,2048]{1,0:T(8,128)(2,1)} all-gather(bf16[32,2048]{1,0:T(8,128)(2,1)S(1)} %all_gather.16), channel_id=1, replica_groups=mesh['x'=4,'z'=8,'y_lo'=2,'y_hi'=4,'core'=2] {'y_lo'}, dimensions={0}, use_global_device_ids=true | all-gather | bytes 393216 | tf_op jit(solution)/shard_map/all_gather | solution.py:28
  30.6 2.6 %copy.38 = bf16[1,128,6144]{1,2,0:T(8,128)(2,1)} copy(bf16[1,128,6144]{2,1,0:T(8,128)(2,1)} %param.7) | data formatting | bytes 3145728 | tf_op jit(solution)/shard_map/optimization_barrier | solution.py:29
  33.2 8.9 %all-to-all-start.1 = ((bf16[128,8,768]{0,2,1:T(8,128)(2,1)}), bf16[128,8,768]{0,2,1:T(8,128)(2,1)}, u32[]{:S(2)}, u32[]{:S(2)}) async-start(bf16[128,8,768]{0,2,1:T(8,128)(2,1)} %bitcast.1), calls=%async_computation.1 | async-start | bytes 3145728 | tf_op jit(solution)/shard_map/all_to_all | solution.py:33
  42.1 3.0 %copy.51 = bf16[16,8,16,512]{3,1,2,0:T(8,128)(2,1)S(1)} copy(bf16[16,8,16,512]{3,2,1,0:T(8,128)(2,1)} %bitcast.86) | data formatting | bytes 4194304
  46.5 2.2 %copy.52 = bf16[16,8,16,512]{3,2,1,0:T(8,128)(2,1)} copy(bf16[16,8,16,512]{3,1,2,0:T(8,128)(2,1)S(1)} %bitcast.82) | data formatting | bytes 4194304
  48.7 25.0 %all-gather.4.cloned.1.call-done = bf16[512,2048]{1,0:T(8,128)(2,1)} async-done(((bf16[64,2048]{1,0:T(8,128)(2,1)}), bf16[512,2048]{1,0:T(8,128)(2,1)}) %all-gather.4.cloned.1.call-update) | async-done | bytes 2097168 | tf_op jit(solution)/shard_map/all_gather | solution.py:30
  73.7 5.2 %all-to-all-done.1 = bf16[128,8,768]{0,2,1:T(8,128)(2,1)} async-done(((bf16[128,8,768]{0,2,1:T(8,128)(2,1)}), bf16[128,8,768]{0,2,1:T(8,128)(2,1)}, u32[]{:S(2)}, u32[]{:S(2)}) %all-to-all-start.1) | async-done | bytes 1572896 | tf_op jit(solution)/shard_map/all_to_all | solution.py:33
  78.9 13.5 %all-to-all-start = ((bf16[64,2,16,512]{3,2,1,0:T(8,128)(2,1)}), bf16[64,2,16,512]{3,2,1,0:T(8,128)(2,1)S(1)}, u32[]{:S(2)}, u32[]{:S(2)}) async-start(bf16[64,2,16,512]{3,2,1,0:T(8,128)(2,1)} %bitcast.83), calls=%async_computation | async-start | bytes 4194304 | tf_op jit(solution)/shard_map/all_to_all | solution.py:53
  93.2 3.6 %copy.39 = bf16[8,128,1,768]{1,0,3,2:T(8,128)(2,1)} copy(bf16[8,128,1,768]{1,3,0,2:T(8,128)(2,1)} %bitcast.3) | data formatting | bytes 3145728 | tf_op jit(solution)/shard_map/all_to_all | solution.py:33
  96.8 3.7 %reshape.80 = bf16[1024,2,3,128]{0,3,2,1:T(8,128)(2,1)} reshape(bf16[8,128,1,768]{1,0,3,2:T(8,128)(2,1)} %copy.39) | data formatting | bytes 3145728 | tf_op jit(solution)/shard_map/reshape | solution.py:35
  100.5 2.5 %slice_bitcast_fusion = (bf16[1024,2,128]{0,2,1:T(8,128)(2,1)}, bf16[1024,2,1,128]{0,3,2,1:T(8,128)(2,1)}, bf16[1024,2,1,128]{0,3,2,1:T(8,128)(2,1)S(1)}) fusion(bf16[1024,2,3,128]{0,3,2,1:T(8,128)(2,1)} %reshape.80), kind=kLoop, calls=%fused_computation.41 | loop fusion | bytes 3145728 | tf_op jit(solution)/shard_map/squeeze | solution.py:62
  103.3 1.3 copy.42
  104.6 35.8 %all-to-all-done = bf16[64,2,16,512]{3,2,1,0:T(8,128)(2,1)S(1)} async-done(((bf16[64,2,16,512]{3,2,1,0:T(8,128)(2,1)}), bf16[64,2,16,512]{3,2,1,0:T(8,128)(2,1)S(1)}, u32[]{:S(2)}, u32[]{:S(2)}) %all-to-all-start) | async-done | bytes 2097184 | tf_op jit(solution)/shard_map/all_to_all | solution.py:53
  140.4 2.4 %not_reduce_fusion = pred[64,2]{1,0:T(8,128)(4,1)S(1)} fusion(bf16[64,2,16,512]{3,2,1,0:T(8,128)(2,1)S(1)} %all-to-all-done), kind=kLoop, calls=%fused_computation.42 | loop fusion | flops 384 | bytes 384 | tf_op jit(solution)/shard_map/not | solution.py:54
  143.1 2.6 %reshape.81 = bf16[2048,2,2,128]{3,2,1,0:T(2,128)(2,1)S(1)} reshape(bf16[64,2,16,512]{3,2,1,0:T(8,128)(2,1)} %copy-done.1) | data formatting | bytes 4194304 | tf_op jit(solution)/shard_map/reshape | solution.py:56
  145.7 3.9 %fusion.43 = (bf16[2048,2,1,128]{3,2,1,0:T(2,128)(2,1)S(1)}, bf16[2048,2,1,128]{3,2,1,0:T(2,128)(2,1)}) fusion(bf16[2048,2,2,128]{3,2,1,0:T(2,128)(2,1)S(1)} %reshape.81), kind=kLoop, calls=%fused_computation.54 | loop fusion | bytes 4194304 | tf_op jit(solution)/shard_map/slice | solution.py:58
  150.2 1.3 copy.45
  151.6 1.8 copy.55
  153.4 27.4 %while.11 = (s32[]{:T(128)}, bf16[2,512,256]{2,1,0:T(8,128)(2,1)S(1)}, bf16[2,512,2,128]{3,1,0,2:T(8,128)(2,1)S(1)}, bf16[2048,2,128]{2,0,1:T(8,128)(2,1)S(1)}, ...) while((s32[]{:T(128)}, ...), condition=%wide.region_10.11_spmd.clone, body=%wide.region_5.10_spmd.clone.sunk | while | flops 1646131712 | bytes 69022040 | solution.py:100
  155.0 2.9 %fusion.69 = (f32[2,512]{1,0:T(2,128)S(1)}, f32[2,512,1024]{2,1,0:T(8,128)}) fusion(pred[512,1024]{1,0:T(8,128)(4,1)S(1)} %iota_compare_fusion.5, bf16[1024,2,128]{2,0,1:T(8,128)(2,1)S(1)} %get-tuple-element.236, bf16[2,512,2,128]{3,1,0,2:T(8,128)(2,1)S(1)} %get-tuple-element.233, s32[]{:T(128)} %get-tuple-element.221), kind=kOutput, calls=%fused_computation.10.clone.1 | convolution fusion | flops 271580160 | bytes 5509124 | tf_op jit(solution)/shard_map/while/body/eval_jaxpr/qhd,khd->hqk/dot_general | solution.py:75
  158.1 1.4 fusion.70
  161.5 1.9 fusion.72
  163.4 1.3 fusion.71
  164.7 2.2 %fusion.74 = bf16[512,2,128]{0,2,1:T(8,128)(2,1)S(1)} fusion(f32[2,512,128]{1,2,0:T(8,128)S(1)} %fusion.71, bf16[2048,2,128]{0,2,1:T(8,128)(2,1)S(1)} %copy-done.2, f32[2,512,2048]{2,1,0:T(8,128)S(1)} %get-tuple-element.210, f32[2,512]{1,0:T(2,128)S(1)} %max.9, pred[2048]{0:T(1024)(128)(4,1)S(1)} %broadcast_in_dim.164, ...), kind=kOutput, calls=%fused_computation.19.clone.1 | convolution fusion | flops 545652736 | bytes 10233856 | tf_op jit(solution)/shard_map/while/body/eval_jaxpr/hqk,khd->qhd/dot_general | solution.py:84
  168.7 2.9 %fusion.69 = (f32[2,512]{1,0:T(2,128)S(1)}, f32[2,512,1024]{2,1,0:T(8,128)}) fusion(pred[512,1024]{1,0:T(8,128)(4,1)S(1)} %iota_compare_fusion.5, bf16[1024,2,128]{2,0,1:T(8,128)(2,1)S(1)} %get-tuple-element.236, bf16[2,512,2,128]{3,1,0,2:T(8,128)(2,1)S(1)} %get-tuple-element.233, s32[]{:T(128)} %get-tuple-element.221), kind=kOutput, calls=%fused_computation.10.clone.1 | convolution fusion | flops 271580160 | bytes 5509124 | tf_op jit(solution)/shard_map/while/body/eval_jaxpr/qhd,khd->hqk/dot_general | solution.py:75
  171.8 1.4 fusion.70
  175.2 1.9 fusion.72
  178.4 2.2 %fusion.74 = bf16[512,2,128]{0,2,1:T(8,128)(2,1)S(1)} fusion(f32[2,512,128]{1,2,0:T(8,128)S(1)} %fusion.71, bf16[2048,2,128]{0,2,1:T(8,128)(2,1)S(1)} %copy-done.2, f32[2,512,2048]{2,1,0:T(8,128)S(1)} %get-tuple-element.210, f32[2,512]{1,0:T(2,128)S(1)} %max.9, pred[2048]{0:T(1024)(128)(4,1)S(1)} %broadcast_in_dim.164, ...), kind=kOutput, calls=%fused_computation.19.clone.1 | convolution fusion | flops 545652736 | bytes 10233856 | tf_op jit(solution)/shard_map/while/body/eval_jaxpr/hqk,khd->qhd/dot_general | solution.py:84
  180.8 22.0 %all_to_all.39 = bf16[8,128,256]{2,1,0:T(8,128)(2,1)S(1)} all-to-all(bf16[8,128,256]{2,1,0:T(8,128)(2,1)S(1)} %bitcast.88), channel_id=1, replica_groups=mesh['x'=4,'z'=8,'y_lo'=2,'y_hi'=4,'core'=2] {'y_hi','core'}, dimensions={0} | all-to-all | bytes 1048576 | tf_op jit(solution)/shard_map/all_to_all | solution.py:101
  203.1 5.5 %fusion.39 = bf16[1,128,2048]{2,1,0:T(8,128)(2,1)} fusion(bf16[128,2048]{0,1:T(8,128)(2,1)S(1)} %bitcast.85, bf16[2048,2048]{1,0:T(8,128)(2,1)} %all-gather.6.cloned.1.call-done), kind=kOutput, calls=%fused_computation.38 | convolution fusion | flops 1074003968 | bytes 9437184 | tf_op jit(solution)/shard_map/dot_general | solution.py:102
  (62 shorter events, 12.9 us)
Async XLA Ops:
  6.5 67.2 %all-gather.4.cloned.1.call-start = ((), (), s32[]{:S(2)}) async-start(), calls=%async_computation.3 | async-start | bytes 2359296 | tf_op jit(solution)/shard_map/all_gather | solution.py:30
  33.2 11.8 %copy-start.5 = (s32[128]{0:T(128)S(1)}, s32[128]{0:T(128)}, u32[]{:S(2)}) copy-start(s32[128]{0:T(128)} %param.9) | copy-start | bytes 1540
  33.2 12.1 %copy-start.6 = (s32[64]{0:T(128)S(1)}, s32[64]{0:T(128)}, u32[]{:S(2)}) copy-start(s32[64]{0:T(128)} %param.10) | copy-start | bytes 772
  33.2 45.7 %all-to-all-start.1 = ((bf16[128,8,768]{0,2,1:T(8,128)(2,1)}), bf16[128,8,768]{0,2,1:T(8,128)(2,1)}, u32[]{:S(2)}, u32[]{:S(2)}) async-start(bf16[128,8,768]{0,2,1:T(8,128)(2,1)} %bitcast.1), calls=%async_computation.1 | async-start | bytes 3145728 | tf_op jit(solution)/shard_map/all_to_all | solution.py:33
  78.9 61.5 %all-to-all-start = ((bf16[64,2,16,512]{3,2,1,0:T(8,128)(2,1)}), bf16[64,2,16,512]{3,2,1,0:T(8,128)(2,1)S(1)}, u32[]{:S(2)}, u32[]{:S(2)}) async-start(bf16[64,2,16,512]{3,2,1,0:T(8,128)(2,1)} %bitcast.83), calls=%async_computation | async-start | bytes 4194304 | tf_op jit(solution)/shard_map/all_to_all | solution.py:53
  92.4 110.7 %all-gather.6.cloned.1.call-start = ((), (), s32[]{:S(2)}) async-start(), calls=%async_computation.4 | async-start | bytes 10485760 | tf_op jit(solution)/shard_map/all_gather | solution.py:52
  140.4 2.6 %copy-start.1 = (bf16[64,2,16,512]{3,2,1,0:T(8,128)(2,1)}, bf16[64,2,16,512]{3,2,1,0:T(8,128)(2,1)S(1)}, u32[]{:S(2)}) copy-start(bf16[64,2,16,512]{3,2,1,0:T(8,128)(2,1)S(1)} %all-to-all-done) | copy-start | bytes 6291460
  149.6 3.8 %copy-start.3 = (bf16[2,512,256]{2,1,0:T(8,128)(2,1)S(1)}, bf16[2,512,256]{2,1,0:T(8,128)(2,1)}, u32[]{:S(2)}) copy-start(bf16[2,512,256]{2,1,0:T(8,128)(2,1)} %custom-call) | copy-start | bytes 1572868
  158.1 2.2 %copy-start = (f32[2,512,1024]{2,1,0:T(8,128)S(1)}, f32[2,512,1024]{2,1,0:T(8,128)}, u32[]{:S(2)}) copy-start(f32[2,512,1024]{2,1,0:T(8,128)} %get-tuple-element.207) | copy-start | bytes 12582916 | tf_op jit(solution)/shard_map/while
  161.5 1.9 copy-start.4
  163.4 1.4 copy-start.2
  171.8 2.2 %copy-start = (f32[2,512,1024]{2,1,0:T(8,128)S(1)}, f32[2,512,1024]{2,1,0:T(8,128)}, u32[]{:S(2)}) copy-start(f32[2,512,1024]{2,1,0:T(8,128)} %get-tuple-element.207) | copy-start | bytes 12582916 | tf_op jit(solution)/shard_map/while
  175.2 1.9 copy-start.4
  177.1 1.4 copy-start.2
Sparse Core Ops, SparseCore 0:
  30.7 42.9 all-gather.3
  95.3 99.6 all-gather.5

commit v6 on v5

v6 whole, which is shorter than its diff:
```python
import functools
import math

import jax
import jax.numpy as jnp
from jax import lax
from jax.experimental import pallas as pl
from jax.experimental.pallas import tpu as pltpu
from jax.sharding import Mesh, PartitionSpec as P

HD = 128
PAGE = 16
MOST = 2

PHYSICAL_SPLIT = {"dp": (("x", 4), ("z", 8), ("y_lo", 2)), "fsdp": (("y_hi", 4), ("core", 2))}
DP = tuple(name for name, _ in PHYSICAL_SPLIT["dp"])
FSDP = tuple(name for name, _ in PHYSICAL_SPLIT["fsdp"])


def attention_kernel(q_ref, kc_ref, vc_ref, kn_ref, vn_ref, live_row_ref, live_col_ref, out_ref, *, scale):
    rows = q_ref.shape[0]
    first = pl.program_id(1) * rows
    contract = (((1,), (1,)), ((), ()))
    q = q_ref[...]
    cache_scores = lax.dot_general(q, kc_ref[...], contract, preferred_element_type=jnp.float32) * scale
    cache_scores = jnp.where(live_row_ref[...] > 0, cache_scores, -jnp.inf)
    group_scores = lax.dot_general(q, kn_ref[...], contract, preferred_element_type=jnp.float32) * scale
    row = first + lax.broadcasted_iota(jnp.int32, group_scores.shape, 0)
    col = lax.broadcasted_iota(jnp.int32, group_scores.shape, 1)
    group_scores = jnp.where(col <= row, group_scores, -jnp.inf)
    row_max = jnp.maximum(
        jnp.max(cache_scores, axis=1, keepdims=True), jnp.max(group_scores, axis=1, keepdims=True)
    )
    cache_expo = jnp.exp(cache_scores - row_max)
    group_expo = jnp.exp(group_scores - row_max)
    row_total = jnp.sum(cache_expo, axis=1, keepdims=True) + jnp.sum(group_expo, axis=1, keepdims=True)
    values = jnp.where(live_col_ref[...] > 0, vc_ref[...], jnp.zeros((), vc_ref.dtype))
    mixture = jnp.dot(cache_expo.astype(jnp.bfloat16), values, preferred_element_type=jnp.float32)
    mixture = mixture + jnp.dot(
        group_expo.astype(jnp.bfloat16), vn_ref[...], preferred_element_type=jnp.float32
    )
    out_ref[...] = (mixture / row_total).astype(out_ref.dtype)


def attention(qkv, cache, live, heads, block_rows):
    group = qkv.shape[0]
    keys = cache.shape[0]
    live = live.astype(jnp.float32)
    flops = 4 * heads * group * (keys + group) * HD
    return pl.pallas_call(
        functools.partial(attention_kernel, scale=1.0 / math.sqrt(HD)),
        grid=(heads, group // block_rows),
        in_specs=[
            pl.BlockSpec((block_rows, HD), lambda h, b: (b, 3 * h)),
            pl.BlockSpec((keys, HD), lambda h, b: (0, 2 * h)),
            pl.BlockSpec((keys, HD), lambda h, b: (0, 2 * h + 1)),
            pl.BlockSpec((group, HD), lambda h, b: (0, 3 * h + 1)),
            pl.BlockSpec((group, HD), lambda h, b: (0, 3 * h + 2)),
            pl.BlockSpec((1, keys), lambda h, b: (0, 0)),
            pl.BlockSpec((keys, 1), lambda h, b: (0, 0)),
        ],
        out_specs=pl.BlockSpec((block_rows, HD), lambda h, b: (b, h)),
        out_shape=jax.ShapeDtypeStruct((group, heads * HD), qkv.dtype),
        cost_estimate=pl.CostEstimate(
            flops=flops,
            transcendentals=heads * group * (keys + group),
            bytes_accessed=2 * (qkv.size + cache.size + group * heads * HD),
        ),
    )(qkv, cache, cache, qkv, qkv, live.reshape(1, keys), live.reshape(keys, 1))


def per_device(group_qkv, cache_pool, page_request, request_host, out_weight, *, fsdp_count, dp_count):
    requests = request_host.shape[0]
    slot_count = page_request.shape[0]
    tokens_here = group_qkv.shape[1]
    features = cache_pool.shape[2]
    heads_here = features // (2 * HD)
    score_scale = 1.0 / math.sqrt(HD)
    width = out_weight.shape[1]

    weight = out_weight
    for name in reversed(DP[2:] + FSDP):
        weight = lax.all_gather(weight, name, axis=0, tiled=True)
    weight, group_qkv = lax.optimization_barrier((weight, group_qkv))
    weight = lax.all_gather(weight, DP[1], axis=0, tiled=True)

    local_qkv = group_qkv.reshape(tokens_here, fsdp_count, heads_here * 3 * HD)
    gathered_qkv = lax.all_to_all(local_qkv, FSDP, split_axis=1, concat_axis=0, tiled=True)
    group_len = tokens_here * fsdp_count
    gathered_qkv = gathered_qkv.reshape(group_len, heads_here * 3 * HD)

    request_ids = jnp.arange(requests, dtype=jnp.int32)
    member = (page_request[:, None] == request_ids[None, :]).astype(jnp.int32)
    slot_rank = jnp.sum(member * (jnp.cumsum(member, axis=0) - 1), axis=1)
    target_host = jnp.sum(member * request_host[None, :], axis=1)
    is_live = jnp.sum(member, axis=1)
    target_slot = jnp.where(is_live > 0, target_host * MOST + slot_rank, -1)
    chosen = target_slot[:, None] == jnp.arange(requests * MOST, dtype=jnp.int32)[None, :]
    flat_pool = cache_pool.reshape(slot_count, PAGE * features)
    packed = jnp.einsum(
        "sp,sf->pf", chosen.astype(jnp.bfloat16), flat_pool, preferred_element_type=jnp.float32
    )
    occupied = jnp.sum(chosen.astype(jnp.int32), axis=0) > 0
    packed = jnp.where(occupied[:, None], packed, jnp.nan)
    packed = packed.astype(jnp.bfloat16).reshape(requests, MOST, PAGE, features)
    weight, packed, gathered_qkv = lax.optimization_barrier((weight, packed, gathered_qkv))
    weight = lax.all_gather(weight, DP[0], axis=0, tiled=True)
    arrived = lax.all_to_all(packed, DP, split_axis=0, concat_axis=0, tiled=True)
    present = jnp.logical_not(jnp.isnan(arrived[:, :, 0, 0]))
    live_tokens = jnp.repeat(present.reshape(requests * MOST), PAGE)
    cached = arrived.reshape(requests * MOST * PAGE, features)
    attn_heads = attention(gathered_qkv, cached, live_tokens, heads_here, min(256, group_len))
    tokens_attn = lax.all_to_all(attn_heads, FSDP, split_axis=0, concat_axis=1, tiled=True)
    summed = jnp.dot(tokens_attn, weight, preferred_element_type=jnp.float32)
    return summed.astype(jnp.bfloat16).reshape(1, tokens_here, width)


def solution(mesh):
    split = [part for axis in mesh.axis_names for part in PHYSICAL_SPLIT[axis]]
    fine = Mesh(mesh.devices.reshape([size for _, size in split]), DP + FSDP)
    return jax.shard_map(
        lambda *args: per_device(
            *args, fsdp_count=mesh.shape["fsdp"], dp_count=mesh.shape["dp"]
        ),
        mesh=fine,
        in_specs=(
            P(DP, FSDP, None),
            P(DP, None, FSDP),
            P(DP),
            P(),
            P(DP + FSDP, None),
        ),
        out_specs=P(DP, FSDP, None),
        check_vma=False,
    )
```

time: 216 us -> 202 us (0.935)
  blocking collectives: 46 us -> 107 us
  waiting for transfers between devices: 66.8 us -> 35.5 us
  local copies, waits for them, and re-layouts: 32.8 us -> 12.1 us
  Pallas kernels: 0 us -> 16.9 us
  matrix products: 21.8 us -> 6.28 us
  starting transfers between devices: 22.4 us -> 8.75 us
  other arithmetic: 11.8 us -> 0.95 us
    all_to_all x0 -> x1, blocking collectives: none -> 61.3 us  [per_device(): lax.all_to_all(packed, DP, split_axis=0, concat_axis=0, tiled=True)]
    all_to_all x1 -> x0, waiting for transfers between devices: 35.8 us -> none  [per_device(): lax.all_to_all(packed, DP, split_axis=0, concat_axis=0, tiled=True)]
    all_to_all x1, waiting for transfers between devices: 5.23 us -> 31.6 us  [per_device(): lax.all_to_all(local_qkv, FSDP, split_axis=1, concat_axis=0, tiled=True)]
    all_gather x1, waiting for transfers between devices: 25 us -> 0.01 us  [per_device(): weight = lax.all_gather(weight, DP[1], axis=0, tiled=True)]
    pallas_call x0 -> x1, Pallas kernels: none -> 16.9 us  [attention(): pl.pallas_call(functools.partial(attention_kernel, scale=1.0 / math.sqrt(...]
    dot_general x8 -> x0, matrix products: 15.6 us -> none  [the longest x2 5.79 us: attend(): jnp.einsum('qhd,khd->hqk', query_block, new_keys, preferred_element_type=...]
    all_to_all x1 -> x0, starting transfers between devices: 13.5 us -> none  [per_device(): lax.all_to_all(packed, DP, split_axis=0, concat_axis=0, tiled=True)]
    slice x4 -> x0, local copies, waits for them, and re-layouts: 7.27 us -> none  [the longest x1 3.88 us: per_device(): cached[:, :, 1]]
  transfers between devices with their start and end apart: 4 -> 3, of which waited for: 3 -> 2; matrix products, arithmetic and copies ran while one was open for 28% -> 6% of each run, Pallas kernels for 0% -> 8%
where the time goes in v6:
time: 202 us; the launch traced here: 201 us
  blocking collectives  107 us (53%)
  waiting for transfers between devices  35.5 us (18%)
  Pallas kernels  16.9 us (8%)
  between operations  13.5 us (7%)
  local copies, waits for them, and re-layouts  12.1 us (6%)
  starting transfers between devices  8.75 us (4%)
  matrix products  6.28 us (3%)
    all_to_all x1, blocking collectives, per_device(): lax.all_to_all(packed, DP, split_axis=0, concat_axis=0, tiled=True)  61.3 us
    all_to_all x1, waiting for transfers between devices, per_device(): lax.all_to_all(local_qkv, FSDP, split_axis=1, concat_axis=0, tiled=True)  31.6 us
    all_gather x3, blocking collectives, per_device(): weight = lax.all_gather(weight, name, axis=0, tiled=True)  24 us
    all_to_all x1, blocking collectives, per_device(): lax.all_to_all(attn_heads, FSDP, split_axis=0, concat_axis=1, tiled=True)  22 us
    pallas_call x1, Pallas kernels, attention(): pl.pallas_call(functools.partial(attention_kernel, scale=1.0 / math.sqrt(...  16.9 us
    all_to_all x1, starting transfers between devices, per_device(): lax.all_to_all(local_qkv, FSDP, split_axis=1, concat_axis=0, tiled=True)  8.74 us
    unnamed x10, local copies, waits for them, and re-layouts  6.89 us
    dot_general x1, matrix products, per_device(): summed = jnp.dot(tokens_attn, weight, preferred_element_type=jnp.float32)  5.46 us
  transfers between devices with their start and end apart: 3, of which 2 were waited for; matrix products, arithmetic and copies ran while one was open for 6% of the time, Pallas kernels for 8%

profile of v6, /device:TPU:1, one launch (start us, length us, event | category | flops | bytes accessed | tf_op | source)
XLA Modules:
  0.0 201.2 jit_solution(9453625913614399917)
XLA Ops:
  6.5 0.0 all-gather.4.cloned.1.call-start
  6.5 8.5 %all-gather = bf16[2,4,2048]{2,1,0:T(4,128)(2,1)S(1)} all-gather(bf16[1,4,2048]{2,1,0:T(4,128)(2,1)} %bitcast.34), channel_id=1, replica_groups=mesh['x'=4,'z'=8,'y_lo'=2,'y_hi'=4,'core'=2] {'core'}, dimensions={0}, use_global_device_ids=true | all-gather | bytes 49152 | tf_op jit(solution)/shard_map/all_gather | solution.py:83
  15.1 10.9 %all_gather.16 = bf16[32,2048]{1,0:T(8,128)(2,1)S(1)} all-gather(bf16[8,2048]{1,0:T(8,128)(2,1)S(1)} %reshape.78), channel_id=1, replica_groups=mesh['x'=4,'z'=8,'y_lo'=2,'y_hi'=4,'core'=2] {'y_hi'}, dimensions={0}, use_global_device_ids=true | all-gather | bytes 163840 | tf_op jit(solution)/shard_map/all_gather | solution.py:83
  26.0 4.6 %all_gather.17 = bf16[64,2048]{1,0:T(8,128)(2,1)} all-gather(bf16[32,2048]{1,0:T(8,128)(2,1)S(1)} %all_gather.16), channel_id=1, replica_groups=mesh['x'=4,'z'=8,'y_lo'=2,'y_hi'=4,'core'=2] {'y_lo'}, dimensions={0}, use_global_device_ids=true | all-gather | bytes 393216 | tf_op jit(solution)/shard_map/all_gather | solution.py:83
  30.6 0.0 all-gather.4.cloned.1.call-update
  30.6 1.7 copy.22
  32.3 1.4 copy.17
  33.8 8.7 %all-to-all-start = ((bf16[128,8,768]{2,0,1:T(8,128)(2,1)}), bf16[128,8,768]{2,0,1:T(8,128)(2,1)}, u32[]{:S(2)}, u32[]{:S(2)}) async-start(bf16[128,8,768]{2,0,1:T(8,128)(2,1)} %copy.17), calls=%async_computation | async-start | bytes 3145728 | tf_op jit(solution)/shard_map/all_to_all | solution.py:88
  42.5 0.0 all-gather.6.cloned.1.call-start
  42.5 3.0 %copy.20 = bf16[16,8,16,512]{3,1,2,0:T(8,128)(2,1)S(1)} copy(bf16[16,8,16,512]{3,2,1,0:T(8,128)(2,1)} %bitcast.31) | data formatting | bytes 4194304
  45.5 0.0 copy-done.1
  45.5 0.1 fusion.2
  45.6 0.2 reduce_window_sum.11
  45.8 0.0 copy-done.2
  45.8 0.2 select_reduce_fusion.1
  46.0 0.1 convert_reduce_fusion
  46.1 0.8 fusion
  47.0 0.8 copy.21
  47.8 31.6 %all-to-all-done = bf16[128,8,768]{2,0,1:T(8,128)(2,1)} async-done(((bf16[128,8,768]{2,0,1:T(8,128)(2,1)}), bf16[128,8,768]{2,0,1:T(8,128)(2,1)}, u32[]{:S(2)}, u32[]{:S(2)}) %all-to-all-start) | async-done | bytes 1572896 | tf_op jit(solution)/shard_map/all_to_all | solution.py:88
  79.4 0.0 all-gather.6.cloned.1.call-update
  79.4 61.3 %all_to_all.39 = bf16[64,2,16,512]{3,2,1,0:T(8,128)(2,1)S(1)} all-to-all(bf16[64,2,16,512]{3,2,1,0:T(8,128)(2,1)S(1)} %bitcast.26), channel_id=1, replica_groups=mesh['x'=4,'z'=8,'y_lo'=2,'y_hi'=4,'core'=2] {'x','z','y_lo'}, dimensions={0} | all-to-all | bytes 4194304 | tf_op jit(solution)/shard_map/all_to_all | solution.py:108
  140.7 1.3 copy-done
  142.0 0.4 fusion.3
  142.3 0.1 reshape.76
  142.5 0.1 broadcast_in_dim.28
  142.5 1.6 convert_element_type.51.live_col_ref
  144.1 0.7 convert_element_type.47.live_row_ref
  144.8 16.9 %shard_map.55 = bf16[1024,256]{1,0:T(8,128)(2,1)} custom-call(bf16[1024,768]{1,0:T(8,128)(2,1)} %bitcast.3.q_ref.kn_ref.vn_ref, bf16[2048,512]{1,0:T(8,128)(2,1)} %bitcast.29, bf16[2048,512]{1,0:T(8,128)(2,1)} %bitcast.30, bf16[1024,768]{1,0:T(8,128)(2,1)} %bitcast.3.q_ref.kn_ref.vn_ref, bf16[1024,768]{1,0:T(8,128)(2,1)} %bitcast.3.q_ref.kn_ref.vn_ref, ...), custom_call_target="tpu_custom_call" | custom-call | flops 3221225472 | bytes 4194304 | tf_op jit(solution)/shard_map/pallas_call | solution.py:50
  161.7 1.3 copy.19
  163.0 22.0 %all_to_all.40 = bf16[8,128,256]{1,2,0:T(8,128)(2,1)S(1)} all-to-all(bf16[8,128,256]{1,2,0:T(8,128)(2,1)S(1)} %copy.19), channel_id=1, replica_groups=mesh['x'=4,'z'=8,'y_lo'=2,'y_hi'=4,'core'=2] {'y_hi','core'}, dimensions={0} | all-to-all | bytes 1048576 | tf_op jit(solution)/shard_map/all_to_all | solution.py:113
  185.0 3.9 %all-gather.6.cloned.1.call-done = bf16[2048,2048]{1,0:T(8,128)(2,1)} async-done(((bf16[512,2048]{1,0:T(8,128)(2,1)}), bf16[2048,2048]{1,0:T(8,128)(2,1)}) %all-gather.6.cloned.1.call-update) | async-done | bytes 8388624 | tf_op jit(solution)/shard_map/all_gather | solution.py:107
  188.9 5.5 %fusion.1 = bf16[1,128,2048]{2,1,0:T(8,128)(2,1)} fusion(bf16[128,2048]{0,1:T(8,128)(2,1)S(1)} %bitcast.28, bf16[2048,2048]{1,0:T(8,128)(2,1)} %all-gather.6.cloned.1.call-done), kind=kOutput, calls=%fused_computation.3 | convolution fusion | flops 1074003968 | bytes 9437184 | tf_op jit(solution)/shard_map/dot_general | solution.py:114
  (7 shorter events, 0.0 us)
Async XLA Ops:
  6.5 72.9 %all-gather.4.cloned.1.call-start = ((), (), s32[]{:S(2)}) async-start(), calls=%async_computation.3 | async-start | bytes 2359296 | tf_op jit(solution)/shard_map/all_gather | solution.py:85
  33.8 45.6 %all-to-all-start = ((bf16[128,8,768]{2,0,1:T(8,128)(2,1)}), bf16[128,8,768]{2,0,1:T(8,128)(2,1)}, u32[]{:S(2)}, u32[]{:S(2)}) async-start(bf16[128,8,768]{2,0,1:T(8,128)(2,1)} %copy.17), calls=%async_computation | async-start | bytes 3145728 | tf_op jit(solution)/shard_map/all_to_all | solution.py:88
  42.5 146.4 %all-gather.6.cloned.1.call-start = ((), (), s32[]{:S(2)}) async-start(), calls=%async_computation.4 | async-start | bytes 10485760 | tf_op jit(solution)/shard_map/all_gather | solution.py:107
  42.5 3.0 %copy-start.1 = (s32[128]{0:T(128)S(1)}, s32[128]{0:T(128)}, u32[]{:S(2)}) copy-start(s32[128]{0:T(128)} %param.7) | copy-start | bytes 1540
  42.5 3.3 %copy-start.2 = (s32[64]{0:T(128)S(1)}, s32[64]{0:T(128)}, u32[]{:S(2)}) copy-start(s32[64]{0:T(128)} %param.8) | copy-start | bytes 772
  140.7 1.3 copy-start
Sparse Core Ops, SparseCore 0:
  30.7 43.5 all-gather.3
  79.5 109.2 all-gather.5

commit v7 on v6

--- a/solution.py
+++ b/solution.py
@@ -79,7 +79,7 @@
     width = out_weight.shape[1]
 
     weight = out_weight
-    for name in reversed(DP[2:] + FSDP):
+    for name in reversed(DP[2:] + FSDP[:-1]):
         weight = lax.all_gather(weight, name, axis=0, tiled=True)
     weight, group_qkv = lax.optimization_barrier((weight, group_qkv))
     weight = lax.all_gather(weight, DP[1], axis=0, tiled=True)
@@ -106,11 +106,17 @@
     weight, packed, gathered_qkv = lax.optimization_barrier((weight, packed, gathered_qkv))
     weight = lax.all_gather(weight, DP[0], axis=0, tiled=True)
     arrived = lax.all_to_all(packed, DP, split_axis=0, concat_axis=0, tiled=True)
+    weight, arrived = lax.optimization_barrier((weight, arrived))
+    weight = lax.all_gather(weight, FSDP[-1], axis=0, tiled=True)
     present = jnp.logical_not(jnp.isnan(arrived[:, :, 0, 0]))
     live_tokens = jnp.repeat(present.reshape(requests * MOST), PAGE)
     cached = arrived.reshape(requests * MOST * PAGE, features)
     attn_heads = attention(gathered_qkv, cached, live_tokens, heads_here, min(256, group_len))
     tokens_attn = lax.all_to_all(attn_heads, FSDP, split_axis=0, concat_axis=1, tiled=True)
+    cores = lax.axis_size(FSDP[-1])
+    rows_here = out_weight.shape[0]
+    tokens_attn = tokens_attn.reshape(tokens_here, width // (cores * rows_here), cores, rows_here)
+    tokens_attn = jnp.transpose(tokens_attn, (0, 2, 1, 3)).reshape(tokens_here, width)
     summed = jnp.dot(tokens_attn, weight, preferred_element_type=jnp.float32)
     return summed.astype(jnp.bfloat16).reshape(1, tokens_here, width)
 

time: 202 us -> 214 us (1.059)
  waiting for transfers between devices: 35.5 us -> 55.8 us
  blocking collectives: 107 us -> 96.8 us
  starting transfers between devices: 8.75 us -> 11.8 us
    all_gather x1, waiting for transfers between devices: 0.01 us -> 36 us  [per_device(): weight = lax.all_gather(weight, DP[1], axis=0, tiled=True)]
    all_to_all x1, waiting for transfers between devices: 31.6 us -> 0.01 us  [per_device(): lax.all_to_all(local_qkv, FSDP, split_axis=1, concat_axis=0, tiled=True)]
    all_gather x1, waiting for transfers between devices: 3.86 us -> 19 us  [per_device(): weight = lax.all_gather(weight, DP[0], axis=0, tiled=True)]
    all_gather x3 -> x2, blocking collectives: 24 us -> 18.2 us  [per_device(): weight = lax.all_gather(weight, name, axis=0, tiled=True)]
    all_to_all x1, blocking collectives: 61.3 us -> 56.2 us  [per_device(): lax.all_to_all(packed, DP, split_axis=0, concat_axis=0, tiled=True)]
    all_to_all x1, starting transfers between devices: 8.74 us -> 11.7 us  [per_device(): lax.all_to_all(local_qkv, FSDP, split_axis=1, concat_axis=0, tiled=True)]
    unnamed x10 -> x8, local copies, waits for them, and re-layouts: 6.89 us -> 5.59 us
  transfers between devices with their start and end apart: 3 -> 4, of which waited for: 2 -> 2; matrix products, arithmetic and copies ran while one was open for 6% -> 5% of each run, Pallas kernels for 8% -> 8%
where the time goes in v7:
time: 214 us
  blocking collectives  96.8 us (45%)
  waiting for transfers between devices  55.8 us (26%)
  Pallas kernels  16.8 us (8%)
  between operations  13.2 us (6%)
  starting transfers between devices  11.8 us (6%)
  local copies, waits for them, and re-layouts  11.1 us (5%)
  matrix products  6.28 us (3%)
    all_to_all x1, blocking collectives, per_device(): lax.all_to_all(packed, DP, split_axis=0, concat_axis=0, tiled=True)  56.2 us
    all_gather x1, waiting for transfers between devices, per_device(): weight = lax.all_gather(weight, DP[1], axis=0, tiled=True)  36 us
    all_to_all x1, blocking collectives, per_device(): lax.all_to_all(attn_heads, FSDP, split_axis=0, concat_axis=1, tiled=True)  22.4 us
    all_gather x1, waiting for transfers between devices, per_device(): weight = lax.all_gather(weight, DP[0], axis=0, tiled=True)  19 us
    all_gather x2, blocking collectives, per_device(): weight = lax.all_gather(weight, name, axis=0, tiled=True)  18.2 us
    pallas_call x1, Pallas kernels, attention(): pl.pallas_call(functools.partial(attention_kernel, scale=1.0 / math.sqrt(...  16.8 us
    all_to_all x1, starting transfers between devices, per_device(): lax.all_to_all(local_qkv, FSDP, split_axis=1, concat_axis=0, tiled=True)  11.7 us
    unnamed x8, local copies, waits for them, and re-layouts  5.59 us
  transfers between devices with their start and end apart: 4, of which 2 were waited for; matrix products, arithmetic and copies ran while one was open for 5% of the time, Pallas kernels for 8%

profile of v7, /device:TPU:1, one launch (start us, length us, event | category | flops | bytes accessed | tf_op | source)
XLA Modules:
  0.0 213.6 jit_solution(8209798672501619171)
XLA Ops:
  6.5 14.3 %all-gather = bf16[4,4,2048]{2,1,0:T(4,128)(2,1)S(1)} all-gather(bf16[1,4,2048]{2,1,0:T(4,128)(2,1)} %bitcast.38), channel_id=1, replica_groups=mesh['x'=4,'z'=8,'y_lo'=2,'y_hi'=4,'core'=2] {'y_hi'}, dimensions={0}, use_global_device_ids=true | all-gather | bytes 81920 | tf_op jit(solution)/shard_map/all_gather | solution.py:83
  20.9 3.9 %all_gather.16 = bf16[32,2048]{1,0:T(8,128)(2,1)} all-gather(bf16[16,2048]{1,0:T(8,128)(2,1)S(1)} %reshape.87), channel_id=1, replica_groups=mesh['x'=4,'z'=8,'y_lo'=2,'y_hi'=4,'core'=2] {'y_lo'}, dimensions={0}, use_global_device_ids=true | all-gather | bytes 196608 | tf_op jit(solution)/shard_map/all_gather | solution.py:83
  24.8 1.7 copy.25
  26.5 1.4 copy.19
  28.0 11.7 %all-to-all-start = ((bf16[128,8,768]{2,0,1:T(8,128)(2,1)}), bf16[128,8,768]{2,0,1:T(8,128)(2,1)}, u32[]{:S(2)}, u32[]{:S(2)}) async-start(bf16[128,8,768]{2,0,1:T(8,128)(2,1)} %copy.19), calls=%async_computation | async-start | bytes 3145728 | tf_op jit(solution)/shard_map/all_to_all | solution.py:88
  39.7 0.7 all-gather.5.cloned.1.call-update
  40.4 0.0 all-gather.7.cloned.1.call-start
  40.4 0.0 copy-start
  40.5 3.0 %copy.23 = bf16[16,8,16,512]{3,1,2,0:T(8,128)(2,1)S(1)} copy(bf16[16,8,16,512]{3,2,1,0:T(8,128)(2,1)} %bitcast.34) | data formatting | bytes 4194304
  43.5 0.1 fusion.2
  43.6 0.2 reduce_window_sum.11
  43.7 0.2 select_reduce_fusion.1
  44.0 0.1 convert_reduce_fusion
  44.1 0.8 fusion
  44.9 0.8 copy.24
  45.7 36.0 %all-gather.5.cloned.1.call-done = bf16[256,2048]{1,0:T(8,128)(2,1)} async-done(((bf16[32,2048]{1,0:T(8,128)(2,1)}), bf16[256,2048]{1,0:T(8,128)(2,1)}) %all-gather.5.cloned.1.call-update) | async-done | bytes 1048592 | tf_op jit(solution)/shard_map/all_gather | solution.py:85
  81.8 0.0 all-gather.7.cloned.1.call-update
  81.8 0.0 all-gather.9.cloned.1.call-start
  81.8 56.2 %all_to_all.36 = bf16[64,2,16,512]{3,2,1,0:T(8,128)(2,1)} all-to-all(bf16[64,2,16,512]{3,2,1,0:T(8,128)(2,1)S(1)} %bitcast.29), channel_id=1, replica_groups=mesh['x'=4,'z'=8,'y_lo'=2,'y_hi'=4,'core'=2] {'x','z','y_lo'}, dimensions={0} | all-to-all | bytes 4194304 | tf_op jit(solution)/shard_map/all_to_all | solution.py:108
  138.0 19.0 %all-gather.7.cloned.1.call-done = bf16[1024,2048]{1,0:T(8,128)(2,1)} async-done(((bf16[256,2048]{1,0:T(8,128)(2,1)}), bf16[1024,2048]{1,0:T(8,128)(2,1)}) %all-gather.7.cloned.1.call-update) | async-done | bytes 4194320 | tf_op jit(solution)/shard_map/all_gather | solution.py:107
  157.0 0.0 all-gather.9.cloned.1.call-update
  157.0 1.3 fusion.3
  158.3 0.1 reshape.85
  158.4 0.1 broadcast_in_dim.28
  158.5 1.6 convert_element_type.51.live_col_ref
  160.1 0.7 convert_element_type.47.live_row_ref
  160.8 16.8 %shard_map.55 = bf16[1024,256]{1,0:T(8,128)(2,1)} custom-call(bf16[1024,768]{1,0:T(8,128)(2,1)} %bitcast.3.q_ref.kn_ref.vn_ref, bf16[2048,512]{1,0:T(8,128)(2,1)} %bitcast.32, bf16[2048,512]{1,0:T(8,128)(2,1)} %bitcast.33, bf16[1024,768]{1,0:T(8,128)(2,1)} %bitcast.3.q_ref.kn_ref.vn_ref, bf16[1024,768]{1,0:T(8,128)(2,1)} %bitcast.3.q_ref.kn_ref.vn_ref, ...), custom_call_target="tpu_custom_call" | custom-call | flops 3221225472 | bytes 4194304 | tf_op jit(solution)/shard_map/pallas_call | solution.py:50
  177.6 1.4 copy.21
  179.0 22.4 %all_to_all.37 = bf16[8,128,256]{1,2,0:T(8,128)(2,1)S(1)} all-to-all(bf16[8,128,256]{1,2,0:T(8,128)(2,1)S(1)} %copy.21), channel_id=1, replica_groups=mesh['x'=4,'z'=8,'y_lo'=2,'y_hi'=4,'core'=2] {'y_hi','core'}, dimensions={0} | all-to-all | bytes 1048576 | tf_op jit(solution)/shard_map/all_to_all | solution.py:115
  201.4 0.2 copy.22
  201.6 0.0 all-gather.9.cloned.1.call-done
  201.6 5.5 %fusion.1 = bf16[1,128,2048]{2,1,0:T(8,128)(2,1)} fusion(bf16[128,2048]{0,1:T(8,128)(2,1)S(1)} %bitcast.31, bf16[2048,2048]{1,0:T(8,128)(2,1)} %all-gather.9.cloned.1.call-done), kind=kOutput, calls=%fused_computation.3 | convolution fusion | flops 1074003968 | bytes 9437184 | tf_op jit(solution)/shard_map/dot_general | solution.py:120
  (8 shorter events, 0.0 us)
Async XLA Ops:
  28.0 53.8 %all-to-all-start = ((bf16[128,8,768]{2,0,1:T(8,128)(2,1)}), bf16[128,8,768]{2,0,1:T(8,128)(2,1)}, u32[]{:S(2)}, u32[]{:S(2)}) async-start(bf16[128,8,768]{2,0,1:T(8,128)(2,1)} %copy.19), calls=%async_computation | async-start | bytes 3145728 | tf_op jit(solution)/shard_map/all_to_all | solution.py:88
  39.7 42.1 %all-gather.5.cloned.1.call-start = ((), (), s32[]{:S(2)}) async-start(), calls=%async_computation.3 | async-start | bytes 1179648 | tf_op jit(solution)/shard_map/all_gather | solution.py:85
  40.4 116.6 %all-gather.7.cloned.1.call-start = ((), (), s32[]{:S(2)}) async-start(), calls=%async_computation.4 | async-start | bytes 5242880 | tf_op jit(solution)/shard_map/all_gather | solution.py:107
  40.4 3.0 %copy-start = (s32[128]{0:T(128)S(1)}, s32[128]{0:T(128)}, u32[]{:S(2)}) copy-start(s32[128]{0:T(128)} %param.7) | copy-start | bytes 1540
  40.5 3.3 %copy-start.1 = (s32[64]{0:T(128)S(1)}, s32[64]{0:T(128)}, u32[]{:S(2)}) copy-start(s32[64]{0:T(128)} %param.8) | copy-start | bytes 772
  81.8 119.8 %all-gather.9.cloned.1.call-start = ((), (), s32[]{:S(2)}) async-start(), calls=%async_computation.5 | async-start | bytes 12582912 | tf_op jit(solution)/shard_map/all_gather | solution.py:110
Sparse Core Ops, SparseCore 0:
  42.5 39.1 all-gather.4
  83.9 73.0 all-gather.6
  159.1 27.7 all-gather.8

commit v8 on v6

--- a/solution.py
+++ b/solution.py
@@ -79,7 +79,7 @@
     width = out_weight.shape[1]
 
     weight = out_weight
-    for name in reversed(DP[2:] + FSDP):
+    for name in (FSDP[1], DP[2]):
         weight = lax.all_gather(weight, name, axis=0, tiled=True)
     weight, group_qkv = lax.optimization_barrier((weight, group_qkv))
     weight = lax.all_gather(weight, DP[1], axis=0, tiled=True)
@@ -105,12 +105,16 @@
     packed = packed.astype(jnp.bfloat16).reshape(requests, MOST, PAGE, features)
     weight, packed, gathered_qkv = lax.optimization_barrier((weight, packed, gathered_qkv))
     weight = lax.all_gather(weight, DP[0], axis=0, tiled=True)
+    weight = lax.all_gather(weight, FSDP[0], axis=0, tiled=True)
     arrived = lax.all_to_all(packed, DP, split_axis=0, concat_axis=0, tiled=True)
     present = jnp.logical_not(jnp.isnan(arrived[:, :, 0, 0]))
     live_tokens = jnp.repeat(present.reshape(requests * MOST), PAGE)
     cached = arrived.reshape(requests * MOST * PAGE, features)
     attn_heads = attention(gathered_qkv, cached, live_tokens, heads_here, min(256, group_len))
     tokens_attn = lax.all_to_all(attn_heads, FSDP, split_axis=0, concat_axis=1, tiled=True)
+    split = [size for _, size in PHYSICAL_SPLIT["dp"] + PHYSICAL_SPLIT["fsdp"]]
+    tokens_attn = tokens_attn.reshape(tokens_here, *split, out_weight.shape[0])
+    tokens_attn = jnp.transpose(tokens_attn, (0, 4, 1, 2, 3, 5, 6)).reshape(tokens_here, width)
     summed = jnp.dot(tokens_attn, weight, preferred_element_type=jnp.float32)
     return summed.astype(jnp.bfloat16).reshape(1, tokens_here, width)
 

time: 202 us -> 297 us (1.47)
  blocking collectives: 107 us -> 180 us
  waiting for transfers between devices: 35.5 us -> 59.9 us
  starting transfers between devices: 8.75 us -> 5.73 us
    all_to_all x1, blocking collectives: 22 us -> 60.9 us  [per_device(): lax.all_to_all(attn_heads, FSDP, split_axis=0, concat_axis=1, tiled=True)]
    all_gather x1, waiting for transfers between devices: 3.86 us -> 36.4 us  [per_device(): weight = lax.all_gather(weight, DP[0], axis=0, tiled=True)]
    all_to_all x1, waiting for transfers between devices: 31.6 us -> 4.66 us  [per_device(): lax.all_to_all(local_qkv, FSDP, split_axis=1, concat_axis=0, tiled=True)]
    all_gather x0 -> x1, blocking collectives: none -> 26.9 us  [per_device(): weight = lax.all_gather(weight, DP[1], axis=0, tiled=True)]
    all_gather x1, waiting for transfers between devices: 0.01 us -> 18.8 us  [per_device(): weight = lax.all_gather(weight, FSDP[0], axis=0, tiled=True)]
    all_to_all x1, blocking collectives: 61.3 us -> 80 us  [per_device(): lax.all_to_all(packed, DP, split_axis=0, concat_axis=0, tiled=True)]
    all_gather x3 -> x2, blocking collectives: 24 us -> 11.9 us  [per_device(): weight = lax.all_gather(weight, name, axis=0, tiled=True)]
    all_to_all x1, starting transfers between devices: 8.74 us -> 5.68 us  [per_device(): lax.all_to_all(local_qkv, FSDP, split_axis=1, concat_axis=0, tiled=True)]
  transfers between devices with their start and end apart: 3 -> 3, of which waited for: 2 -> 3; matrix products, arithmetic and copies ran while one was open for 6% -> 3% of each run, Pallas kernels for 8% -> 6%
where the time goes in v8:
time: 297 us; the launch traced here: 295 us
  blocking collectives  180 us (61%)
  waiting for transfers between devices  59.9 us (20%)
  Pallas kernels  16.8 us (6%)
  between operations  13.5 us (5%)
  local copies, waits for them, and re-layouts  12.3 us (4%)
  matrix products  6.28 us (2%)
  starting transfers between devices  5.73 us (2%)
    all_to_all x1, blocking collectives, per_device(): lax.all_to_all(packed, DP, split_axis=0, concat_axis=0, tiled=True)  80 us
    all_to_all x1, blocking collectives, per_device(): lax.all_to_all(attn_heads, FSDP, split_axis=0, concat_axis=1, tiled=True)  60.9 us
    all_gather x1, waiting for transfers between devices, per_device(): weight = lax.all_gather(weight, DP[0], axis=0, tiled=True)  36.4 us
    all_gather x1, blocking collectives, per_device(): weight = lax.all_gather(weight, DP[1], axis=0, tiled=True)  26.9 us
    all_gather x1, waiting for transfers between devices, per_device(): weight = lax.all_gather(weight, FSDP[0], axis=0, tiled=True)  18.8 us
    pallas_call x1, Pallas kernels, attention(): pl.pallas_call(functools.partial(attention_kernel, scale=1.0 / math.sqrt(...  16.8 us
    all_gather x2, blocking collectives, per_device(): weight = lax.all_gather(weight, name, axis=0, tiled=True)  11.9 us
    unnamed x10, local copies, waits for them, and re-layouts  6.89 us
  transfers between devices with their start and end apart: 3, of which 3 were waited for; matrix products, arithmetic and copies ran while one was open for 3% of the time, Pallas kernels for 6%

profile of v8, /device:TPU:1, one launch (start us, length us, event | category | flops | bytes accessed | tf_op | source)
XLA Modules:
  0.0 295.3 jit_solution(17000156467171553083)
XLA Ops:
  6.5 8.5 %all-gather = bf16[2,4,2048]{2,1,0:T(4,128)(2,1)S(1)} all-gather(bf16[1,4,2048]{2,1,0:T(4,128)(2,1)} %bitcast.38), channel_id=1, replica_groups=mesh['x'=4,'z'=8,'y_lo'=2,'y_hi'=4,'core'=2] {'core'}, dimensions={0}, use_global_device_ids=true | all-gather | bytes 49152 | tf_op jit(solution)/shard_map/all_gather | solution.py:83
  15.1 3.4 %all_gather.16 = bf16[16,2048]{1,0:T(8,128)(2,1)S(1)} all-gather(bf16[8,2048]{1,0:T(8,128)(2,1)S(1)} %reshape.87), channel_id=1, replica_groups=mesh['x'=4,'z'=8,'y_lo'=2,'y_hi'=4,'core'=2] {'y_lo'}, dimensions={0}, use_global_device_ids=true | all-gather | bytes 98304 | tf_op jit(solution)/shard_map/all_gather | solution.py:83
  18.5 1.7 copy.25
  20.3 1.4 copy.19
  21.7 5.7 %all-to-all-start = ((bf16[128,8,768]{2,0,1:T(8,128)(2,1)}), bf16[128,8,768]{2,0,1:T(8,128)(2,1)}, u32[]{:S(2)}, u32[]{:S(2)}) async-start(bf16[128,8,768]{2,0,1:T(8,128)(2,1)} %copy.19), calls=%async_computation | async-start | bytes 3145728 | tf_op jit(solution)/shard_map/all_to_all | solution.py:88
  27.4 3.0 %copy.23 = bf16[16,8,16,512]{3,1,2,0:T(8,128)(2,1)S(1)} copy(bf16[16,8,16,512]{3,2,1,0:T(8,128)(2,1)} %bitcast.34) | data formatting | bytes 4194304
  30.4 0.0 copy-done.1
  30.4 0.1 fusion.2
  30.5 0.2 reduce_window_sum.11
  30.7 0.2 select_reduce_fusion.1
  30.9 0.1 convert_reduce_fusion
  31.0 0.8 fusion
  31.8 0.8 copy.24
  32.7 26.9 %all_gather.17 = bf16[128,2048]{1,0:T(8,128)(2,1)} all-gather(bf16[16,2048]{1,0:T(8,128)(2,1)S(1)} %all_gather.16), channel_id=1, replica_groups=mesh['x'=4,'z'=8,'y_lo'=2,'y_hi'=4,'core'=2] {'z'}, dimensions={0}, use_global_device_ids=true | all-gather | bytes 589824 | tf_op jit(solution)/shard_map/all_gather | solution.py:85
  59.6 4.7 %all-to-all-done = bf16[128,8,768]{2,0,1:T(8,128)(2,1)} async-done(((bf16[128,8,768]{2,0,1:T(8,128)(2,1)}), bf16[128,8,768]{2,0,1:T(8,128)(2,1)}, u32[]{:S(2)}, u32[]{:S(2)}) %all-to-all-start) | async-done | bytes 1572896 | tf_op jit(solution)/shard_map/all_to_all | solution.py:88
  64.2 0.0 all-gather.4.cloned.1.call-update
  64.3 0.0 all-gather.6.cloned.1.call-start
  64.3 36.4 %all-gather.4.cloned.1.call-done = bf16[512,2048]{1,0:T(8,128)(2,1)} async-done(((bf16[128,2048]{1,0:T(8,128)(2,1)}), bf16[512,2048]{1,0:T(8,128)(2,1)}) %all-gather.4.cloned.1.call-update) | async-done | bytes 2097168 | tf_op jit(solution)/shard_map/all_gather | solution.py:107
  100.7 0.0 all-gather.6.cloned.1.call-update
  100.7 80.0 %all_to_all.36 = bf16[64,2,16,512]{3,2,1,0:T(8,128)(2,1)S(1)} all-to-all(bf16[64,2,16,512]{3,2,1,0:T(8,128)(2,1)S(1)} %bitcast.29), channel_id=1, replica_groups=mesh['x'=4,'z'=8,'y_lo'=2,'y_hi'=4,'core'=2] {'x','z','y_lo'}, dimensions={0} | all-to-all | bytes 4194304 | tf_op jit(solution)/shard_map/all_to_all | solution.py:109
  180.8 1.3 copy-done
  182.1 0.4 fusion.3
  182.4 0.1 reshape.85
  182.6 0.1 broadcast_in_dim.28
  182.6 1.6 convert_element_type.51.live_col_ref
  184.2 0.7 convert_element_type.47.live_row_ref
  184.9 16.8 %shard_map.55 = bf16[1024,256]{1,0:T(8,128)(2,1)} custom-call(bf16[1024,768]{1,0:T(8,128)(2,1)} %bitcast.3.q_ref.kn_ref.vn_ref, bf16[2048,512]{1,0:T(8,128)(2,1)} %bitcast.32, bf16[2048,512]{1,0:T(8,128)(2,1)} %bitcast.33, bf16[1024,768]{1,0:T(8,128)(2,1)} %bitcast.3.q_ref.kn_ref.vn_ref, bf16[1024,768]{1,0:T(8,128)(2,1)} %bitcast.3.q_ref.kn_ref.vn_ref, ...), custom_call_target="tpu_custom_call" | custom-call | flops 3221225472 | bytes 4194304 | tf_op jit(solution)/shard_map/pallas_call | solution.py:50
  201.7 1.3 copy.21
  203.0 60.9 %all_to_all.37 = bf16[8,128,256]{1,2,0:T(8,128)(2,1)S(1)} all-to-all(bf16[8,128,256]{1,2,0:T(8,128)(2,1)S(1)} %copy.21), channel_id=1, replica_groups=mesh['x'=4,'z'=8,'y_lo'=2,'y_hi'=4,'core'=2] {'y_hi','core'}, dimensions={0} | all-to-all | bytes 1048576 | tf_op jit(solution)/shard_map/all_to_all | solution.py:114
  264.0 0.2 copy.22
  264.2 18.8 %all-gather.6.cloned.1.call-done = bf16[2048,2048]{1,0:T(8,128)(2,1)} async-done(((bf16[512,2048]{1,0:T(8,128)(2,1)}), bf16[2048,2048]{1,0:T(8,128)(2,1)}) %all-gather.6.cloned.1.call-update) | async-done | bytes 8388624 | tf_op jit(solution)/shard_map/all_gather | solution.py:108
  283.1 5.5 %fusion.1 = bf16[1,128,2048]{2,1,0:T(8,128)(2,1)} fusion(bf16[128,2048]{0,1:T(8,128)(2,1)S(1)} %bitcast.31, bf16[2048,2048]{1,0:T(8,128)(2,1)} %all-gather.6.cloned.1.call-done), kind=kOutput, calls=%fused_computation.3 | convolution fusion | flops 1074003968 | bytes 9437184 | tf_op jit(solution)/shard_map/dot_general | solution.py:118
  (8 shorter events, 0.0 us)
Async XLA Ops:
  21.7 42.6 %all-to-all-start = ((bf16[128,8,768]{2,0,1:T(8,128)(2,1)}), bf16[128,8,768]{2,0,1:T(8,128)(2,1)}, u32[]{:S(2)}, u32[]{:S(2)}) async-start(bf16[128,8,768]{2,0,1:T(8,128)(2,1)} %copy.19), calls=%async_computation | async-start | bytes 3145728 | tf_op jit(solution)/shard_map/all_to_all | solution.py:88
  27.4 73.3 %all-gather.4.cloned.1.call-start = ((), (), s32[]{:S(2)}) async-start(), calls=%async_computation.3 | async-start | bytes 2621440 | tf_op jit(solution)/shard_map/all_gather | solution.py:107
  27.4 3.0 %copy-start.1 = (s32[128]{0:T(128)S(1)}, s32[128]{0:T(128)}, u32[]{:S(2)}) copy-start(s32[128]{0:T(128)} %param.7) | copy-start | bytes 1540
  27.4 3.3 %copy-start.2 = (s32[64]{0:T(128)S(1)}, s32[64]{0:T(128)}, u32[]{:S(2)}) copy-start(s32[64]{0:T(128)} %param.8) | copy-start | bytes 772
  64.3 218.8 %all-gather.6.cloned.1.call-start = ((), (), s32[]{:S(2)}) async-start(), calls=%async_computation.4 | async-start | bytes 10485760 | tf_op jit(solution)/shard_map/all_gather | solution.py:108
  180.8 1.3 copy-start
Sparse Core Ops, SparseCore 0:
  64.4 36.2 all-gather.3
  102.8 180.1 all-gather.5

commit v9 on v6

--- a/solution.py
+++ b/solution.py
@@ -82,7 +82,7 @@
     for name in reversed(DP[2:] + FSDP):
         weight = lax.all_gather(weight, name, axis=0, tiled=True)
     weight, group_qkv = lax.optimization_barrier((weight, group_qkv))
-    weight = lax.all_gather(weight, DP[1], axis=0, tiled=True)
+    weight = lax.all_gather(weight, DP[0], axis=0, tiled=True)
 
     local_qkv = group_qkv.reshape(tokens_here, fsdp_count, heads_here * 3 * HD)
     gathered_qkv = lax.all_to_all(local_qkv, FSDP, split_axis=1, concat_axis=0, tiled=True)
@@ -104,13 +104,16 @@
     packed = jnp.where(occupied[:, None], packed, jnp.nan)
     packed = packed.astype(jnp.bfloat16).reshape(requests, MOST, PAGE, features)
     weight, packed, gathered_qkv = lax.optimization_barrier((weight, packed, gathered_qkv))
-    weight = lax.all_gather(weight, DP[0], axis=0, tiled=True)
+    weight = lax.all_gather(weight, DP[1], axis=0, tiled=True)
     arrived = lax.all_to_all(packed, DP, split_axis=0, concat_axis=0, tiled=True)
     present = jnp.logical_not(jnp.isnan(arrived[:, :, 0, 0]))
     live_tokens = jnp.repeat(present.reshape(requests * MOST), PAGE)
     cached = arrived.reshape(requests * MOST * PAGE, features)
     attn_heads = attention(gathered_qkv, cached, live_tokens, heads_here, min(256, group_len))
     tokens_attn = lax.all_to_all(attn_heads, FSDP, split_axis=0, concat_axis=1, tiled=True)
+    outer = [size for _, size in PHYSICAL_SPLIT["dp"][:2]]
+    tokens_attn = tokens_attn.reshape(tokens_here, *outer, width // math.prod(outer))
+    tokens_attn = jnp.transpose(tokens_attn, (0, 2, 1, 3)).reshape(tokens_here, width)
     summed = jnp.dot(tokens_attn, weight, preferred_element_type=jnp.float32)
     return summed.astype(jnp.bfloat16).reshape(1, tokens_here, width)
 

time: 202 us -> 233 us (1.15)
  waiting for transfers between devices: 35.5 us -> 57.7 us
  blocking collectives: 107 us -> 116 us
    all_to_all x1, waiting for transfers between devices: 31.6 us -> 4.67 us  [per_device(): lax.all_to_all(local_qkv, FSDP, split_axis=1, concat_axis=0, tiled=True)]
    all_gather x1, waiting for transfers between devices: 0.01 us -> 26.1 us  [per_device(): weight = lax.all_gather(weight, DP[1], axis=0, tiled=True)]
    all_gather x1, waiting for transfers between devices: 3.86 us -> 26.1 us  [per_device(): weight = lax.all_gather(weight, DP[0], axis=0, tiled=True)]
    all_to_all x1, blocking collectives: 61.3 us -> 70.4 us  [per_device(): lax.all_to_all(packed, DP, split_axis=0, concat_axis=0, tiled=True)]
  transfers between devices with their start and end apart: 3 -> 3, of which waited for: 2 -> 3; matrix products, arithmetic and copies ran while one was open for 6% -> 4% of each run, Pallas kernels for 8% -> 7%
where the time goes in v9:
time: 233 us; the launch traced here: 232 us
  blocking collectives  116 us (50%)
  waiting for transfers between devices  57.7 us (25%)
  Pallas kernels  16.8 us (7%)
  between operations  13.5 us (6%)
  local copies, waits for them, and re-layouts  12.3 us (5%)
  starting transfers between devices  8.78 us (4%)
  matrix products  6.28 us (3%)
    all_to_all x1, blocking collectives, per_device(): lax.all_to_all(packed, DP, split_axis=0, concat_axis=0, tiled=True)  70.4 us
    all_gather x1, waiting for transfers between devices, per_device(): weight = lax.all_gather(weight, DP[1], axis=0, tiled=True)  26.1 us
    all_gather x1, waiting for transfers between devices, per_device(): weight = lax.all_gather(weight, DP[0], axis=0, tiled=True)  26.1 us
    all_gather x3, blocking collectives, per_device(): weight = lax.all_gather(weight, name, axis=0, tiled=True)  24 us
    all_to_all x1, blocking collectives, per_device(): lax.all_to_all(attn_heads, FSDP, split_axis=0, concat_axis=1, tiled=True)  21.7 us
    pallas_call x1, Pallas kernels, attention(): pl.pallas_call(functools.partial(attention_kernel, scale=1.0 / math.sqrt(...  16.8 us
    all_to_all x1, starting transfers between devices, per_device(): lax.all_to_all(local_qkv, FSDP, split_axis=1, concat_axis=0, tiled=True)  8.74 us
    unnamed x10, local copies, waits for them, and re-layouts  6.98 us
  transfers between devices with their start and end apart: 3, of which 3 were waited for; matrix products, arithmetic and copies ran while one was open for 4% of the time, Pallas kernels for 7%

profile of v9, /device:TPU:1, one launch (start us, length us, event | category | flops | bytes accessed | tf_op | source)
XLA Modules:
  0.0 232.3 jit_solution(4195633907202071166)
XLA Ops:
  6.5 8.5 %all-gather = bf16[2,4,2048]{2,1,0:T(4,128)(2,1)S(1)} all-gather(bf16[1,4,2048]{2,1,0:T(4,128)(2,1)} %bitcast.38), channel_id=1, replica_groups=mesh['x'=4,'z'=8,'y_lo'=2,'y_hi'=4,'core'=2] {'core'}, dimensions={0}, use_global_device_ids=true | all-gather | bytes 49152 | tf_op jit(solution)/shard_map/all_gather | solution.py:83
  15.1 10.9 %all_gather.16 = bf16[32,2048]{1,0:T(8,128)(2,1)S(1)} all-gather(bf16[8,2048]{1,0:T(8,128)(2,1)S(1)} %reshape.87), channel_id=1, replica_groups=mesh['x'=4,'z'=8,'y_lo'=2,'y_hi'=4,'core'=2] {'y_hi'}, dimensions={0}, use_global_device_ids=true | all-gather | bytes 163840 | tf_op jit(solution)/shard_map/all_gather | solution.py:83
  26.0 4.6 %all_gather.17 = bf16[64,2048]{1,0:T(8,128)(2,1)} all-gather(bf16[32,2048]{1,0:T(8,128)(2,1)S(1)} %all_gather.16), channel_id=1, replica_groups=mesh['x'=4,'z'=8,'y_lo'=2,'y_hi'=4,'core'=2] {'y_lo'}, dimensions={0}, use_global_device_ids=true | all-gather | bytes 393216 | tf_op jit(solution)/shard_map/all_gather | solution.py:83
  30.6 1.7 copy.25
  32.3 1.4 copy.19
  33.7 8.7 %all-to-all-start = ((bf16[128,8,768]{2,0,1:T(8,128)(2,1)}), bf16[128,8,768]{2,0,1:T(8,128)(2,1)}, u32[]{:S(2)}, u32[]{:S(2)}) async-start(bf16[128,8,768]{2,0,1:T(8,128)(2,1)} %copy.19), calls=%async_computation | async-start | bytes 3145728 | tf_op jit(solution)/shard_map/all_to_all | solution.py:88
  42.5 0.7 all-gather.4.cloned.1.call-update
  43.2 0.0 all-gather.6.cloned.1.call-start
  43.3 0.0 copy-start.1
  43.3 0.0 copy-start.2
  43.3 3.0 %copy.23 = bf16[16,8,16,512]{3,1,2,0:T(8,128)(2,1)S(1)} copy(bf16[16,8,16,512]{3,2,1,0:T(8,128)(2,1)} %bitcast.34) | data formatting | bytes 4194304
  46.3 0.1 fusion.2
  46.4 0.2 reduce_window_sum.11
  46.5 0.2 select_reduce_fusion.1
  46.8 0.1 convert_reduce_fusion
  46.9 0.8 fusion
  47.7 0.8 copy.24
  48.5 26.1 %all-gather.4.cloned.1.call-done = bf16[256,2048]{1,0:T(8,128)(2,1)} async-done(((bf16[64,2048]{1,0:T(8,128)(2,1)}), bf16[256,2048]{1,0:T(8,128)(2,1)}) %all-gather.4.cloned.1.call-update) | async-done | bytes 1048592 | tf_op jit(solution)/shard_map/all_gather | solution.py:85
  74.7 4.7 %all-to-all-done = bf16[128,8,768]{2,0,1:T(8,128)(2,1)} async-done(((bf16[128,8,768]{2,0,1:T(8,128)(2,1)}), bf16[128,8,768]{2,0,1:T(8,128)(2,1)}, u32[]{:S(2)}, u32[]{:S(2)}) %all-to-all-start) | async-done | bytes 1572896 | tf_op jit(solution)/shard_map/all_to_all | solution.py:88
  79.4 0.0 all-gather.6.cloned.1.call-update
  79.4 70.4 %all_to_all.36 = bf16[64,2,16,512]{3,2,1,0:T(8,128)(2,1)S(1)} all-to-all(bf16[64,2,16,512]{3,2,1,0:T(8,128)(2,1)S(1)} %bitcast.29), channel_id=1, replica_groups=mesh['x'=4,'z'=8,'y_lo'=2,'y_hi'=4,'core'=2] {'x','z','y_lo'}, dimensions={0} | all-to-all | bytes 4194304 | tf_op jit(solution)/shard_map/all_to_all | solution.py:108
  149.8 1.4 copy-done
  151.2 0.4 fusion.3
  151.5 0.1 reshape.85
  151.7 0.1 broadcast_in_dim.28
  151.7 1.6 convert_element_type.51.live_col_ref
  153.3 0.7 convert_element_type.47.live_row_ref
  154.0 16.8 %shard_map.55 = bf16[1024,256]{1,0:T(8,128)(2,1)} custom-call(bf16[1024,768]{1,0:T(8,128)(2,1)} %bitcast.3.q_ref.kn_ref.vn_ref, bf16[2048,512]{1,0:T(8,128)(2,1)} %bitcast.32, bf16[2048,512]{1,0:T(8,128)(2,1)} %bitcast.33, bf16[1024,768]{1,0:T(8,128)(2,1)} %bitcast.3.q_ref.kn_ref.vn_ref, bf16[1024,768]{1,0:T(8,128)(2,1)} %bitcast.3.q_ref.kn_ref.vn_ref, ...), custom_call_target="tpu_custom_call" | custom-call | flops 3221225472 | bytes 4194304 | tf_op jit(solution)/shard_map/pallas_call | solution.py:50
  170.8 1.3 copy.21
  172.2 21.7 %all_to_all.37 = bf16[8,128,256]{1,2,0:T(8,128)(2,1)S(1)} all-to-all(bf16[8,128,256]{1,2,0:T(8,128)(2,1)S(1)} %copy.21), channel_id=1, replica_groups=mesh['x'=4,'z'=8,'y_lo'=2,'y_hi'=4,'core'=2] {'y_hi','core'}, dimensions={0} | all-to-all | bytes 1048576 | tf_op jit(solution)/shard_map/all_to_all | solution.py:113
  193.9 26.1 %all-gather.6.cloned.1.call-done = bf16[2048,2048]{1,0:T(8,128)(2,1)} async-done(((bf16[256,2048]{1,0:T(8,128)(2,1)}), bf16[2048,2048]{1,0:T(8,128)(2,1)}) %all-gather.6.cloned.1.call-update) | async-done | bytes 8388624 | tf_op jit(solution)/shard_map/all_gather | solution.py:107
  220.1 5.5 %fusion.1 = bf16[1,128,2048]{2,1,0:T(8,128)(2,1)} fusion(bf16[128,2048]{0,1:T(8,128)(2,1)S(1)} %bitcast.31, bf16[2048,2048]{1,0:T(8,128)(2,1)} %all-gather.6.cloned.1.call-done), kind=kOutput, calls=%fused_computation.3 | convolution fusion | flops 1074003968 | bytes 9437184 | tf_op jit(solution)/shard_map/dot_general | solution.py:117
  (8 shorter events, 0.1 us)
Async XLA Ops:
  33.7 45.6 %all-to-all-start = ((bf16[128,8,768]{2,0,1:T(8,128)(2,1)}), bf16[128,8,768]{2,0,1:T(8,128)(2,1)}, u32[]{:S(2)}, u32[]{:S(2)}) async-start(bf16[128,8,768]{2,0,1:T(8,128)(2,1)} %copy.19), calls=%async_computation | async-start | bytes 3145728 | tf_op jit(solution)/shard_map/all_to_all | solution.py:88
  42.5 32.2 %all-gather.4.cloned.1.call-start = ((), (), s32[]{:S(2)}) async-start(), calls=%async_computation.3 | async-start | bytes 1310720 | tf_op jit(solution)/shard_map/all_gather | solution.py:85
  43.2 176.8 %all-gather.6.cloned.1.call-start = ((), (), s32[]{:S(2)}) async-start(), calls=%async_computation.4 | async-start | bytes 9437184 | tf_op jit(solution)/shard_map/all_gather | solution.py:107
  43.3 3.0 %copy-start.1 = (s32[128]{0:T(128)S(1)}, s32[128]{0:T(128)}, u32[]{:S(2)}) copy-start(s32[128]{0:T(128)} %param.7) | copy-start | bytes 1540
  43.3 3.3 %copy-start.2 = (s32[64]{0:T(128)S(1)}, s32[64]{0:T(128)}, u32[]{:S(2)}) copy-start(s32[64]{0:T(128)} %param.8) | copy-start | bytes 772
  149.8 1.4 copy-start
Sparse Core Ops, SparseCore 0:
  45.4 29.2 all-gather.3
  79.5 140.5 all-gather.5

commit v10 on v6

--- a/solution.py
+++ b/solution.py
@@ -104,13 +104,19 @@
     packed = jnp.where(occupied[:, None], packed, jnp.nan)
     packed = packed.astype(jnp.bfloat16).reshape(requests, MOST, PAGE, features)
     weight, packed, gathered_qkv = lax.optimization_barrier((weight, packed, gathered_qkv))
+    half = weight.shape[0] // 2
+    weight = lax.dynamic_slice_in_dim(weight, lax.axis_index(FSDP[-1]) * half, half, axis=0)
     weight = lax.all_gather(weight, DP[0], axis=0, tiled=True)
     arrived = lax.all_to_all(packed, DP, split_axis=0, concat_axis=0, tiled=True)
+    weight, arrived = lax.optimization_barrier((weight, arrived))
+    weight = lax.all_gather(weight, FSDP[-1], axis=0, tiled=True)
     present = jnp.logical_not(jnp.isnan(arrived[:, :, 0, 0]))
     live_tokens = jnp.repeat(present.reshape(requests * MOST), PAGE)
     cached = arrived.reshape(requests * MOST * PAGE, features)
     attn_heads = attention(gathered_qkv, cached, live_tokens, heads_here, min(256, group_len))
     tokens_attn = lax.all_to_all(attn_heads, FSDP, split_axis=0, concat_axis=1, tiled=True)
+    tokens_attn = tokens_attn.reshape(tokens_here, lax.axis_size(DP[0]), 2, half)
+    tokens_attn = jnp.transpose(tokens_attn, (0, 2, 1, 3)).reshape(tokens_here, width)
     summed = jnp.dot(tokens_attn, weight, preferred_element_type=jnp.float32)
     return summed.astype(jnp.bfloat16).reshape(1, tokens_here, width)
 

time: 202 us -> 211 us (1.045)
  waiting for transfers between devices: 35.5 us -> 45.7 us
    all_gather x1, waiting for transfers between devices: 3.86 us -> 14.1 us  [per_device(): weight = lax.all_gather(weight, DP[0], axis=0, tiled=True)]
    dynamic_slice x0 -> x1, local copies, waits for them, and re-layouts: none -> 2.32 us  [per_device(): lax.dynamic_slice_in_dim(weight, lax.axis_index(FSDP[-1]) * half, half, a...]
    unnamed x10 -> x8, local copies, waits for them, and re-layouts: 6.89 us -> 5.59 us
  transfers between devices with their start and end apart: 3 -> 4, of which waited for: 2 -> 2; matrix products, arithmetic and copies ran while one was open for 6% -> 6% of each run, Pallas kernels for 8% -> 8%
where the time goes in v10:
time: 211 us
  blocking collectives  106 us (50%)
  waiting for transfers between devices  45.7 us (22%)
  Pallas kernels  16.8 us (8%)
  between operations  13.2 us (6%)
  local copies, waits for them, and re-layouts  12.1 us (6%)
  starting transfers between devices  8.79 us (4%)
  matrix products  6.28 us (3%)
    all_to_all x1, blocking collectives, per_device(): lax.all_to_all(packed, DP, split_axis=0, concat_axis=0, tiled=True)  61.4 us
    all_to_all x1, waiting for transfers between devices, per_device(): lax.all_to_all(local_qkv, FSDP, split_axis=1, concat_axis=0, tiled=True)  31.6 us
    all_gather x3, blocking collectives, per_device(): weight = lax.all_gather(weight, name, axis=0, tiled=True)  24 us
    all_to_all x1, blocking collectives, per_device(): lax.all_to_all(attn_heads, FSDP, split_axis=0, concat_axis=1, tiled=True)  20.4 us
    pallas_call x1, Pallas kernels, attention(): pl.pallas_call(functools.partial(attention_kernel, scale=1.0 / math.sqrt(...  16.8 us
    all_gather x1, waiting for transfers between devices, per_device(): weight = lax.all_gather(weight, DP[0], axis=0, tiled=True)  14.1 us
    all_to_all x1, starting transfers between devices, per_device(): lax.all_to_all(local_qkv, FSDP, split_axis=1, concat_axis=0, tiled=True)  8.74 us
    unnamed x8, local copies, waits for them, and re-layouts  5.59 us
  transfers between devices with their start and end apart: 4, of which 2 were waited for; matrix products, arithmetic and copies ran while one was open for 6% of the time, Pallas kernels for 8%

profile of v10, /device:TPU:1, one launch (start us, length us, event | category | flops | bytes accessed | tf_op | source)
XLA Modules:
  0.0 210.6 jit_solution(3623493280306328992)
XLA Ops:
  6.5 8.5 %all-gather = bf16[2,4,2048]{2,1,0:T(4,128)(2,1)S(1)} all-gather(bf16[1,4,2048]{2,1,0:T(4,128)(2,1)} %bitcast.38), channel_id=1, replica_groups=mesh['x'=4,'z'=8,'y_lo'=2,'y_hi'=4,'core'=2] {'core'}, dimensions={0}, use_global_device_ids=true | all-gather | bytes 49152 | tf_op jit(solution)/shard_map/all_gather | solution.py:83
  15.1 10.9 %all_gather.19 = bf16[32,2048]{1,0:T(8,128)(2,1)S(1)} all-gather(bf16[8,2048]{1,0:T(8,128)(2,1)S(1)} %reshape.87), channel_id=1, replica_groups=mesh['x'=4,'z'=8,'y_lo'=2,'y_hi'=4,'core'=2] {'y_hi'}, dimensions={0}, use_global_device_ids=true | all-gather | bytes 163840 | tf_op jit(solution)/shard_map/all_gather | solution.py:83
  26.0 4.6 %all_gather.20 = bf16[64,2048]{1,0:T(8,128)(2,1)} all-gather(bf16[32,2048]{1,0:T(8,128)(2,1)S(1)} %all_gather.19), channel_id=1, replica_groups=mesh['x'=4,'z'=8,'y_lo'=2,'y_hi'=4,'core'=2] {'y_lo'}, dimensions={0}, use_global_device_ids=true | all-gather | bytes 393216 | tf_op jit(solution)/shard_map/all_gather | solution.py:83
  30.6 0.0 all-gather.5.cloned.1.call-update
  30.6 1.7 copy.26
  32.3 1.4 copy.21
  33.8 8.7 %all-to-all-start = ((bf16[128,8,768]{2,0,1:T(8,128)(2,1)}), bf16[128,8,768]{2,0,1:T(8,128)(2,1)}, u32[]{:S(2)}, u32[]{:S(2)}) async-start(bf16[128,8,768]{2,0,1:T(8,128)(2,1)} %copy.21), calls=%async_computation | async-start | bytes 3145728 | tf_op jit(solution)/shard_map/all_to_all | solution.py:88
  42.5 3.0 %copy.24 = bf16[16,8,16,512]{3,1,2,0:T(8,128)(2,1)S(1)} copy(bf16[16,8,16,512]{3,2,1,0:T(8,128)(2,1)} %bitcast.34) | data formatting | bytes 4194304
  45.5 0.0 copy-done
  45.5 0.1 fusion.2
  45.6 0.2 reduce_window_sum.11
  45.8 0.2 select_reduce_fusion.1
  46.0 0.1 convert_reduce_fusion
  46.1 0.8 fusion
  47.0 0.8 copy.25
  47.8 31.6 %all-to-all-done = bf16[128,8,768]{2,0,1:T(8,128)(2,1)} async-done(((bf16[128,8,768]{2,0,1:T(8,128)(2,1)}), bf16[128,8,768]{2,0,1:T(8,128)(2,1)}, u32[]{:S(2)}, u32[]{:S(2)}) %all-to-all-start) | async-done | bytes 1572896 | tf_op jit(solution)/shard_map/all_to_all | solution.py:88
  79.4 2.3 %constant_dynamic-slice_fusion = bf16[256,2048]{1,0:T(8,128)(2,1)} fusion(bf16[512,2048]{1,0:T(8,128)(2,1)} %all-gather.5.cloned.1.call-done, s32[]{:T(128)S(6)} %select_n.17), kind=kLoop, calls=%fused_computation.16 | loop fusion | bytes 2097156 | tf_op jit(solution)/shard_map/dynamic_slice | solution.py:108
  81.7 0.0 all-gather.7.cloned.1.call-update
  81.7 0.0 all-gather.9.cloned.1.call-start
  81.8 61.4 %all_to_all.36 = bf16[64,2,16,512]{3,2,1,0:T(8,128)(2,1)} all-to-all(bf16[64,2,16,512]{3,2,1,0:T(8,128)(2,1)S(1)} %bitcast.29), channel_id=1, replica_groups=mesh['x'=4,'z'=8,'y_lo'=2,'y_hi'=4,'core'=2] {'x','z','y_lo'}, dimensions={0} | all-to-all | bytes 4194304 | tf_op jit(solution)/shard_map/all_to_all | solution.py:110
  143.1 14.1 %all-gather.7.cloned.1.call-done = bf16[1024,2048]{1,0:T(8,128)(2,1)} async-done(((bf16[256,2048]{1,0:T(8,128)(2,1)}), bf16[1024,2048]{1,0:T(8,128)(2,1)}) %all-gather.7.cloned.1.call-update) | async-done | bytes 4194320 | tf_op jit(solution)/shard_map/all_gather | solution.py:109
  157.2 0.0 all-gather.9.cloned.1.call-update
  157.3 1.3 fusion.3
  158.6 0.1 reshape.85
  158.7 0.1 broadcast_in_dim.28
  158.8 1.6 convert_element_type.51.live_col_ref
  160.4 0.7 convert_element_type.47.live_row_ref
  161.1 16.8 %shard_map.55 = bf16[1024,256]{1,0:T(8,128)(2,1)} custom-call(bf16[1024,768]{1,0:T(8,128)(2,1)} %bitcast.3.q_ref.kn_ref.vn_ref, bf16[2048,512]{1,0:T(8,128)(2,1)} %bitcast.32, bf16[2048,512]{1,0:T(8,128)(2,1)} %bitcast.33, bf16[1024,768]{1,0:T(8,128)(2,1)} %bitcast.3.q_ref.kn_ref.vn_ref, bf16[1024,768]{1,0:T(8,128)(2,1)} %bitcast.3.q_ref.kn_ref.vn_ref, ...), custom_call_target="tpu_custom_call" | custom-call | flops 3221225472 | bytes 4194304 | tf_op jit(solution)/shard_map/pallas_call | solution.py:50
  177.9 20.4 %all_to_all.37 = bf16[8,128,256]{2,1,0:T(8,128)(2,1)S(1)} all-to-all(bf16[8,128,256]{2,1,0:T(8,128)(2,1)} %bitcast.37), channel_id=1, replica_groups=mesh['x'=4,'z'=8,'y_lo'=2,'y_hi'=4,'core'=2] {'y_hi','core'}, dimensions={0} | all-to-all | bytes 1048576 | tf_op jit(solution)/shard_map/all_to_all | solution.py:117
  198.3 0.3 copy.23
  198.5 0.0 all-gather.9.cloned.1.call-done
  198.6 5.5 %fusion.1 = bf16[1,128,2048]{2,1,0:T(8,128)(2,1)} fusion(bf16[128,2048]{0,1:T(8,128)(2,1)S(1)} %bitcast.31, bf16[2048,2048]{1,0:T(8,128)(2,1)} %all-gather.9.cloned.1.call-done), kind=kOutput, calls=%fused_computation.3 | convolution fusion | flops 1074003968 | bytes 9437184 | tf_op jit(solution)/shard_map/dot_general | solution.py:120
  (9 shorter events, 0.0 us)
Async XLA Ops:
  6.5 72.9 %all-gather.5.cloned.1.call-start = ((), (), s32[]{:S(2)}) async-start(), calls=%async_computation.3 | async-start | bytes 2359296 | tf_op jit(solution)/shard_map/all_gather | solution.py:85
  33.8 45.6 %all-to-all-start = ((bf16[128,8,768]{2,0,1:T(8,128)(2,1)}), bf16[128,8,768]{2,0,1:T(8,128)(2,1)}, u32[]{:S(2)}, u32[]{:S(2)}) async-start(bf16[128,8,768]{2,0,1:T(8,128)(2,1)} %copy.21), calls=%async_computation | async-start | bytes 3145728 | tf_op jit(solution)/shard_map/all_to_all | solution.py:88
  42.5 114.7 %all-gather.7.cloned.1.call-start = ((), (), s32[]{:S(2)}) async-start(), calls=%async_computation.4 | async-start | bytes 5242880 | tf_op jit(solution)/shard_map/all_gather | solution.py:109
  42.5 3.0 %copy-start = (s32[128]{0:T(128)S(1)}, s32[128]{0:T(128)}, u32[]{:S(2)}) copy-start(s32[128]{0:T(128)} %param.7) | copy-start | bytes 1540
  42.5 3.3 %copy-start.1 = (s32[64]{0:T(128)S(1)}, s32[64]{0:T(128)}, u32[]{:S(2)}) copy-start(s32[64]{0:T(128)} %param.8) | copy-start | bytes 772
  81.7 116.8 %all-gather.9.cloned.1.call-start = ((), (), s32[]{:S(2)}) async-start(), calls=%async_computation.5 | async-start | bytes 12582912 | tf_op jit(solution)/shard_map/all_gather | solution.py:112
Sparse Core Ops, SparseCore 0:
  30.7 43.5 all-gather.4
  81.9 75.3 all-gather.6
  159.3 25.8 all-gather.8

commit v11 on v6

--- a/solution.py
+++ b/solution.py
@@ -69,6 +69,19 @@
     )(qkv, cache, cache, qkv, qkv, live.reshape(1, keys), live.reshape(keys, 1))
 
 
+def ring_gather(block, name):
+    n = lax.axis_size(name)
+    assert n == 4
+    forward = [(i, (i + 1) % n) for i in range(n)]
+    backward = [(i, (i - 1) % n) for i in range(n)]
+    from_prev = lax.ppermute(block, name, forward)
+    from_next = lax.ppermute(block, name, backward)
+    from_opposite = lax.ppermute(from_prev, name, forward)
+    stack = jnp.stack([block, from_next, from_opposite, from_prev])
+    stack = jnp.roll(stack, lax.axis_index(name), axis=0)
+    return stack.reshape(n * block.shape[0], *block.shape[1:])
+
+
 def per_device(group_qkv, cache_pool, page_request, request_host, out_weight, *, fsdp_count, dp_count):
     requests = request_host.shape[0]
     slot_count = page_request.shape[0]
@@ -78,9 +91,9 @@
     score_scale = 1.0 / math.sqrt(HD)
     width = out_weight.shape[1]
 
-    weight = out_weight
-    for name in reversed(DP[2:] + FSDP):
-        weight = lax.all_gather(weight, name, axis=0, tiled=True)
+    weight = lax.all_gather(out_weight, FSDP[1], axis=0, tiled=True)
+    weight = ring_gather(weight, FSDP[0])
+    weight = lax.all_gather(weight, DP[2], axis=0, tiled=True)
     weight, group_qkv = lax.optimization_barrier((weight, group_qkv))
     weight = lax.all_gather(weight, DP[1], axis=0, tiled=True)
 

time: 202 us -> 205 us (1.015)
  blocking collectives: 107 us -> 97.7 us
  starting transfers between devices: 8.75 us -> 17.9 us
  waiting for transfers between devices: 35.5 us -> 42.4 us
  local copies, waits for them, and re-layouts: 12.1 us -> 9.16 us
    all_gather x3 -> x2, blocking collectives: 24 us -> 13.2 us  [the longest x1 8.65 us: per_device(): weight = lax.all_gather(out_weight, FSDP[1], axis=0, tiled=True)]
    ppermute x0 -> x3, starting transfers between devices: none -> 9.43 us  [the longest x1 4.26 us: ring_gather(): from_prev = lax.ppermute(block, name, forward)]
    ppermute x0 -> x3, waiting for transfers between devices: none -> 5.96 us  [the longest x1 3.5 us: ring_gather(): from_opposite = lax.ppermute(from_prev, name, forward)]
    unnamed x10 -> x21, local copies, waits for them, and re-layouts: 6.89 us -> 3.9 us
    all_to_all x1, blocking collectives: 22 us -> 24.9 us  [per_device(): lax.all_to_all(attn_heads, FSDP, split_axis=0, concat_axis=1, tiled=True)]
  transfers between devices with their start and end apart: 3 -> 6, of which waited for: 2 -> 4; matrix products, arithmetic and copies ran while one was open for 6% -> 5% of each run, Pallas kernels for 8% -> 8%
where the time goes in v11:
time: 205 us
  blocking collectives  97.7 us (48%)
  waiting for transfers between devices  42.4 us (21%)
  starting transfers between devices  17.9 us (9%)
  Pallas kernels  16.8 us (8%)
  between operations  13.6 us (7%)
  local copies, waits for them, and re-layouts  9.16 us (4%)
  matrix products  6.28 us (3%)
    all_to_all x1, blocking collectives, per_device(): lax.all_to_all(packed, DP, split_axis=0, concat_axis=0, tiled=True)  59.6 us
    all_to_all x1, waiting for transfers between devices, per_device(): lax.all_to_all(local_qkv, FSDP, split_axis=1, concat_axis=0, tiled=True)  33.2 us
    all_to_all x1, blocking collectives, per_device(): lax.all_to_all(attn_heads, FSDP, split_axis=0, concat_axis=1, tiled=True)  24.9 us
    pallas_call x1, Pallas kernels, attention(): pl.pallas_call(functools.partial(attention_kernel, scale=1.0 / math.sqrt(...  16.8 us
    all_gather x1, blocking collectives, per_device(): weight = lax.all_gather(out_weight, FSDP[1], axis=0, tiled=True)  8.65 us
    all_to_all x1, starting transfers between devices, per_device(): lax.all_to_all(local_qkv, FSDP, split_axis=1, concat_axis=0, tiled=True)  8.44 us
    dot_general x1, matrix products, per_device(): summed = jnp.dot(tokens_attn, weight, preferred_element_type=jnp.float32)  5.46 us
    all_gather x1, blocking collectives, per_device(): weight = lax.all_gather(weight, DP[2], axis=0, tiled=True)  4.59 us
  transfers between devices with their start and end apart: 6, of which 4 were waited for; matrix products, arithmetic and copies ran while one was open for 5% of the time, Pallas kernels for 8%

profile of v11, /device:TPU:1, one launch (start us, length us, event | category | flops | bytes accessed | tf_op | source)
XLA Modules:
  0.0 204.8 jit_solution(2122833154210610812)
XLA Ops:
  6.5 8.7 %all-gather = bf16[2,4,2048]{2,1,0:T(4,128)(2,1)S(1)} all-gather(bf16[1,4,2048]{2,1,0:T(4,128)(2,1)} %bitcast.45), channel_id=1, replica_groups=mesh['x'=4,'z'=8,'y_lo'=2,'y_hi'=4,'core'=2] {'core'}, dimensions={0}, use_global_device_ids=true | all-gather | bytes 49152 | tf_op jit(solution)/shard_map/all_gather | solution.py:94
  15.2 1.9 collective-permute-start
  17.1 4.3 %collective-permute-start.1 = (bf16[8,2048]{1,0:T(8,128)(2,1)S(1)}, bf16[8,2048]{1,0:T(8,128)(2,1)S(1)}, u32[]{:S(2)}, u32[]{:S(2)}) collective-permute-start(bf16[8,2048]{1,0:T(8,128)(2,1)S(1)} %reshape.82), channel_id=1, source_target_pairs={{0,2},{2,4},{4,6},{6,0},{1,3},{3,5},{5,7},{7,1},{8,10},{10,12},{12... | collective-permute-start | bytes 98312 | tf_op jit(solution)/shard_map/ppermute | solution.py:77
  21.5 2.5 %collective-permute-done.1 = bf16[8,2048]{1,0:T(8,128)(2,1)S(1)} collective-permute-done((bf16[8,2048]{1,0:T(8,128)(2,1)S(1)}, bf16[8,2048]{1,0:T(8,128)(2,1)S(1)}, u32[]{:S(2)}, u32[]{:S(2)}) %collective-permute-start.1) | collective-permute-done | bytes 32800 | tf_op jit(solution)/shard_map/ppermute | solution.py:77
  23.9 3.2 %collective-permute-start.2 = (bf16[8,2048]{1,0:T(8,128)(2,1)S(1)}, bf16[8,2048]{1,0:T(8,128)(2,1)S(1)}, u32[]{:S(2)}, u32[]{:S(2)}) collective-permute-start(bf16[8,2048]{1,0:T(8,128)(2,1)S(1)} %collective-permute-done.1), channel_id=1, source_target_pairs={{0,2},{2,4},{4,6},{6,0},{1,3},{3,5},{5,7},{7,1},{8,10},{10,12},{12... | collective-permute-start | bytes 98312 | tf_op jit(solution)/shard_map/ppermute | solution.py:79
  27.2 3.5 %collective-permute-done.2 = bf16[8,2048]{1,0:T(8,128)(2,1)S(1)} collective-permute-done((bf16[8,2048]{1,0:T(8,128)(2,1)S(1)}, bf16[8,2048]{1,0:T(8,128)(2,1)S(1)}, u32[]{:S(2)}, u32[]{:S(2)}) %collective-permute-start.2) | collective-permute-done | bytes 32800 | tf_op jit(solution)/shard_map/ppermute | solution.py:79
  30.8 4.6 %all_gather.13 = bf16[64,2048]{1,0:T(8,128)(2,1)} all-gather(bf16[32,2048]{1,0:T(8,128)(2,1)S(1)} %dynamic-slice_bitcast_fusion), channel_id=1, replica_groups=mesh['x'=4,'z'=8,'y_lo'=2,'y_hi'=4,'core'=2] {'y_lo'}, dimensions={0}, use_global_device_ids=true | all-gather | bytes 393216 | tf_op jit(solution)/shard_map/all_gather | solution.py:96
  35.4 0.0 all-gather.4.cloned.1.call-update
  35.4 0.3 copy.22
  35.7 1.4 copy.17
  37.2 8.4 %all-to-all-start = ((bf16[128,8,768]{2,0,1:T(8,128)(2,1)}), bf16[128,8,768]{2,0,1:T(8,128)(2,1)}, u32[]{:S(2)}, u32[]{:S(2)}) async-start(bf16[128,8,768]{2,0,1:T(8,128)(2,1)} %copy.17), calls=%async_computation | async-start | bytes 3145728 | tf_op jit(solution)/shard_map/all_to_all | solution.py:101
  45.6 0.1 fusion.2
  45.7 0.2 reduce_window_sum.11
  45.9 1.4 copy.20
  47.3 0.2 select_reduce_fusion.1
  47.5 0.1 convert_reduce_fusion
  47.6 0.8 fusion
  48.5 0.8 copy.21
  49.3 33.2 %all-to-all-done = bf16[128,8,768]{2,0,1:T(8,128)(2,1)} async-done(((bf16[128,8,768]{2,0,1:T(8,128)(2,1)}), bf16[128,8,768]{2,0,1:T(8,128)(2,1)}, u32[]{:S(2)}, u32[]{:S(2)}) %all-to-all-start) | async-done | bytes 1572896 | tf_op jit(solution)/shard_map/all_to_all | solution.py:101
  82.5 0.0 all-gather.6.cloned.1.call-update
  82.5 59.6 %all_to_all.39 = bf16[64,2,16,512]{3,2,1,0:T(8,128)(2,1)S(1)} all-to-all(bf16[64,2,16,512]{3,2,1,0:T(8,128)(2,1)S(1)} %bitcast.37), channel_id=1, replica_groups=mesh['x'=4,'z'=8,'y_lo'=2,'y_hi'=4,'core'=2] {'x','z','y_lo'}, dimensions={0} | all-to-all | bytes 4194304 | tf_op jit(solution)/shard_map/all_to_all | solution.py:121
  142.1 1.3 copy-done
  143.4 0.4 fusion.3
  143.7 0.1 reshape.80
  143.9 0.1 broadcast_in_dim.28
  143.9 1.6 convert_element_type.51.live_col_ref
  145.5 0.7 convert_element_type.47.live_row_ref
  146.2 16.8 %shard_map.55 = bf16[1024,256]{1,0:T(8,128)(2,1)} custom-call(bf16[1024,768]{1,0:T(8,128)(2,1)} %bitcast.7.q_ref.kn_ref.vn_ref, bf16[2048,512]{1,0:T(8,128)(2,1)} %bitcast.40, bf16[2048,512]{1,0:T(8,128)(2,1)} %bitcast.41, bf16[1024,768]{1,0:T(8,128)(2,1)} %bitcast.7.q_ref.kn_ref.vn_ref, bf16[1024,768]{1,0:T(8,128)(2,1)} %bitcast.7.q_ref.kn_ref.vn_ref, ...), custom_call_target="tpu_custom_call" | custom-call | flops 3221225472 | bytes 4194304 | tf_op jit(solution)/shard_map/pallas_call | solution.py:50
  163.0 1.3 copy.19
  164.3 24.9 %all_to_all.40 = bf16[8,128,256]{1,2,0:T(8,128)(2,1)S(1)} all-to-all(bf16[8,128,256]{1,2,0:T(8,128)(2,1)S(1)} %copy.19), channel_id=1, replica_groups=mesh['x'=4,'z'=8,'y_lo'=2,'y_hi'=4,'core'=2] {'y_hi','core'}, dimensions={0} | all-to-all | bytes 1048576 | tf_op jit(solution)/shard_map/all_to_all | solution.py:126
  189.3 3.2 %all-gather.6.cloned.1.call-done = bf16[2048,2048]{1,0:T(8,128)(2,1)} async-done(((bf16[512,2048]{1,0:T(8,128)(2,1)}), bf16[2048,2048]{1,0:T(8,128)(2,1)}) %all-gather.6.cloned.1.call-update) | async-done | bytes 8388624 | tf_op jit(solution)/shard_map/all_gather | solution.py:120
  192.5 5.5 %fusion.1 = bf16[1,128,2048]{2,1,0:T(8,128)(2,1)} fusion(bf16[128,2048]{0,1:T(8,128)(2,1)S(1)} %bitcast.39, bf16[2048,2048]{1,0:T(8,128)(2,1)} %all-gather.6.cloned.1.call-done), kind=kOutput, calls=%fused_computation.3 | convolution fusion | flops 1074003968 | bytes 9437184 | tf_op jit(solution)/shard_map/dot_general | solution.py:127
  (26 shorter events, 0.1 us)
Async XLA Ops:
  6.5 28.8 %copy-start.2 = (bf16[1,128,6144]{2,1,0:T(8,128)(2,1)S(1)}, bf16[1,128,6144]{2,1,0:T(8,128)(2,1)}, u32[]{:S(2)}) copy-start(bf16[1,128,6144]{2,1,0:T(8,128)(2,1)} %param.5) | copy-start | bytes 4718596
  6.5 75.9 %all-gather.4.cloned.1.call-start = ((), (), s32[]{:S(2)}) async-start(), calls=%async_computation.3 | async-start | bytes 2359296 | tf_op jit(solution)/shard_map/all_gather | solution.py:98
  15.2 12.0 %collective-permute-start = (bf16[8,2048]{1,0:T(8,128)(2,1)S(1)}, bf16[8,2048]{1,0:T(8,128)(2,1)S(1)}, u32[]{:S(2)}, u32[]{:S(2)}) collective-permute-start(bf16[8,2048]{1,0:T(8,128)(2,1)S(1)} %reshape.82), channel_id=1, source_target_pairs={{0,6},{2,0},{4,2},{6,4},{1,7},{3,1},{5,3},{7,5},{8,14},{10,8},{12,... | collective-permute-start | bytes 98312 | tf_op jit(solution)/shard_map/ppermute | solution.py:78
  17.1 6.8 %collective-permute-start.1 = (bf16[8,2048]{1,0:T(8,128)(2,1)S(1)}, bf16[8,2048]{1,0:T(8,128)(2,1)S(1)}, u32[]{:S(2)}, u32[]{:S(2)}) collective-permute-start(bf16[8,2048]{1,0:T(8,128)(2,1)S(1)} %reshape.82), channel_id=1, source_target_pairs={{0,2},{2,4},{4,6},{6,0},{1,3},{3,5},{5,7},{7,1},{8,10},{10,12},{12... | collective-permute-start | bytes 98312 | tf_op jit(solution)/shard_map/ppermute | solution.py:77
  23.9 6.8 %collective-permute-start.2 = (bf16[8,2048]{1,0:T(8,128)(2,1)S(1)}, bf16[8,2048]{1,0:T(8,128)(2,1)S(1)}, u32[]{:S(2)}, u32[]{:S(2)}) collective-permute-start(bf16[8,2048]{1,0:T(8,128)(2,1)S(1)} %collective-permute-done.1), channel_id=1, source_target_pairs={{0,2},{2,4},{4,6},{6,0},{1,3},{3,5},{5,7},{7,1},{8,10},{10,12},{12... | collective-permute-start | bytes 98312 | tf_op jit(solution)/shard_map/ppermute | solution.py:79
  37.2 8.4 %copy-start.3 = (s32[128]{0:T(128)S(1)}, s32[128]{0:T(128)}, u32[]{:S(2)}) copy-start(s32[128]{0:T(128)} %param.7) | copy-start | bytes 1540
  37.2 8.7 %copy-start.1 = (bf16[128,16,512]{2,1,0:T(8,128)(2,1)S(1)}, bf16[128,16,512]{2,1,0:T(8,128)(2,1)}, u32[]{:S(2)}) copy-start(bf16[128,16,512]{2,1,0:T(8,128)(2,1)} %param.6) | copy-start | bytes 6291460
  37.2 45.3 %all-to-all-start = ((bf16[128,8,768]{2,0,1:T(8,128)(2,1)}), bf16[128,8,768]{2,0,1:T(8,128)(2,1)}, u32[]{:S(2)}, u32[]{:S(2)}) async-start(bf16[128,8,768]{2,0,1:T(8,128)(2,1)} %copy.17), calls=%async_computation | async-start | bytes 3145728 | tf_op jit(solution)/shard_map/all_to_all | solution.py:101
  45.6 146.9 %all-gather.6.cloned.1.call-start = ((), (), s32[]{:S(2)}) async-start(), calls=%async_computation.4 | async-start | bytes 10485760 | tf_op jit(solution)/shard_map/all_gather | solution.py:120
  45.9 1.4 copy-start.4
  142.1 1.3 copy-start
Sparse Core Ops, SparseCore 0:
  35.5 42.8 all-gather.3
  82.6 109.8 all-gather.5

commit v12 on v6

--- a/solution.py
+++ b/solution.py
@@ -78,9 +78,7 @@
     score_scale = 1.0 / math.sqrt(HD)
     width = out_weight.shape[1]
 
-    weight = out_weight
-    for name in reversed(DP[2:] + FSDP):
-        weight = lax.all_gather(weight, name, axis=0, tiled=True)
+    weight = lax.all_gather(out_weight, DP[2:] + FSDP, axis=0, tiled=True)
     weight, group_qkv = lax.optimization_barrier((weight, group_qkv))
     weight = lax.all_gather(weight, DP[1], axis=0, tiled=True)
 

time: 202 us -> 200 us (0.990)
  blocking collectives: 107 us -> 112 us
  waiting for transfers between devices: 35.5 us -> 31.2 us
  starting transfers between devices: 8.75 us -> 6.15 us
    all_to_all x1, waiting for transfers between devices: 31.6 us -> 23.8 us  [per_device(): lax.all_to_all(local_qkv, FSDP, split_axis=1, concat_axis=0, tiled=True)]
    all_to_all x1, blocking collectives: 61.3 us -> 67.3 us  [per_device(): lax.all_to_all(packed, DP, split_axis=0, concat_axis=0, tiled=True)]
    all_gather x1, waiting for transfers between devices: 0.01 us -> 4.41 us  [per_device(): weight = lax.all_gather(weight, DP[1], axis=0, tiled=True)]
    all_to_all x1, starting transfers between devices: 8.74 us -> 6.14 us  [per_device(): lax.all_to_all(local_qkv, FSDP, split_axis=1, concat_axis=0, tiled=True)]
    all_gather x3 -> x1, blocking collectives: 24 us -> 21.9 us  [per_device(): weight = lax.all_gather(out_weight, DP[2:] + FSDP, axis=0, tiled=True)]
    unnamed x10 -> x9, local copies, waits for them, and re-layouts: 6.89 us -> 6.87 us
  transfers between devices with their start and end apart: 3 -> 3, of which waited for: 2 -> 3; matrix products, arithmetic and copies ran while one was open for 6% -> 6% of each run, Pallas kernels for 8% -> 8%
where the time goes in v12:
time: 200 us
  blocking collectives  112 us (56%)
  waiting for transfers between devices  31.2 us (16%)
  Pallas kernels  16.9 us (8%)
  between operations  13.5 us (7%)
  local copies, waits for them, and re-layouts  12.9 us (6%)
  matrix products  6.28 us (3%)
  starting transfers between devices  6.15 us (3%)
    all_to_all x1, blocking collectives, per_device(): lax.all_to_all(packed, DP, split_axis=0, concat_axis=0, tiled=True)  67.3 us
    all_to_all x1, waiting for transfers between devices, per_device(): lax.all_to_all(local_qkv, FSDP, split_axis=1, concat_axis=0, tiled=True)  23.8 us
    all_to_all x1, blocking collectives, per_device(): lax.all_to_all(attn_heads, FSDP, split_axis=0, concat_axis=1, tiled=True)  22.9 us
    all_gather x1, blocking collectives, per_device(): weight = lax.all_gather(out_weight, DP[2:] + FSDP, axis=0, tiled=True)  21.9 us
    pallas_call x1, Pallas kernels, attention(): pl.pallas_call(functools.partial(attention_kernel, scale=1.0 / math.sqrt(...  16.9 us
    unnamed x9, local copies, waits for them, and re-layouts  6.87 us
    all_to_all x1, starting transfers between devices, per_device(): lax.all_to_all(local_qkv, FSDP, split_axis=1, concat_axis=0, tiled=True)  6.14 us
    dot_general x1, matrix products, per_device(): summed = jnp.dot(tokens_attn, weight, preferred_element_type=jnp.float32)  5.46 us
  transfers between devices with their start and end apart: 3, of which 3 were waited for; matrix products, arithmetic and copies ran while one was open for 6% of the time, Pallas kernels for 8%

profile of v12, /device:TPU:1, one launch (start us, length us, event | category | flops | bytes accessed | tf_op | source)
XLA Modules:
  0.0 199.8 jit_solution(16490746311494704817)
XLA Ops:
  6.5 0.0 all-gather.4.cloned.1.call-start
  6.5 21.9 %all-gather = bf16[16,4,2048]{2,1,0:T(4,128)(2,1)S(1)} all-gather(bf16[1,4,2048]{2,1,0:T(4,128)(2,1)} %bitcast.34), channel_id=1, replica_groups=mesh['x'=4,'z'=8,'y_lo'=2,'y_hi'=4,'core'=2] {'y_lo','y_hi','core'}, dimensions={0}, use_global_device_ids=true | all-gather | bytes 278528 | tf_op jit(solution)/shard_map/all_gather | solution.py:81
  28.4 0.8 reshape.78
  29.2 0.0 all-gather.4.cloned.1.call-update
  29.2 1.7 copy.22
  31.0 1.4 copy.17
  32.4 6.1 %all-to-all-start = ((bf16[128,8,768]{2,0,1:T(8,128)(2,1)}), bf16[128,8,768]{2,0,1:T(8,128)(2,1)}, u32[]{:S(2)}, u32[]{:S(2)}) async-start(bf16[128,8,768]{2,0,1:T(8,128)(2,1)} %copy.17), calls=%async_computation | async-start | bytes 3145728 | tf_op jit(solution)/shard_map/all_to_all | solution.py:86
  38.6 0.0 all-gather.6.cloned.1.call-start
  38.6 3.0 %copy.20 = bf16[16,8,16,512]{3,1,2,0:T(8,128)(2,1)S(1)} copy(bf16[16,8,16,512]{3,2,1,0:T(8,128)(2,1)} %bitcast.31) | data formatting | bytes 4194304
  41.6 0.0 copy-done.1
  41.6 0.1 fusion.2
  41.7 0.2 reduce_window_sum.11
  41.8 0.0 copy-done.2
  41.8 0.2 select_reduce_fusion.1
  42.1 0.1 convert_reduce_fusion
  42.2 0.8 fusion
  43.0 0.8 copy.21
  43.8 23.8 %all-to-all-done = bf16[128,8,768]{2,0,1:T(8,128)(2,1)} async-done(((bf16[128,8,768]{2,0,1:T(8,128)(2,1)}), bf16[128,8,768]{2,0,1:T(8,128)(2,1)}, u32[]{:S(2)}, u32[]{:S(2)}) %all-to-all-start) | async-done | bytes 1572896 | tf_op jit(solution)/shard_map/all_to_all | solution.py:86
  67.7 4.4 %all-gather.4.cloned.1.call-done = bf16[512,2048]{1,0:T(8,128)(2,1)} async-done(((bf16[64,2048]{1,0:T(8,128)(2,1)}), bf16[512,2048]{1,0:T(8,128)(2,1)}) %all-gather.4.cloned.1.call-update) | async-done | bytes 2097168 | tf_op jit(solution)/shard_map/all_gather | solution.py:83
  72.1 0.0 all-gather.6.cloned.1.call-update
  72.1 67.3 %all_to_all.39 = bf16[64,2,16,512]{3,2,1,0:T(8,128)(2,1)S(1)} all-to-all(bf16[64,2,16,512]{3,2,1,0:T(8,128)(2,1)S(1)} %bitcast.26), channel_id=1, replica_groups=mesh['x'=4,'z'=8,'y_lo'=2,'y_hi'=4,'core'=2] {'x','z','y_lo'}, dimensions={0} | all-to-all | bytes 4194304 | tf_op jit(solution)/shard_map/all_to_all | solution.py:106
  139.4 1.3 copy-done
  140.7 0.4 fusion.3
  141.1 0.1 reshape.76
  141.2 0.1 broadcast_in_dim.28
  141.3 1.6 convert_element_type.51.live_col_ref
  142.9 0.7 convert_element_type.47.live_row_ref
  143.6 16.9 %shard_map.55 = bf16[1024,256]{1,0:T(8,128)(2,1)} custom-call(bf16[1024,768]{1,0:T(8,128)(2,1)} %bitcast.3.q_ref.kn_ref.vn_ref, bf16[2048,512]{1,0:T(8,128)(2,1)} %bitcast.29, bf16[2048,512]{1,0:T(8,128)(2,1)} %bitcast.30, bf16[1024,768]{1,0:T(8,128)(2,1)} %bitcast.3.q_ref.kn_ref.vn_ref, bf16[1024,768]{1,0:T(8,128)(2,1)} %bitcast.3.q_ref.kn_ref.vn_ref, ...), custom_call_target="tpu_custom_call" | custom-call | flops 3221225472 | bytes 4194304 | tf_op jit(solution)/shard_map/pallas_call | solution.py:50
  160.4 1.3 copy.19
  161.8 22.9 %all_to_all.40 = bf16[8,128,256]{1,2,0:T(8,128)(2,1)S(1)} all-to-all(bf16[8,128,256]{1,2,0:T(8,128)(2,1)S(1)} %copy.19), channel_id=1, replica_groups=mesh['x'=4,'z'=8,'y_lo'=2,'y_hi'=4,'core'=2] {'y_hi','core'}, dimensions={0} | all-to-all | bytes 1048576 | tf_op jit(solution)/shard_map/all_to_all | solution.py:111
  184.7 2.9 %all-gather.6.cloned.1.call-done = bf16[2048,2048]{1,0:T(8,128)(2,1)} async-done(((bf16[512,2048]{1,0:T(8,128)(2,1)}), bf16[2048,2048]{1,0:T(8,128)(2,1)}) %all-gather.6.cloned.1.call-update) | async-done | bytes 8388624 | tf_op jit(solution)/shard_map/all_gather | solution.py:105
  187.5 5.5 %fusion.1 = bf16[1,128,2048]{2,1,0:T(8,128)(2,1)} fusion(bf16[128,2048]{0,1:T(8,128)(2,1)S(1)} %bitcast.28, bf16[2048,2048]{1,0:T(8,128)(2,1)} %all-gather.6.cloned.1.call-done), kind=kOutput, calls=%fused_computation.3 | convolution fusion | flops 1074003968 | bytes 9437184 | tf_op jit(solution)/shard_map/dot_general | solution.py:112
  (5 shorter events, 0.0 us)
Async XLA Ops:
  6.5 65.6 %all-gather.4.cloned.1.call-start = ((), (), s32[]{:S(2)}) async-start(), calls=%async_computation.3 | async-start | bytes 2359296 | tf_op jit(solution)/shard_map/all_gather | solution.py:83
  32.4 35.3 %all-to-all-start = ((bf16[128,8,768]{2,0,1:T(8,128)(2,1)}), bf16[128,8,768]{2,0,1:T(8,128)(2,1)}, u32[]{:S(2)}, u32[]{:S(2)}) async-start(bf16[128,8,768]{2,0,1:T(8,128)(2,1)} %copy.17), calls=%async_computation | async-start | bytes 3145728 | tf_op jit(solution)/shard_map/all_to_all | solution.py:86
  38.6 149.0 %all-gather.6.cloned.1.call-start = ((), (), s32[]{:S(2)}) async-start(), calls=%async_computation.4 | async-start | bytes 10485760 | tf_op jit(solution)/shard_map/all_gather | solution.py:105
  38.6 3.0 %copy-start.1 = (s32[128]{0:T(128)S(1)}, s32[128]{0:T(128)}, u32[]{:S(2)}) copy-start(s32[128]{0:T(128)} %param.7) | copy-start | bytes 1540
  38.6 3.3 %copy-start.2 = (s32[64]{0:T(128)S(1)}, s32[64]{0:T(128)}, u32[]{:S(2)}) copy-start(s32[64]{0:T(128)} %param.8) | copy-start | bytes 772
  139.4 1.3 copy-start
Sparse Core Ops, SparseCore 0:
  29.3 42.7 all-gather.3
  74.2 113.2 all-gather.5
